TPU v7x, 256 devices: a whole 4x4x8 slice. The times are simulated.
256 devices in a mesh: det: 16 (over z, core), orb: 16 (over x, y).
Axes of the slice: x: 4, y: 4, z: 8, core: 2. Of those that a mesh axis runs over, the one named last changes fastest.
Arguments:
- orbitals: bfloat16 [64, 1024, 256], P('det', 'orb'), may hold values from -0.06 to 1.06
- dfit: bfloat16 [64, 1024, 1024], P('orb'), may hold values from -0.5 to 0.5, as said below
- pair_left: int32 [32], P('det'), may hold values from 0 to 63, as said below
- pair_right: int32 [32], P('det'), may hold values from 0 to 63
- pair_count: int32 [16], P('det'), may hold values from 1 to 2, as said below
- pair_weight: float32 [32], P('det'), may hold values from 1 to 4
- aux_screen: int32 [32, 64], P('det', 'orb'), may hold values 0 or 1
Outputs:
- gradient: float32 [64, 1024, 256], P('det', 'orb')
Inputs may be any that keep to these rules, and one draw needn't show every extreme that they name: `pair_left`: slot s names a determinant among numbers (s // 2) * 4 to (s // 2 + 1) * 4 - 1. `pair_count`: some det index has all 2 slots live. `dfit`: every matrix is symmetric.
All inputs are finite; a program needn't handle non-finite values. No bound on the sum of `aux_screen` on one device may be relied on, other than what follows from the above.
Results may differ from a plain program's by a relative error of at most 0.0022.
Values may be sent and summed in bfloat16 or wider, within the bound.
No kernel may reach another device: no remote copies, remote signals or barrier semaphores. Data moves between devices by JAX's collectives and lax.ppermute only.
A program may use at most 64 MiB of HBM per device.

v0:
```python
import jax
import jax.numpy as jnp
from jax import lax
from jax.sharding import PartitionSpec as P

NS = 3


def newton(correlation):
    eye = jnp.eye(correlation.shape[-1], dtype=jnp.float32)
    inverse = jnp.broadcast_to(eye, correlation.shape)
    for sweep in range(NS):
        product = jnp.einsum("bij,bjk->bik", correlation, inverse, precision=lax.Precision.HIGHEST)
        inverse = jnp.einsum(
            "bij,bjk->bik", inverse, 2.0 * eye - product, precision=lax.Precision.HIGHEST
        )
    return inverse


def process(dfit, left_rows, right_rows, weights, screen):
    correlation_part = jnp.einsum(
        "brc,brd->bcd", left_rows, right_rows, preferred_element_type=jnp.float32
    )
    correlation = lax.psum(correlation_part, "orb")
    inverse = newton(correlation)
    moved_rows = jnp.einsum(
        "brc,bcd->brd", right_rows.astype(jnp.float32), inverse, precision=lax.Precision.HIGHEST
    ).astype(jnp.bfloat16)
    left_full, moved_full = (
        lax.all_gather(left_rows, "orb", axis=1, tiled=True),
        lax.all_gather(moved_rows, "orb", axis=1, tiled=True),
    )
    applied = jnp.einsum(
        "qst,btc->bqsc", dfit, moved_full, preferred_element_type=jnp.float32
    ).astype(jnp.bfloat16)
    projected = jnp.einsum(
        "bsc,qst->bqct", left_full, dfit, preferred_element_type=jnp.float32
    ).astype(jnp.bfloat16)
    exchange = jnp.einsum(
        "bqct,btd->bqcd", projected, moved_full, preferred_element_type=jnp.float32
    )
    factor = 2.0 * weights[:, None, None, None] * screen.astype(jnp.float32)[:, :, None, None]
    scaled = (factor * exchange).astype(jnp.bfloat16)
    left_term = jnp.einsum("bqsc,bqdc->sbd", applied, scaled, preferred_element_type=jnp.float32)
    moved_term = jnp.einsum("bqcs,bqcd->sbd", projected, scaled, preferred_element_type=jnp.float32)
    summed = lax.psum_scatter(
        jnp.concatenate([left_term, moved_term], axis=1), "orb", scatter_dimension=0, tiled=True
    )
    batch = left_rows.shape[0]
    left_grad = jnp.transpose(summed[:, :batch], (1, 0, 2))
    moved_grad = jnp.transpose(summed[:, batch:], (1, 0, 2))
    right_grad = jnp.einsum("brc,bdc->brd", moved_grad, inverse, precision=lax.Precision.HIGHEST)
    return (left_grad, right_grad)


def local(orbitals, dfit, pair_left, pair_right, pair_count, pair_weight, aux_screen):
    det_local = orbitals.shape[0]
    capacity = pair_left.shape[0]
    slot_index = jnp.arange(capacity, dtype=jnp.int32)
    weights = jnp.where(slot_index < pair_count[0], pair_weight, jnp.zeros_like(pair_weight))
    left_local = pair_left % det_local
    left_rows = jnp.take(orbitals, left_local, axis=0)
    everyone = lax.all_gather(orbitals, "det", axis=0, tiled=True)
    right_rows = jnp.take(everyone, pair_right, axis=0)

    def one_slot(slot, grads):

        def select_slot(array):
            return lax.dynamic_slice_in_dim(array, slot, 1, 0)

        left_one, right_one = process(
            dfit,
            select_slot(left_rows),
            select_slot(right_rows),
            select_slot(weights),
            select_slot(aux_screen),
        )
        return (
            lax.dynamic_update_slice_in_dim(grads[0], left_one, slot, 0),
            lax.dynamic_update_slice_in_dim(grads[1], right_one, slot, 0),
        )

    zeros = jnp.zeros(left_rows.shape, jnp.float32)
    left_grad, right_grad = lax.fori_loop(0, capacity, one_slot, (zeros, zeros))
    owners = (left_local[:, None] == jnp.arange(det_local, dtype=jnp.int32)[None, :]).astype(
        jnp.float32
    )
    own_sum = jnp.einsum("pn,prc->nrc", owners, left_grad, precision=lax.Precision.HIGHEST)
    places = jnp.arange(det_local * lax.axis_size("det"), dtype=jnp.int32)
    match = (pair_right[:, None] == places[None, :]).astype(jnp.float32)
    returned = lax.psum_scatter(
        jnp.einsum("pn,prc->nrc", match, right_grad, precision=lax.Precision.HIGHEST),
        "det",
        scatter_dimension=0,
        tiled=True,
    )
    return own_sum + returned


def solution(mesh):
    in_specs = (
        P("det", "orb", None),
        P("orb", None, None),
        P("det"),
        P("det"),
        P("det"),
        P("det"),
        P("det", "orb"),
    )
    out_specs = P("det", "orb", None)
    return jax.shard_map(local, mesh=mesh, in_specs=in_specs, out_specs=out_specs, check_vma=False)
```

profile of v0, /device:TPU:32, one launch (start us, length us, event | category | flops | bytes accessed | tf_op | source)
XLA Modules:
  0.0 616.9 jit_solution(5396601231880543745)
XLA Ops:
  6.5 0.7 all-gather.5.cloned.1.call-update
  7.9 0.7 compare_and_fusion.1
  8.6 1.5 gather_fusion
  10.8 0.7 compare_and_fusion
  12.1 38.4 %all-gather.5.cloned.1.call-done = bf16[64,64,256]{2,1,0:T(8,128)(2,1)} async-done(((bf16[4,64,256]{2,1,0:T(8,128)(2,1)}), bf16[64,64,256]{2,1,0:T(8,128)(2,1)}) %all-gather.5.cloned.1.call-update) | async-done | bytes 2097168 | tf_op jit(solution)/shard_map/all_gather | solution.py:63
  50.6 2.1 gather_fusion.1
  52.8 488.6 %while.15 = (s32[]{:T(128)}, f32[2,64,256]{2,0,1:T(2,128)}, f32[2,64,256]{2,0,1:T(2,128)}, f32[2]{0:T(128)S(1)}, s32[2,4]{1,0:T(2,128)}, /*index=5*/bf16[2,64,25...) while((s32[]{:T(128)}, f32[2,64,256]{2,0,1:T(2,128)}, ...), condition=%wide.region_3.4_spmd, body=%wide.region_0.3_spmd.sunk | while | flops 7227064320 | bytes 65279744 | solution.py:84
  52.9 0.9 fusion.130
  53.9 24.2 %all_gather.19 = bf16[1,1024,256]{2,1,0:T(8,128)(2,1)S(1)} all-gather(bf16[1,64,256]{2,1,0:T(8,128)(2,1)S(1)} %constant_dynamic-slice_fusion.6), channel_id=1, replica_groups=mesh['det'=16,'orb'=16] {'orb'}, dimensions={1}, use_global_device_ids=true | all-gather | bytes 557056 | tf_op jit(solution)/shard_map/while/body/eval_jaxpr/all_gather | solution.py:30
  78.1 5.8 convolution_convert_fusion.4
  85.2 65.8 %all-reduce.6.cloned.1.call-done = f32[256,256]{1,0:T(8,128)} async-done(((f32[256,256]{1,0:T(8,128)}), f32[256,256]{1,0:T(8,128)}) %all-reduce.6.cloned.1.call-update) | async-done | bytes 262160 | tf_op jit(solution)/shard_map/while/body/eval_jaxpr/psum | solution.py:24
  151.0 1.3 convolution_subtract_fusion.6
  152.6 1.3 convolution_subtract_fusion.7
  155.3 23.3 %all-gather.2 = bf16[1024,256]{1,0:T(8,128)(2,1)S(1)} all-gather(bf16[64,256]{1,0:T(8,128)(2,1)S(1)} %convolution_convert_fusion.5), channel_id=2, replica_groups=mesh['det'=16,'orb'=16] {'orb'}, dimensions={0}, use_global_device_ids=true | all-gather | bytes 557056 | tf_op jit(solution)/shard_map/while/body/eval_jaxpr/all_gather | solution.py:31
  178.6 0.8 copy-done.2
  179.4 0.7 fusion.135
  180.2 0.8 copy-done.1
  181.0 0.7 fusion.136
  181.7 7.7 %fusion.137 = f32[1024,1,256]{0,2,1:T(8,128)} fusion(bf16[4,256,256]{2,1,0:T(8,128)(2,1)} %copy-done.1, bf16[4,1024,1024]{2,1,0:T(8,128)(2,1)} %get-tuple-element.280, bf16[1024,256]{1,0:T(8,128)(2,1)} %copy-done.2), kind=kOutput, calls=%fused_computation.12.clone.1 | convolution fusion | flops 2685403136 | bytes 10485760 | tf_op jit(solution)/shard_map/while/body/eval_jaxpr/bqsc,bqdc->sbd/dot_general | solution.py:44
  189.4 1.4 pad_maximum_fusion.2
  190.8 2.4 copy.46
  195.0 98.0 %all-reduce.8.cloned.1.call-done = f32[1024,2,256]{2,1,0:T(2,128)} async-done(((f32[1024,2,256]{2,1,0:T(2,128)}), f32[1024,2,256]{2,1,0:T(2,128)}) %all-reduce.8.cloned.1.call-update) | async-done | bytes 2097168 | tf_op jit(solution)/shard_map/while
  293.0 1.1 constant_dynamic-slice_fusion.7
  294.6 0.9 dynamic_update_slice.16
  295.5 0.9 dynamic_update_slice.17
  297.1 0.9 fusion.130
  298.1 23.5 %all_gather.19 = bf16[1,1024,256]{2,1,0:T(8,128)(2,1)S(1)} all-gather(bf16[1,64,256]{2,1,0:T(8,128)(2,1)S(1)} %constant_dynamic-slice_fusion.6), channel_id=1, replica_groups=mesh['det'=16,'orb'=16] {'orb'}, dimensions={1}, use_global_device_ids=true | all-gather | bytes 557056 | tf_op jit(solution)/shard_map/while/body/eval_jaxpr/all_gather | solution.py:30
  321.6 5.8 convolution_convert_fusion.4
  328.7 66.7 %all-reduce.6.cloned.1.call-done = f32[256,256]{1,0:T(8,128)} async-done(((f32[256,256]{1,0:T(8,128)}), f32[256,256]{1,0:T(8,128)}) %all-reduce.6.cloned.1.call-update) | async-done | bytes 262160 | tf_op jit(solution)/shard_map/while/body/eval_jaxpr/psum | solution.py:24
  395.3 1.3 convolution_subtract_fusion.6
  396.9 1.3 convolution_subtract_fusion.7
  399.7 23.3 %all-gather.2 = bf16[1024,256]{1,0:T(8,128)(2,1)S(1)} all-gather(bf16[64,256]{1,0:T(8,128)(2,1)S(1)} %convolution_convert_fusion.5), channel_id=2, replica_groups=mesh['det'=16,'orb'=16] {'orb'}, dimensions={0}, use_global_device_ids=true | all-gather | bytes 557056 | tf_op jit(solution)/shard_map/while/body/eval_jaxpr/all_gather | solution.py:31
  423.0 0.8 copy-done.2
  423.8 0.7 fusion.135
  424.5 0.8 copy-done.1
  425.3 0.7 fusion.136
  426.0 7.7 %fusion.137 = f32[1024,1,256]{0,2,1:T(8,128)} fusion(bf16[4,256,256]{2,1,0:T(8,128)(2,1)} %copy-done.1, bf16[4,1024,1024]{2,1,0:T(8,128)(2,1)} %get-tuple-element.280, bf16[1024,256]{1,0:T(8,128)(2,1)} %copy-done.2), kind=kOutput, calls=%fused_computation.12.clone.1 | convolution fusion | flops 2685403136 | bytes 10485760 | tf_op jit(solution)/shard_map/while/body/eval_jaxpr/bqsc,bqdc->sbd/dot_general | solution.py:44
  433.7 1.4 pad_maximum_fusion.2
  435.1 2.4 copy.46
  439.4 98.0 %all-reduce.8.cloned.1.call-done = f32[1024,2,256]{2,1,0:T(2,128)} async-done(((f32[1024,2,256]{2,1,0:T(2,128)}), f32[1024,2,256]{2,1,0:T(2,128)}) %all-reduce.8.cloned.1.call-update) | async-done | bytes 2097168 | tf_op jit(solution)/shard_map/while
  537.4 1.1 constant_dynamic-slice_fusion.7
  538.9 0.9 dynamic_update_slice.16
  539.9 0.9 dynamic_update_slice.17
  541.4 2.8 fusion.39
  544.3 4.4 copy.30
  548.7 0.9 copy-done.7
  550.1 58.3 %reduce-scatter.2.cloned.1.call-done = f32[4,64,256]{2,1,0:T(8,128)} async-done(((f32[64,64,256]{2,1,0:T(8,128)}), f32[4,64,256]{2,1,0:T(8,128)}) %reduce-scatter.2.cloned.1.call-update) | async-done | bytes 262160 | tf_op jit(solution)/shard_map/reduce_scatter | solution.py:91
  608.4 1.7 copy_add_fusion
  (78 shorter events, 11.4 us)
Async XLA Ops:
  6.5 44.1 %all-gather.5.cloned.1.call-start = ((), (), s32[]{:S(2)}) async-start(), calls=%async_computation.1 | async-start | bytes 2228224 | tf_op jit(solution)/shard_map/all_gather | solution.py:63
  52.8 488.6 %copy-start.9 = (s32[2]{0:T(128)S(1)}, s32[2]{0:T(128)}, u32[]{:S(2)}) copy-start(s32[2]{0:T(128)} %param.12) | copy-start | bytes 28
  52.8 98.1 %all-reduce.6.cloned.1.call-start = ((), (), s32[]{:S(2)}) async-start(), calls=%async_computation.3 | async-start | bytes 524288 | tf_op jit(solution)/shard_map/while/body/eval_jaxpr/psum | solution.py:24
  53.8 239.2 %all-reduce.8.cloned.1.call-start = ((), (), s32[]{:S(2)}) async-start(), calls=%async_computation.4 | async-start | bytes 4194304 | tf_op jit(solution)/shard_map/while
  78.1 7.0 %copy-start.8 = (s32[2,4]{1,0:T(2,128)S(1)}, s32[2,4]{1,0:T(2,128)}, u32[]{:S(2)}) copy-start(s32[2,4]{1,0:T(2,128)} %get-tuple-element.278) | copy-start | bytes 100 | tf_op jit(solution)/shard_map/while
  151.0 3.3 copy-start
  178.6 0.8 copy-start.2
  180.2 0.8 copy-start.1
  193.1 0.7 copy-start.10
  193.1 101.4 %copy-start.5 = (f32[2,64,256]{2,0,1:T(2,128)S(1)}, f32[2,64,256]{2,0,1:T(2,128)}, u32[]{:S(2)}) copy-start(f32[2,64,256]{2,0,1:T(2,128)} %get-tuple-element.260) | copy-start | bytes 393220 | tf_op jit(solution)/shard_map/while
  193.1 102.4 %copy-start.3 = (f32[2,64,256]{2,0,1:T(2,128)S(1)}, f32[2,64,256]{2,0,1:T(2,128)}, u32[]{:S(2)}) copy-start(f32[2,64,256]{2,0,1:T(2,128)} %get-tuple-element.261) | copy-start | bytes 393220 | tf_op jit(solution)/shard_map/while
  295.5 1.0 copy-start.6
  296.4 0.6 copy-start.4
  297.1 98.2 %all-reduce.6.cloned.1.call-start = ((), (), s32[]{:S(2)}) async-start(), calls=%async_computation.3 | async-start | bytes 524288 | tf_op jit(solution)/shard_map/while/body/eval_jaxpr/psum | solution.py:24
  298.0 239.4 %all-reduce.8.cloned.1.call-start = ((), (), s32[]{:S(2)}) async-start(), calls=%async_computation.4 | async-start | bytes 4194304 | tf_op jit(solution)/shard_map/while
  321.6 7.0 %copy-start.8 = (s32[2,4]{1,0:T(2,128)S(1)}, s32[2,4]{1,0:T(2,128)}, u32[]{:S(2)}) copy-start(s32[2,4]{1,0:T(2,128)} %get-tuple-element.278) | copy-start | bytes 100 | tf_op jit(solution)/shard_map/while
  395.3 3.3 copy-start
  423.0 0.8 copy-start.2
  424.5 0.8 copy-start.1
  437.5 0.7 copy-start.10
  437.5 101.4 %copy-start.5 = (f32[2,64,256]{2,0,1:T(2,128)S(1)}, f32[2,64,256]{2,0,1:T(2,128)}, u32[]{:S(2)}) copy-start(f32[2,64,256]{2,0,1:T(2,128)} %get-tuple-element.260) | copy-start | bytes 393220 | tf_op jit(solution)/shard_map/while
  437.5 102.4 %copy-start.3 = (f32[2,64,256]{2,0,1:T(2,128)S(1)}, f32[2,64,256]{2,0,1:T(2,128)}, u32[]{:S(2)}) copy-start(f32[2,64,256]{2,0,1:T(2,128)} %get-tuple-element.261) | copy-start | bytes 393220 | tf_op jit(solution)/shard_map/while
  539.8 1.0 copy-start.6
  540.8 0.6 copy-start.4
  541.4 66.9 %reduce-scatter.2.cloned.1.call-start = ((), (), s32[]{:S(2)}) async-start(), calls=%async_computation.2 | async-start | bytes 4456448 | tf_op jit(solution)/shard_map/reduce_scatter | solution.py:91
  548.7 0.9 copy-start.7
Sparse Core Ops, SparseCore 0:
  9.2 41.3 all-gather.4
  56.8 94.1 all-reduce.5
  193.3 99.6 all-reduce.7
  300.7 94.5 all-reduce.5
  437.6 99.6 all-reduce.7
  548.8 59.5 reduce-scatter.1
where the time goes:
time: 621 us; the launch traced here: 617 us
  waiting for transfers between devices  426 us (69%)
  blocking collectives  94.3 us (15%)
  matrix products  44.2 us (7%)
  local copies, waits for them, and re-layouts  27.8 us (4%)
  between operations  14.1 us (2%)
  other arithmetic  7.37 us (1%)
    while x6, waiting for transfers between devices  196 us
    psum x2, waiting for transfers between devices, process(): correlation = lax.psum(correlation_part, 'orb')  132 us
    reduce_scatter x1, waiting for transfers between devices, local(): lax.psum_scatter(jnp.einsum('pn,prc->nrc', match, right_grad, precision=l...  58.3 us
    all_gather x2, blocking collectives, process(): lax.all_gather(left_rows, 'orb', axis=1, tiled=True)  47.7 us
    all_gather x2, blocking collectives, process(): lax.all_gather(moved_rows, 'orb', axis=1, tiled=True)  46.6 us
    all_gather x1, waiting for transfers between devices, local(): everyone = lax.all_gather(orbitals, 'det', axis=0, tiled=True)  38.4 us
    dot_general x2, matrix products, process(): jnp.einsum('bqsc,bqdc->sbd', applied, scaled, preferred_element_type=jnp....  15.3 us
  transfers between devices with their start and end apart: 6, of which 6 were waited for; matrix products, arithmetic and copies ran while one was open for 3% of the time, Pallas kernels for 0%

commit v1 on v0

v1 whole, which is shorter than its diff:
```python
import jax
import jax.numpy as jnp
from jax import lax
from jax.sharding import PartitionSpec as P

NS = 3
HI = lax.Precision.HIGHEST


def newton(correlation):
    eye = jnp.eye(correlation.shape[-1], dtype=jnp.float32)
    inverse = 2.0 * eye - correlation
    for sweep in range(NS - 1):
        product = jnp.einsum("bij,bjk->bik", correlation, inverse, precision=HI)
        inverse = jnp.einsum("bij,bjk->bik", inverse, 2.0 * eye - product, precision=HI)
    return inverse


def local(orbitals, dfit, pair_left, pair_right, pair_count, pair_weight, aux_screen):
    det_local, rows, nocc = orbitals.shape
    capacity = pair_left.shape[0]
    n_det = lax.axis_size("det")
    n_orb = lax.axis_size("orb")
    me = lax.axis_index("det")
    slot_index = jnp.arange(capacity, dtype=jnp.int32)
    weights = jnp.where(slot_index < pair_count[0], pair_weight, jnp.zeros_like(pair_weight))
    left_local = pair_left % det_local
    left_rows = jnp.take(orbitals, left_local, axis=0)

    right_all = lax.all_gather(pair_right, "det", axis=0, tiled=True)
    send = jnp.take(orbitals, right_all % det_local, axis=0).reshape(n_det, capacity, rows, nocc)
    got = lax.all_to_all(send, "det", 0, 0, tiled=True)
    owner = pair_right // det_local
    right_rows = got[owner, slot_index]

    both = jnp.concatenate([left_rows, right_rows], axis=0)
    spread = jnp.broadcast_to(both[None], (n_orb,) + both.shape)
    gathered = lax.all_to_all(spread, "orb", 0, 0, tiled=True)
    gathered = jnp.transpose(gathered, (1, 0, 2, 3)).reshape(2 * capacity, n_orb * rows, nocc)
    left_full = gathered[:capacity]
    right_full = gathered[capacity:]

    correlation = jnp.einsum("brc,brd->bcd", left_full, right_full, preferred_element_type=jnp.float32)
    inverse = newton(correlation)
    moved_full = jnp.einsum(
        "brc,bcd->brd", right_full.astype(jnp.float32), inverse, precision=HI
    ).astype(jnp.bfloat16)

    stacked = jnp.concatenate([moved_full, left_full], axis=2)
    stacked = jnp.transpose(stacked, (1, 0, 2)).reshape(n_orb * rows, capacity * 2 * nocc)
    product = jnp.einsum("qst,tk->qsk", dfit, stacked, preferred_element_type=jnp.float32).astype(jnp.bfloat16)
    product = product.reshape(dfit.shape[0], n_orb * rows, capacity, 2, nocc)
    applied = product[:, :, :, 0]
    projected_t = product[:, :, :, 1]
    exchange = jnp.einsum("qtbc,btd->bqcd", projected_t, moved_full, preferred_element_type=jnp.float32)
    factor = 2.0 * weights[:, None, None, None] * aux_screen.astype(jnp.float32)[:, :, None, None]
    scaled = (factor * exchange).astype(jnp.bfloat16)
    left_term = jnp.einsum("qsbc,bqdc->bsd", applied, scaled, preferred_element_type=jnp.float32)
    moved_term = jnp.einsum("qsbc,bqcd->bsd", projected_t, scaled, preferred_element_type=jnp.float32)

    terms = jnp.stack([left_term, moved_term], axis=0).reshape(2, capacity, n_orb, rows, nocc)
    terms = jnp.transpose(terms, (2, 0, 1, 3, 4))
    parts = lax.all_to_all(terms, "orb", 0, 0, tiled=True)
    summed = jnp.sum(parts, axis=0)
    left_grad = summed[0]
    moved_grad = summed[1]
    right_grad = jnp.einsum("brc,bdc->brd", moved_grad, inverse, precision=HI)

    own = left_local[:, None] == jnp.arange(det_local, dtype=jnp.int32)[None, :]
    own_sum = jnp.sum(jnp.where(own[:, :, None, None], left_grad[:, None], 0.0), axis=0)

    back = jnp.broadcast_to(right_grad[None], (n_det,) + right_grad.shape)
    came = lax.all_to_all(back, "det", 0, 0, tiled=True)
    mine = right_all.reshape(n_det, capacity)[:, :, None] == (
        me * det_local + jnp.arange(det_local, dtype=jnp.int32)
    )[None, None, :]
    returned = jnp.sum(jnp.where(mine[:, :, :, None, None], came[:, :, None], 0.0), axis=(0, 1))
    return own_sum + returned


def solution(mesh):
    in_specs = (
        P("det", "orb", None),
        P("orb", None, None),
        P("det"),
        P("det"),
        P("det"),
        P("det"),
        P("det", "orb"),
    )
    out_specs = P("det", "orb", None)
    return jax.shard_map(local, mesh=mesh, in_specs=in_specs, out_specs=out_specs, check_vma=False)
```

time: 621 us -> 244 us (0.39)
  waiting for transfers between devices: 426 us -> 101 us
  blocking collectives: 94.3 us -> 70.5 us
  matrix products: 44.2 us -> 22.8 us
  starting transfers between devices: 0.14 us -> 19.2 us
  between operations: 14.1 us -> 1.65 us
  local copies, waits for them, and re-layouts: 27.8 us -> 19.5 us
    while x6 -> x0, waiting for transfers between devices: 196 us -> none
    psum x2 -> x0, waiting for transfers between devices: 132 us -> none  [process(): correlation = lax.psum(correlation_part, 'orb')]
    all_to_all x0 -> x3, waiting for transfers between devices: none -> 101 us  [the longest x1 46.8 us: local(): came = lax.all_to_all(back, 'det', 0, 0, tiled=True)]
    all_gather x4 -> x0, blocking collectives: 94.3 us -> none  [the longest x2 47.7 us: process(): lax.all_gather(left_rows, 'orb', axis=1, tiled=True)]
    reduce_scatter x1 -> x0, waiting for transfers between devices: 58.3 us -> none  [local(): lax.psum_scatter(jnp.einsum('pn,prc->nrc', match, right_grad, precision=l...]
    all_to_all x0 -> x1, blocking collectives: none -> 55.1 us  [local(): parts = lax.all_to_all(terms, 'orb', 0, 0, tiled=True)]
    all_gather x1 -> x0, waiting for transfers between devices: 38.4 us -> none  [local(): everyone = lax.all_gather(orbitals, 'det', axis=0, tiled=True)]
    dot_general x28 -> x11, matrix products: 44.2 us -> 22.8 us  [the longest x1 11.3 us: local(): jnp.einsum('qst,tk->qsk', dfit, stacked, preferred_element_type=jnp.float32)]
  transfers between devices with their start and end apart: 6 -> 3, of which waited for: 6 -> 3; matrix products, arithmetic and copies ran while one was open for 3% -> 0% of each run, Pallas kernels for 0% -> 0%
where the time goes in v1:
time: 244 us; the launch traced here: 240 us
  waiting for transfers between devices  101 us (41%)
  blocking collectives  70.5 us (29%)
  matrix products  22.8 us (9%)
  local copies, waits for them, and re-layouts  19.5 us (8%)
  starting transfers between devices  19.2 us (8%)
  other arithmetic  5.94 us (2%)
    all_to_all x1, blocking collectives, local(): parts = lax.all_to_all(terms, 'orb', 0, 0, tiled=True)  55.1 us
    all_to_all x1, waiting for transfers between devices, local(): came = lax.all_to_all(back, 'det', 0, 0, tiled=True)  46.8 us
    all_to_all x1, waiting for transfers between devices, local(): gathered = lax.all_to_all(spread, 'orb', 0, 0, tiled=True)  29.9 us
    all_to_all x1, waiting for transfers between devices, local(): got = lax.all_to_all(send, 'det', 0, 0, tiled=True)  23.9 us
    unnamed x1, blocking collectives  15.4 us
    dot_general x1, matrix products, local(): jnp.einsum('qst,tk->qsk', dfit, stacked, preferred_element_type=jnp.float32)  11.3 us
    unnamed x24, local copies, waits for them, and re-layouts  9.85 us
    all_to_all x1, starting transfers between devices, local(): came = lax.all_to_all(back, 'det', 0, 0, tiled=True)  7.74 us
  transfers between devices with their start and end apart: 3, of which 3 were waited for; matrix products, arithmetic and copies ran while one was open for 0% of the time, Pallas kernels for 0%

profile of v1, /device:TPU:32, one launch (start us, length us, event | category | flops | bytes accessed | tf_op | source)
XLA Modules:
  0.0 240.2 jit_solution(3160535435821954559)
XLA Ops:
  0.0 1.3 dynamic-slice
  2.0 0.9 dynamic-update-slice
  2.9 15.4 %all-reduce = s32[32]{0:T(128)S(1)} all-reduce(s32[32]{0:T(128)S(1)} %dynamic-update-slice), channel_id=1, replica_groups=mesh['det'=16,'orb'=16] {'det'}, use_global_device_ids=true, to_apply=%add | all-reduce | flops 32 | bytes 256
  18.3 0.1 broadcast_in_dim.99
  18.4 0.6 gather_fusion.1
  19.0 1.1 broadcast_select_fusion
  20.1 4.4 %all-to-all-start = ((bf16[16,2,64,256]{3,2,1,0:T(8,128)(2,1)}), bf16[16,2,64,256]{3,2,1,0:T(8,128)(2,1)S(1)}, u32[]{:S(2)}, u32[]{:S(2)}) async-start(bf16[16,2,64,256]{3,2,1,0:T(8,128)(2,1)} %broadcast_select_fusion), calls=%async_computation | async-start | bytes 2097152 | tf_op jit(solution)/shard_map/all_to_all | solution.py:32
  24.6 0.0 copy-start.9
  24.6 0.0 copy-start.6
  24.6 0.6 gather_fusion
  25.2 0.1 broadcast_select_fusion.1
  25.3 23.9 %all-to-all-done = bf16[16,2,64,256]{3,2,1,0:T(8,128)(2,1)S(1)} async-done(((bf16[16,2,64,256]{3,2,1,0:T(8,128)(2,1)}), bf16[16,2,64,256]{3,2,1,0:T(8,128)(2,1)S(1)}, u32[]{:S(2)}, u32[]{:S(2)}) %all-to-all-start) | async-done | bytes 1048608 | tf_op jit(solution)/shard_map/all_to_all | solution.py:32
  49.2 0.6 gather_fusion.2
  49.8 1.6 broadcast_in_dim.104
  51.4 7.0 %all-to-all-start.1 = ((bf16[16,4,64,256]{3,2,1,0:T(8,128)(2,1)}), bf16[16,4,64,256]{3,2,1,0:T(8,128)(2,1)S(1)}, u32[]{:S(2)}, u32[]{:S(2)}) async-start(bf16[16,4,64,256]{3,2,1,0:T(8,128)(2,1)} %broadcast_in_dim.104), calls=%async_computation.1 | async-start | bytes 4194304 | tf_op jit(solution)/shard_map/all_to_all | solution.py:38
  59.1 0.1 convert_multiply_fusion
  59.2 29.9 %all-to-all-done.1 = bf16[16,4,64,256]{3,2,1,0:T(8,128)(2,1)S(1)} async-done(((bf16[16,4,64,256]{3,2,1,0:T(8,128)(2,1)}), bf16[16,4,64,256]{3,2,1,0:T(8,128)(2,1)S(1)}, u32[]{:S(2)}, u32[]{:S(2)}) %all-to-all-start.1) | async-done | bytes 2097184 | tf_op jit(solution)/shard_map/all_to_all | solution.py:38
  89.2 0.1 copy.59
  89.3 0.1 fusion.21
  89.5 0.5 copy.34
  90.0 0.5 fusion.22
  90.5 0.7 convolution_subtract_fusion.1
  91.2 0.7 fusion.5
  91.9 0.7 convolution_subtract_fusion
  92.5 0.7 fusion.23
  93.2 1.0 convolution_convert_fusion.1
  94.3 0.2 pad_maximum_fusion.1
  94.4 0.8 copy-done.3
  95.3 11.3 %convolution_convert_fusion = bf16[1024,4,1024]{2,0,1:T(8,128)(2,1)S(1)} fusion(bf16[1024,1024,1]{0,1,2:T(8,128)(2,1)S(1)} %bitcast.77, bf16[4,1024,1024]{2,1,0:T(8,128)(2,1)} %param.8), kind=kOutput, calls=%fused_computation.4 | convolution fusion | flops 8594128896 | bytes 18874368 | tf_op jit(solution)/shard_map/qst,tk->qsk/dot_general | solution.py:51
  106.6 3.7 %fusion.20 = (bf16[4,1024,2,1,256]{1,4,3,2,0:T(8,128)(2,1)}, bf16[4,1024,2,1,256]{1,4,3,2,0:T(8,128)(2,1)}) fusion(bf16[4,1024,2,2,256]{1,4,3,2,0:T(8,128)(2,1)S(1)} %bitcast.73), kind=kLoop, calls=%fused_computation.63 | loop fusion | bytes 16777216 | tf_op jit(solution)/shard_map/slice | solution.py:53
  110.3 6.4 %copy.50 = bf16[4,1024,2,1,256]{4,1,0,2,3:T(8,128)(2,1)} copy(bf16[4,1024,2,1,256]{1,4,3,2,0:T(8,128)(2,1)} %get-tuple-element.9) | data formatting | bytes 8388608
  116.7 3.6 %multiply_convert_fusion = bf16[2,4,256,256]{3,2,1,0:T(8,128)(2,1)S(1)} fusion(bf16[4,1024,2,1,256]{1,4,3,2,0:T(8,128)(2,1)} %get-tuple-element.10, bf16[2,1024,256]{1,2,0:T(8,128)(2,1)S(1)} %copy-done.4, f32[2,4]{1,0:T(2,128)S(1)} %convert_multiply_fusion), kind=kOutput, calls=%fused_computation.14 | convolution fusion | flops 1074790400 | bytes 6291488 | tf_op jit(solution)/shard_map/qtbc,btd->bqcd/dot_general | solution.py:55
  120.4 1.8 fusion.2
  122.2 0.4 copy-done.2
  122.5 1.3 fusion
  123.8 0.3 copy_bitcast_fusion.1
  124.1 55.1 %all_to_all.20 = f32[16,2,2,64,256]{4,3,2,1,0:T(8,128)} all-to-all(f32[16,2,2,64,256]{4,3,2,1,0:T(8,128)S(1)} %copy_bitcast_fusion.1), channel_id=1, replica_groups=mesh['det'=16,'orb'=16] {'orb'}, dimensions={0} | all-to-all | bytes 8388608 | tf_op jit(solution)/shard_map/all_to_all | solution.py:63
  179.2 2.5 %reduce_sum.27 = f32[2,2,64,256]{3,2,1,0:T(8,128)S(1)} reduce(f32[16,2,2,64,256]{4,3,2,1,0:T(8,128)} %all_to_all.20, f32[]{:T(128)} %constant.75.clone.1), dimensions={0}, to_apply=%region_0.1 | reduce | flops 983040 | bytes 4456452 | tf_op jit(solution)/shard_map/reduce_sum | solution.py:64
  181.7 0.6 fusion.11
  182.3 1.6 broadcast_in_dim.109
  183.9 7.7 %all-to-all-start.3 = ((f32[16,2,64,256]{3,2,1,0:T(8,128)}), f32[16,2,64,256]{3,2,1,0:T(8,128)S(1)}, u32[]{:S(2)}, u32[]{:S(2)}) async-start(f32[16,2,64,256]{3,2,1,0:T(8,128)} %broadcast_in_dim.109), calls=%async_computation.3 | async-start | bytes 4194304 | tf_op jit(solution)/shard_map/all_to_all | solution.py:73
  191.6 0.1 eq.55
  191.7 0.1 iota_compare_fusion.1
  191.8 0.1 broadcast_compare_fusion
  191.9 0.1 select_reduce_fusion.1
  192.0 46.8 %all-to-all-done.3 = f32[16,2,64,256]{3,2,1,0:T(8,128)S(1)} async-done(((f32[16,2,64,256]{3,2,1,0:T(8,128)}), f32[16,2,64,256]{3,2,1,0:T(8,128)S(1)}, u32[]{:S(2)}, u32[]{:S(2)}) %all-to-all-start.3) | async-done | bytes 2097184 | tf_op jit(solution)/shard_map/all_to_all | solution.py:73
  238.8 0.6 select_reduce_fusion
  239.4 0.7 add.47
  (28 shorter events, 0.1 us)
Async XLA Ops:
  0.0 18.4 %copy-start = (bf16[4,64,256]{2,1,0:T(8,128)(2,1)S(1)}, bf16[4,64,256]{2,1,0:T(8,128)(2,1)}, u32[]{:S(2)}) copy-start(bf16[4,64,256]{2,1,0:T(8,128)(2,1)} %param.7) | copy-start | bytes 393220
  0.0 25.2 %copy-start.8 = (s32[2]{0:T(128)S(1)}, s32[2]{0:T(128)}, u32[]{:S(2)}) copy-start(s32[2]{0:T(128)} %param.10) | copy-start | bytes 28
  0.0 24.6 %copy-start.7 = (s32[2]{0:T(128)S(1)}, s32[2]{0:T(128)}, u32[]{:S(2)}) copy-start(s32[2]{0:T(128)} %param.9) | copy-start | bytes 28
  20.1 29.1 %all-to-all-start = ((bf16[16,2,64,256]{3,2,1,0:T(8,128)(2,1)}), bf16[16,2,64,256]{3,2,1,0:T(8,128)(2,1)S(1)}, u32[]{:S(2)}, u32[]{:S(2)}) async-start(bf16[16,2,64,256]{3,2,1,0:T(8,128)(2,1)} %broadcast_select_fusion), calls=%async_computation | async-start | bytes 2097152 | tf_op jit(solution)/shard_map/all_to_all | solution.py:32
  24.6 34.5 %copy-start.9 = (f32[2]{0:T(128)S(1)}, f32[2]{0:T(128)}, u32[]{:S(2)}) copy-start(f32[2]{0:T(128)} %param.12) | copy-start | bytes 28
  24.6 34.5 %copy-start.6 = (s32[2,4]{1,0:T(2,128)S(1)}, s32[2,4]{1,0:T(2,128)}, u32[]{:S(2)}) copy-start(s32[2,4]{1,0:T(2,128)} %param.13) | copy-start | bytes 100
  51.4 37.8 %all-to-all-start.1 = ((bf16[16,4,64,256]{3,2,1,0:T(8,128)(2,1)}), bf16[16,4,64,256]{3,2,1,0:T(8,128)(2,1)S(1)}, u32[]{:S(2)}, u32[]{:S(2)}) async-start(bf16[16,4,64,256]{3,2,1,0:T(8,128)(2,1)} %broadcast_in_dim.104), calls=%async_computation.1 | async-start | bytes 4194304 | tf_op jit(solution)/shard_map/all_to_all | solution.py:38
  94.2 1.0 copy-start.3
  110.3 6.4 %copy-start.4 = (bf16[2,1024,256]{1,2,0:T(8,128)(2,1)S(1)}, bf16[2,1024,256]{1,2,0:T(8,128)(2,1)}, u32[]{:S(2)}) copy-start(bf16[2,1024,256]{1,2,0:T(8,128)(2,1)} %copy-done.3) | copy-start | bytes 3145732
  116.7 3.6 %copy-start.5 = (bf16[4,1024,2,1,256]{1,4,3,2,0:T(8,128)(2,1)S(1)}, bf16[4,1024,2,1,256]{1,4,3,2,0:T(8,128)(2,1)}, u32[]{:S(2)}) copy-start(bf16[4,1024,2,1,256]{1,4,3,2,0:T(8,128)(2,1)} %get-tuple-element.10) | copy-start | bytes 12582916
  120.4 2.2 copy-start.2
  182.3 57.9 %copy-start.1 = (bf16[4,64,256]{2,1,0:T(8,128)(2,1)S(1)}, bf16[4,64,256]{2,1,0:T(8,128)(2,1)}, u32[]{:S(2)}) copy-start(bf16[4,64,256]{2,1,0:T(8,128)(2,1)} %param.7) | copy-start | bytes 393220
  183.9 54.9 %all-to-all-start.3 = ((f32[16,2,64,256]{3,2,1,0:T(8,128)}), f32[16,2,64,256]{3,2,1,0:T(8,128)S(1)}, u32[]{:S(2)}, u32[]{:S(2)}) async-start(f32[16,2,64,256]{3,2,1,0:T(8,128)} %broadcast_in_dim.109), calls=%async_computation.3 | async-start | bytes 4194304 | tf_op jit(solution)/shard_map/all_to_all | solution.py:73

commit v2 on v1

v2 whole, which is shorter than its diff:
```python
import jax
import jax.numpy as jnp
from jax import lax
from jax.sharding import PartitionSpec as P

NS = 3
HI = lax.Precision.HIGHEST


def newton(correlation):
    eye = jnp.eye(correlation.shape[-1], dtype=jnp.float32)
    inverse = 2.0 * eye - correlation
    for sweep in range(NS - 1):
        product = jnp.einsum("bij,bjk->bik", correlation, inverse, precision=HI)
        inverse = jnp.einsum("bij,bjk->bik", inverse, 2.0 * eye - product, precision=HI)
    return inverse


def gather_rows(rows_local, n_orb):
    spread = jnp.broadcast_to(rows_local[None], (n_orb,) + rows_local.shape)
    got = lax.all_to_all(spread, "orb", 0, 0, tiled=True)
    count, rows, nocc = rows_local.shape
    return jnp.transpose(got, (1, 0, 2, 3)).reshape(count, n_orb * rows, nocc)


def scatter_rows(full, n_orb):
    count, total, nocc = full.shape
    parts = jnp.transpose(full.reshape(count, n_orb, total // n_orb, nocc), (1, 0, 2, 3))
    got = lax.all_to_all(parts, "orb", 0, 0, tiled=True)
    return jnp.sum(got, axis=0)


def local(orbitals, dfit, pair_left, pair_right, pair_count, pair_weight, aux_screen):
    det_local, rows, nocc = orbitals.shape
    capacity = pair_left.shape[0]
    n_det = lax.axis_size("det")
    n_orb = lax.axis_size("orb")
    me = lax.axis_index("det")
    slot_index = jnp.arange(capacity, dtype=jnp.int32)
    weights = jnp.where(slot_index < pair_count[0], pair_weight, jnp.zeros_like(pair_weight))
    left_local = pair_left % det_local
    left_rows = jnp.take(orbitals, left_local, axis=0)
    left_full = gather_rows(left_rows, n_orb)

    right_all = lax.all_to_all(
        jnp.broadcast_to(pair_right[None], (n_det, capacity)), "det", 0, 0, tiled=True
    ).reshape(n_det * capacity)
    send = jnp.take(orbitals, right_all % det_local, axis=0).reshape(n_det, capacity, rows, nocc)
    got = lax.all_to_all(send, "det", 0, 0, tiled=True)
    owner = pair_right // det_local
    right_rows = got[owner, slot_index]
    right_full = gather_rows(right_rows, n_orb)

    left_stack = jnp.transpose(left_full, (1, 0, 2)).reshape(n_orb * rows, capacity * nocc)
    projected_t = jnp.einsum(
        "qst,tk->qsk", dfit, left_stack, preferred_element_type=jnp.float32
    ).astype(jnp.bfloat16).reshape(dfit.shape[0], n_orb * rows, capacity, nocc)

    correlation = jnp.einsum("brc,brd->bcd", left_full, right_full, preferred_element_type=jnp.float32)
    inverse = newton(correlation)
    moved_full = jnp.einsum(
        "brc,bcd->brd", right_full.astype(jnp.float32), inverse, precision=HI
    ).astype(jnp.bfloat16)
    moved_stack = jnp.transpose(moved_full, (1, 0, 2)).reshape(n_orb * rows, capacity * nocc)
    applied = jnp.einsum(
        "qst,tk->qsk", dfit, moved_stack, preferred_element_type=jnp.float32
    ).astype(jnp.bfloat16).reshape(dfit.shape[0], n_orb * rows, capacity, nocc)

    exchange = jnp.einsum("qtbc,btd->bqcd", projected_t, moved_full, preferred_element_type=jnp.float32)
    factor = 2.0 * weights[:, None, None, None] * aux_screen.astype(jnp.float32)[:, :, None, None]
    scaled = (factor * exchange).astype(jnp.bfloat16)
    moved_term = jnp.einsum("qsbc,bqcd->bsd", projected_t, scaled, preferred_element_type=jnp.float32)
    moved_grad = scatter_rows(moved_term, n_orb)
    right_grad = jnp.einsum("brc,bdc->brd", moved_grad, inverse, precision=HI)

    back = jnp.broadcast_to(right_grad[None], (n_det,) + right_grad.shape)
    came = lax.all_to_all(back, "det", 0, 0, tiled=True)

    left_term = jnp.einsum("qsbc,bqdc->bsd", applied, scaled, preferred_element_type=jnp.float32)
    left_grad = scatter_rows(left_term, n_orb)
    own = left_local[:, None] == jnp.arange(det_local, dtype=jnp.int32)[None, :]
    own_sum = jnp.sum(jnp.where(own[:, :, None, None], left_grad[:, None], 0.0), axis=0)

    mine = right_all.reshape(n_det, capacity)[:, :, None] == (
        me * det_local + jnp.arange(det_local, dtype=jnp.int32)
    )[None, None, :]
    returned = jnp.sum(jnp.where(mine[:, :, :, None, None], came[:, :, None], 0.0), axis=(0, 1))
    return own_sum + returned


def solution(mesh):
    in_specs = (
        P("det", "orb", None),
        P("orb", None, None),
        P("det"),
        P("det"),
        P("det"),
        P("det"),
        P("det", "orb"),
    )
    out_specs = P("det", "orb", None)
    return jax.shard_map(local, mesh=mesh, in_specs=in_specs, out_specs=out_specs, check_vma=False)
```

time: 244 us -> 241 us (0.988)
  blocking collectives: 70.5 us -> 0 us
  waiting for transfers between devices: 101 us -> 139 us
  starting transfers between devices: 19.2 us -> 45.3 us
  matrix products: 22.8 us -> 28.2 us
  local copies, waits for them, and re-layouts: 19.5 us -> 14.5 us
  other arithmetic: 5.94 us -> 8.47 us
    all_to_all x1 -> x0, blocking collectives: 55.1 us -> none  [local(): parts = lax.all_to_all(terms, 'orb', 0, 0, tiled=True)]
    all_to_all x1 -> x5, waiting for transfers between devices: 29.9 us -> 70.8 us  [the longest x2 43.1 us: scatter_rows(): got = lax.all_to_all(parts, 'orb', 0, 0, tiled=True)]
    all_to_all x1 -> x5, starting transfers between devices: 7.03 us -> 27.3 us  [the longest x2 10.8 us: gather_rows(): got = lax.all_to_all(spread, 'orb', 0, 0, tiled=True)]
    unnamed x1 -> x0, blocking collectives: 15.4 us -> none
    unnamed x24 -> x20, local copies, waits for them, and re-layouts: 9.85 us -> 2.31 us
    dot_general x1 -> x2, matrix products: 11.3 us -> 18.5 us  [the longest x1 10.2 us: local(): jnp.einsum('qst,tk->qsk', dfit, left_stack, preferred_element_type=jnp.fl...]
    all_to_all x1, starting transfers between devices: 7.74 us -> 13.2 us  [local(): came = lax.all_to_all(back, 'det', 0, 0, tiled=True)]
    slice x3 -> x0, local copies, waits for them, and re-layouts: 4.4 us -> none  [the longest x1 3.73 us: local(): applied = product[:, :, :, 0]]
  transfers between devices with their start and end apart: 3 -> 7, of which waited for: 3 -> 7; matrix products, arithmetic and copies ran while one was open for 0% -> 13% of each run, Pallas kernels for 0% -> 0%
where the time goes in v2:
time: 241 us; the launch traced here: 237 us
  waiting for transfers between devices  139 us (58%)
  starting transfers between devices  45.3 us (19%)
  matrix products  28.2 us (12%)
  local copies, waits for them, and re-layouts  14.5 us (6%)
  other arithmetic  8.47 us (4%)
    all_to_all x1, waiting for transfers between devices, local(): came = lax.all_to_all(back, 'det', 0, 0, tiled=True)  46.8 us
    all_to_all x2, waiting for transfers between devices, scatter_rows(): got = lax.all_to_all(parts, 'orb', 0, 0, tiled=True)  43.1 us
    all_to_all x2, waiting for transfers between devices, gather_rows(): got = lax.all_to_all(spread, 'orb', 0, 0, tiled=True)  23 us
    all_to_all x1, waiting for transfers between devices, local(): got = lax.all_to_all(send, 'det', 0, 0, tiled=True)  21.8 us
    all_to_all x1, starting transfers between devices, local(): came = lax.all_to_all(back, 'det', 0, 0, tiled=True)  13.2 us
    all_to_all x2, starting transfers between devices, gather_rows(): got = lax.all_to_all(spread, 'orb', 0, 0, tiled=True)  10.8 us
    dot_general x1, matrix products, local(): jnp.einsum('qst,tk->qsk', dfit, left_stack, preferred_element_type=jnp.fl...  10.2 us
    all_to_all x1, starting transfers between devices, local(): lax.all_to_all(jnp.broadcast_to(pair_right[None], (n_det, capacity)), 'de...  8.59 us
  transfers between devices with their start and end apart: 7, of which 7 were waited for; matrix products, arithmetic and copies ran while one was open for 13% of the time, Pallas kernels for 0%

profile of v2, /device:TPU:32, one launch (start us, length us, event | category | flops | bytes accessed | tf_op | source)
XLA Modules:
  0.0 236.8 jit_solution(202805419208031336)
XLA Ops:
  0.0 1.3 broadcast_in_dim.103
  1.3 8.6 %all-to-all-start = ((s32[16,1,2]{2,1,0:T(1,128)}), s32[16,1,2]{2,1,0:T(1,128)S(1)}, u32[]{:S(2)}, u32[]{:S(2)}) async-start(s32[16,1,2]{2,1,0:T(1,128)} %broadcast_in_dim.103), calls=%async_computation | async-start | bytes 16384 | tf_op jit(solution)/shard_map/all_to_all | solution.py:45
  9.9 0.7 compare_and_fusion
  10.6 0.6 gather_fusion.2
  11.2 4.8 %all-to-all-done = s32[16,1,2]{2,1,0:T(1,128)S(1)} async-done(((s32[16,1,2]{2,1,0:T(1,128)}), s32[16,1,2]{2,1,0:T(1,128)S(1)}, u32[]{:S(2)}, u32[]{:S(2)}) %all-to-all-start) | async-done | bytes 160 | tf_op jit(solution)/shard_map/all_to_all | solution.py:45
  16.0 1.1 broadcast_in_dim.111
  17.2 7.2 %all-to-all-start.3 = ((bf16[16,2,64,256]{3,2,1,0:T(8,128)(2,1)}), bf16[16,2,64,256]{3,2,1,0:T(8,128)(2,1)S(1)}, u32[]{:S(2)}, u32[]{:S(2)}) async-start(bf16[16,2,64,256]{3,2,1,0:T(8,128)(2,1)} %broadcast_in_dim.111), calls=%async_computation.3 | async-start | bytes 2097152 | tf_op jit(solution)/shard_map/all_to_all | solution.py:21
  24.4 0.1 copy.44
  24.6 0.5 broadcast.240
  25.1 0.7 reduce.3
  25.9 0.6 gather_fusion
  26.5 1.1 broadcast_select_fusion
  27.6 14.5 %all-to-all-done.3 = bf16[16,2,64,256]{3,2,1,0:T(8,128)(2,1)S(1)} async-done(((bf16[16,2,64,256]{3,2,1,0:T(8,128)(2,1)}), bf16[16,2,64,256]{3,2,1,0:T(8,128)(2,1)S(1)}, u32[]{:S(2)}, u32[]{:S(2)}) %all-to-all-start.3) | async-done | bytes 1048608 | tf_op jit(solution)/shard_map/all_to_all | solution.py:21
  42.2 4.9 %all-to-all-start.1 = ((bf16[16,2,64,256]{3,2,1,0:T(8,128)(2,1)}), bf16[16,2,64,256]{3,2,1,0:T(8,128)(2,1)S(1)}, u32[]{:S(2)}, u32[]{:S(2)}) async-start(bf16[16,2,64,256]{3,2,1,0:T(8,128)(2,1)} %broadcast_select_fusion), calls=%async_computation.1 | async-start | bytes 2097152 | tf_op jit(solution)/shard_map/all_to_all | solution.py:49
  47.8 0.7 fusion.16
  48.6 1.3 copy.49
  49.9 21.8 %all-to-all-done.1 = bf16[16,2,64,256]{3,2,1,0:T(8,128)(2,1)S(1)} async-done(((bf16[16,2,64,256]{3,2,1,0:T(8,128)(2,1)}), bf16[16,2,64,256]{3,2,1,0:T(8,128)(2,1)S(1)}, u32[]{:S(2)}, u32[]{:S(2)}) %all-to-all-start.1) | async-done | bytes 1048608 | tf_op jit(solution)/shard_map/all_to_all | solution.py:49
  71.7 0.6 gather_fusion.1
  72.3 1.1 broadcast_in_dim.107
  73.4 3.7 %all-to-all-start.2 = ((bf16[16,2,64,256]{3,2,1,0:T(8,128)(2,1)}), bf16[16,2,64,256]{3,2,1,0:T(8,128)(2,1)S(1)}, u32[]{:S(2)}, u32[]{:S(2)}) async-start(bf16[16,2,64,256]{3,2,1,0:T(8,128)(2,1)} %broadcast_in_dim.107), calls=%async_computation.2 | async-start | bytes 2097152 | tf_op jit(solution)/shard_map/all_to_all | solution.py:21
  77.0 10.2 %convolution_convert_fusion = bf16[512,4,1024]{2,0,1:T(8,128)(2,1)} fusion(bf16[1024,512,1]{0,1,2:T(8,128)(2,1)} %bitcast.81, bf16[4,1024,1024]{2,1,0:T(8,128)(2,1)} %param.8), kind=kOutput, calls=%fused_computation.6 | convolution fusion | flops 4297064448 | bytes 13631488 | tf_op jit(solution)/shard_map/qst,tk->qsk/dot_general | solution.py:55
  87.2 8.4 %all-to-all-done.2 = bf16[16,2,64,256]{3,2,1,0:T(8,128)(2,1)S(1)} async-done(((bf16[16,2,64,256]{3,2,1,0:T(8,128)(2,1)}), bf16[16,2,64,256]{3,2,1,0:T(8,128)(2,1)S(1)}, u32[]{:S(2)}, u32[]{:S(2)}) %all-to-all-start.2) | async-done | bytes 1048608 | tf_op jit(solution)/shard_map/all_to_all | solution.py:21
  95.8 0.5 fusion.25
  96.3 0.7 convolution_subtract_fusion.1
  97.0 0.7 fusion.9
  97.7 0.7 convolution_subtract_fusion
  98.4 0.7 fusion.26
  99.0 1.0 convolution_convert_fusion.2
  100.1 0.9 copy-done.2
  101.0 1.3 multiply_convert_fusion
  102.3 1.8 fusion.5
  104.1 1.5 copy.76
  105.6 3.9 %all-to-all-start.5 = ((f32[16,2,64,256]{3,2,1,0:T(8,128)}), f32[16,2,64,256]{3,2,1,0:T(8,128)S(1)}, u32[]{:S(2)}, u32[]{:S(2)}) async-start(f32[16,2,64,256]{3,2,1,0:T(8,128)} %bitcast.76), calls=%async_computation.5 | async-start | bytes 4194304 | tf_op jit(solution)/shard_map/all_to_all | solution.py:29
  109.5 8.3 %convolution_convert_fusion.1 = bf16[512,4,1024]{2,0,1:T(8,128)(2,1)S(1)} fusion(bf16[1024,512,1]{0,1,2:T(8,128)(2,1)} %bitcast.82, bf16[4,1024,1024]{2,1,0:T(8,128)(2,1)} %param.8), kind=kOutput, calls=%fused_computation.7 | convolution fusion | flops 4297064448 | bytes 13631488 | tf_op jit(solution)/shard_map/qst,tk->qsk/dot_general | solution.py:65
  117.8 1.8 fusion.7
  119.6 1.5 copy.77
  121.1 17.7 %all-to-all-done.5 = f32[16,2,64,256]{3,2,1,0:T(8,128)S(1)} async-done(((f32[16,2,64,256]{3,2,1,0:T(8,128)}), f32[16,2,64,256]{3,2,1,0:T(8,128)S(1)}, u32[]{:S(2)}, u32[]{:S(2)}) %all-to-all-start.5) | async-done | bytes 2097184 | tf_op jit(solution)/shard_map/all_to_all | solution.py:29
  138.8 1.3 copy-done.1
  140.1 4.0 %all-to-all-start.4 = ((f32[16,2,64,256]{3,2,1,0:T(8,128)}), f32[16,2,64,256]{3,2,1,0:T(8,128)S(1)}, u32[]{:S(2)}, u32[]{:S(2)}) async-start(f32[16,2,64,256]{3,2,1,0:T(8,128)} %bitcast.75), calls=%async_computation.4 | async-start | bytes 4194304 | tf_op jit(solution)/shard_map/all_to_all | solution.py:29
  144.1 1.7 reduce_sum.38
  145.8 0.6 fusion.27
  146.4 25.4 %all-to-all-done.4 = f32[16,2,64,256]{3,2,1,0:T(8,128)S(1)} async-done(((f32[16,2,64,256]{3,2,1,0:T(8,128)}), f32[16,2,64,256]{3,2,1,0:T(8,128)S(1)}, u32[]{:S(2)}, u32[]{:S(2)}) %all-to-all-start.4) | async-done | bytes 2097184 | tf_op jit(solution)/shard_map/all_to_all | solution.py:29
  171.8 1.6 broadcast_in_dim.115
  173.4 13.2 %all-to-all-start.6 = ((f32[16,2,64,256]{3,2,1,0:T(8,128)}), f32[16,2,64,256]{3,2,1,0:T(8,128)}, u32[]{:S(2)}, u32[]{:S(2)}) async-start(f32[16,2,64,256]{3,2,1,0:T(8,128)} %broadcast_in_dim.115), calls=%async_computation.6 | async-start | bytes 4194304 | tf_op jit(solution)/shard_map/all_to_all | solution.py:77
  186.8 0.1 reduce_sum.36
  187.0 46.8 %all-to-all-done.6 = f32[16,2,64,256]{3,2,1,0:T(8,128)} async-done(((f32[16,2,64,256]{3,2,1,0:T(8,128)}), f32[16,2,64,256]{3,2,1,0:T(8,128)}, u32[]{:S(2)}, u32[]{:S(2)}) %all-to-all-start.6) | async-done | bytes 2097184 | tf_op jit(solution)/shard_map/all_to_all | solution.py:77
  233.8 2.2 select_reduce_fusion
  236.1 0.7 add.73
  (36 shorter events, 1.0 us)
Async XLA Ops:
  0.0 10.6 %copy-start = (bf16[4,64,256]{2,1,0:T(8,128)(2,1)S(1)}, bf16[4,64,256]{2,1,0:T(8,128)(2,1)}, u32[]{:S(2)}) copy-start(bf16[4,64,256]{2,1,0:T(8,128)(2,1)} %param.7) | copy-start | bytes 393220
  1.3 14.7 %all-to-all-start = ((s32[16,1,2]{2,1,0:T(1,128)}), s32[16,1,2]{2,1,0:T(1,128)S(1)}, u32[]{:S(2)}, u32[]{:S(2)}) async-start(s32[16,1,2]{2,1,0:T(1,128)} %broadcast_in_dim.103), calls=%async_computation | async-start | bytes 16384 | tf_op jit(solution)/shard_map/all_to_all | solution.py:45
  10.6 0.6 copy-start.6
  17.2 30.6 %copy-start.4 = (s32[2]{0:T(128)S(1)}, s32[2]{0:T(128)}, u32[]{:S(2)}) copy-start(s32[2]{0:T(128)} %param.10) | copy-start | bytes 28
  17.2 31.3 %copy-start.3 = (s32[2,4]{1,0:T(2,128)S(1)}, s32[2,4]{1,0:T(2,128)}, u32[]{:S(2)}) copy-start(s32[2,4]{1,0:T(2,128)} %param.13) | copy-start | bytes 100
  17.2 25.0 %all-to-all-start.3 = ((bf16[16,2,64,256]{3,2,1,0:T(8,128)(2,1)}), bf16[16,2,64,256]{3,2,1,0:T(8,128)(2,1)S(1)}, u32[]{:S(2)}, u32[]{:S(2)}) async-start(bf16[16,2,64,256]{3,2,1,0:T(8,128)(2,1)} %broadcast_in_dim.111), calls=%async_computation.3 | async-start | bytes 2097152 | tf_op jit(solution)/shard_map/all_to_all | solution.py:21
  42.2 29.5 %all-to-all-start.1 = ((bf16[16,2,64,256]{3,2,1,0:T(8,128)(2,1)}), bf16[16,2,64,256]{3,2,1,0:T(8,128)(2,1)S(1)}, u32[]{:S(2)}, u32[]{:S(2)}) async-start(bf16[16,2,64,256]{3,2,1,0:T(8,128)(2,1)} %broadcast_select_fusion), calls=%async_computation.1 | async-start | bytes 2097152 | tf_op jit(solution)/shard_map/all_to_all | solution.py:49
  73.4 22.3 %all-to-all-start.2 = ((bf16[16,2,64,256]{3,2,1,0:T(8,128)(2,1)}), bf16[16,2,64,256]{3,2,1,0:T(8,128)(2,1)S(1)}, u32[]{:S(2)}, u32[]{:S(2)}) async-start(bf16[16,2,64,256]{3,2,1,0:T(8,128)(2,1)} %broadcast_in_dim.107), calls=%async_computation.2 | async-start | bytes 2097152 | tf_op jit(solution)/shard_map/all_to_all | solution.py:21
  97.0 4.0 %copy-start.5 = (bf16[512,4,1024]{2,0,1:T(8,128)(2,1)S(1)}, bf16[512,4,1024]{2,0,1:T(8,128)(2,1)}, u32[]{:S(2)}) copy-start(bf16[512,4,1024]{2,0,1:T(8,128)(2,1)} %convolution_convert_fusion) | copy-start | bytes 12582916
  100.1 1.0 copy-start.2
  102.3 3.3 %copy-start.8 = (bf16[2,4,256,256]{3,2,1,0:T(8,128)(2,1)}, bf16[2,4,256,256]{3,2,1,0:T(8,128)(2,1)S(1)}, u32[]{:S(2)}) copy-start(bf16[2,4,256,256]{3,2,1,0:T(8,128)(2,1)S(1)} %multiply_convert_fusion) | copy-start | bytes 3145732
  105.6 33.2 %all-to-all-start.5 = ((f32[16,2,64,256]{3,2,1,0:T(8,128)}), f32[16,2,64,256]{3,2,1,0:T(8,128)S(1)}, u32[]{:S(2)}, u32[]{:S(2)}) async-start(f32[16,2,64,256]{3,2,1,0:T(8,128)} %bitcast.76), calls=%async_computation.5 | async-start | bytes 4194304 | tf_op jit(solution)/shard_map/all_to_all | solution.py:29
  109.5 8.3 %copy-start.9 = (bf16[2,4,256,256]{3,2,1,0:T(8,128)(2,1)S(1)}, bf16[2,4,256,256]{3,2,1,0:T(8,128)(2,1)}, u32[]{:S(2)}) copy-start(bf16[2,4,256,256]{3,2,1,0:T(8,128)(2,1)} %copy-done.8) | copy-start | bytes 3145732
  138.8 1.3 copy-start.1
  140.1 31.7 %all-to-all-start.4 = ((f32[16,2,64,256]{3,2,1,0:T(8,128)}), f32[16,2,64,256]{3,2,1,0:T(8,128)S(1)}, u32[]{:S(2)}, u32[]{:S(2)}) async-start(f32[16,2,64,256]{3,2,1,0:T(8,128)} %bitcast.75), calls=%async_computation.4 | async-start | bytes 4194304 | tf_op jit(solution)/shard_map/all_to_all | solution.py:29
  144.1 42.4 %copy-start.7 = (s32[2]{0:T(128)S(1)}, s32[2]{0:T(128)}, u32[]{:S(2)}) copy-start(s32[2]{0:T(128)} %copy-done.6) | copy-start | bytes 28
  173.4 60.5 %all-to-all-start.6 = ((f32[16,2,64,256]{3,2,1,0:T(8,128)}), f32[16,2,64,256]{3,2,1,0:T(8,128)}, u32[]{:S(2)}, u32[]{:S(2)}) async-start(f32[16,2,64,256]{3,2,1,0:T(8,128)} %broadcast_in_dim.115), calls=%async_computation.6 | async-start | bytes 4194304 | tf_op jit(solution)/shard_map/all_to_all | solution.py:77

commit v3 on v2

--- a/solution.py
+++ b/solution.py
@@ -40,15 +40,13 @@
     weights = jnp.where(slot_index < pair_count[0], pair_weight, jnp.zeros_like(pair_weight))
     left_local = pair_left % det_local
     left_rows = jnp.take(orbitals, left_local, axis=0)
+
+    marks = jnp.zeros((1, rows * nocc), jnp.bfloat16).at[0, :capacity].set(pair_right.astype(jnp.bfloat16))
+    carried = jnp.concatenate([orbitals, marks.reshape(1, rows, nocc)], axis=0)
+    everyone = lax.all_gather(carried, "det", axis=0, tiled=False)
+    right_all = everyone[:, det_local].reshape(n_det, rows * nocc)[:, :capacity].astype(jnp.int32).reshape(-1)
     left_full = gather_rows(left_rows, n_orb)
-
-    right_all = lax.all_to_all(
-        jnp.broadcast_to(pair_right[None], (n_det, capacity)), "det", 0, 0, tiled=True
-    ).reshape(n_det * capacity)
-    send = jnp.take(orbitals, right_all % det_local, axis=0).reshape(n_det, capacity, rows, nocc)
-    got = lax.all_to_all(send, "det", 0, 0, tiled=True)
-    owner = pair_right // det_local
-    right_rows = got[owner, slot_index]
+    right_rows = everyone[pair_right // det_local, pair_right % det_local]
     right_full = gather_rows(right_rows, n_orb)
 
     left_stack = jnp.transpose(left_full, (1, 0, 2)).reshape(n_orb * rows, capacity * nocc)
@@ -73,17 +71,15 @@
     moved_grad = scatter_rows(moved_term, n_orb)
     right_grad = jnp.einsum("brc,bdc->brd", moved_grad, inverse, precision=HI)
 
-    back = jnp.broadcast_to(right_grad[None], (n_det,) + right_grad.shape)
-    came = lax.all_to_all(back, "det", 0, 0, tiled=True)
+    came = lax.all_gather(right_grad, "det", axis=0, tiled=False)
 
     left_term = jnp.einsum("qsbc,bqdc->bsd", applied, scaled, preferred_element_type=jnp.float32)
     left_grad = scatter_rows(left_term, n_orb)
     own = left_local[:, None] == jnp.arange(det_local, dtype=jnp.int32)[None, :]
     own_sum = jnp.sum(jnp.where(own[:, :, None, None], left_grad[:, None], 0.0), axis=0)
 
-    mine = right_all.reshape(n_det, capacity)[:, :, None] == (
-        me * det_local + jnp.arange(det_local, dtype=jnp.int32)
-    )[None, None, :]
+    asked = right_all.reshape(n_det, capacity)
+    mine = asked[:, :, None] == (me * det_local + jnp.arange(det_local, dtype=jnp.int32))[None, None, :]
     returned = jnp.sum(jnp.where(mine[:, :, :, None, None], came[:, :, None], 0.0), axis=(0, 1))
     return own_sum + returned
 

time: 241 us -> 176 us (0.73); the launches traced: 237 us -> 175 us
  waiting for transfers between devices: 139 us -> 65.5 us
  blocking collectives: 0 us -> 30.6 us
  starting transfers between devices: 45.3 us -> 17.7 us
  between operations: 0.98 us -> 14.4 us
  local copies, waits for them, and re-layouts: 14.5 us -> 10.6 us
    all_to_all x3 -> x0, waiting for transfers between devices: 73.4 us -> none  [the longest x1 46.8 us: local(): came = lax.all_to_all(back, 'det', 0, 0, tiled=True)]
    all_to_all x0 -> x1, blocking collectives: none -> 30.6 us  [scatter_rows(): got = lax.all_to_all(parts, 'orb', 0, 0, tiled=True)]
    all_to_all x3 -> x0, starting transfers between devices: 26.6 us -> none  [the longest x1 13.2 us: local(): came = lax.all_to_all(back, 'det', 0, 0, tiled=True)]
    all_to_all x2 -> x1, waiting for transfers between devices: 43.1 us -> 26.2 us  [scatter_rows(): got = lax.all_to_all(parts, 'orb', 0, 0, tiled=True)]
    all_gather x0 -> x2, waiting for transfers between devices: none -> 13.6 us  [the longest x1 13.6 us: local(): everyone = lax.all_gather(carried, 'det', axis=0, tiled=False)]
    all_to_all x2 -> x1, starting transfers between devices: 7.85 us -> 3.72 us  [scatter_rows(): got = lax.all_to_all(parts, 'orb', 0, 0, tiled=True)]
    all_to_all x2, starting transfers between devices: 10.8 us -> 14 us  [gather_rows(): got = lax.all_to_all(spread, 'orb', 0, 0, tiled=True)]
    broadcast_in_dim x2 -> x0, local copies, waits for them, and re-layouts: 2.85 us -> none  [the longest x1 1.56 us: local(): back = jnp.broadcast_to(right_grad[None], (n_det,) + right_grad.shape)]
  transfers between devices with their start and end apart: 7 -> 5, of which waited for: 7 -> 4; matrix products, arithmetic and copies ran while one was open for 13% -> 15% of each run, Pallas kernels for 0% -> 0%
where the time goes in v3:
time: 176 us; the launch traced here: 175 us
  waiting for transfers between devices  65.5 us (37%)
  blocking collectives  30.6 us (17%)
  matrix products  28.2 us (16%)
  starting transfers between devices  17.7 us (10%)
  between operations  14.4 us (8%)
  local copies, waits for them, and re-layouts  10.6 us (6%)
  other arithmetic  7.92 us (4%)
    all_to_all x1, blocking collectives, scatter_rows(): got = lax.all_to_all(parts, 'orb', 0, 0, tiled=True)  30.6 us
    all_to_all x1, waiting for transfers between devices, scatter_rows(): got = lax.all_to_all(parts, 'orb', 0, 0, tiled=True)  26.2 us
    all_to_all x2, waiting for transfers between devices, gather_rows(): got = lax.all_to_all(spread, 'orb', 0, 0, tiled=True)  25.6 us
    all_to_all x2, starting transfers between devices, gather_rows(): got = lax.all_to_all(spread, 'orb', 0, 0, tiled=True)  14 us
    all_gather x1, waiting for transfers between devices, local(): everyone = lax.all_gather(carried, 'det', axis=0, tiled=False)  13.6 us
    dot_general x1, matrix products, local(): jnp.einsum('qst,tk->qsk', dfit, left_stack, preferred_element_type=jnp.fl...  9.45 us
    dot_general x1, matrix products, local(): jnp.einsum('qst,tk->qsk', dfit, moved_stack, preferred_element_type=jnp.f...  8.32 us
    all_to_all x1, starting transfers between devices, scatter_rows(): got = lax.all_to_all(parts, 'orb', 0, 0, tiled=True)  3.72 us
  transfers between devices with their start and end apart: 5, of which 4 were waited for; matrix products, arithmetic and copies ran while one was open for 15% of the time, Pallas kernels for 0%

profile of v3, /device:TPU:32, one launch (start us, length us, event | category | flops | bytes accessed | tf_op | source)
XLA Modules:
  0.0 175.0 jit_solution(13580288851838503229)
XLA Ops:
  6.5 0.6 compare_reduce_fusion
  7.2 1.3 fusion.15
  8.5 0.1 pad_reduce_fusion
  8.6 1.6 pad_maximum_fusion
  10.2 0.7 compare_and_fusion
  10.9 1.5 gather_fusion.1
  12.3 0.1 broadcast_select_fusion
  12.4 1.1 broadcast_in_dim.90
  13.5 7.0 %all-to-all-start.1 = ((bf16[16,2,64,256]{3,2,1,0:T(8,128)(2,1)}), bf16[16,2,64,256]{3,2,1,0:T(8,128)(2,1)S(1)}, u32[]{:S(2)}, u32[]{:S(2)}) async-start(bf16[16,2,64,256]{3,2,1,0:T(8,128)(2,1)} %broadcast_in_dim.90), calls=%async_computation.1 | async-start | bytes 2097152 | tf_op jit(solution)/shard_map/all_to_all | solution.py:21
  21.3 0.1 convert_multiply_fusion
  21.4 16.9 %all-to-all-done.1 = bf16[16,2,64,256]{3,2,1,0:T(8,128)(2,1)S(1)} async-done(((bf16[16,2,64,256]{3,2,1,0:T(8,128)(2,1)}), bf16[16,2,64,256]{3,2,1,0:T(8,128)(2,1)S(1)}, u32[]{:S(2)}, u32[]{:S(2)}) %all-to-all-start.1) | async-done | bytes 1048608 | tf_op jit(solution)/shard_map/all_to_all | solution.py:21
  38.3 0.1 copy.35
  38.4 0.5 copy.38
  39.0 13.6 %all-gather.5.cloned.1.call-done = bf16[80,64,256]{2,1,0:T(8,128)(2,1)} async-done(((bf16[5,64,256]{2,1,0:T(8,128)(2,1)}), bf16[80,64,256]{2,1,0:T(8,128)(2,1)}) %all-gather.5.cloned.1.call-update) | async-done | bytes 2621456 | tf_op jit(solution)/shard_map/all_gather | solution.py:46
  52.6 2.3 %gather_fusion = bf16[2,64,256]{2,1,0:T(8,128)(2,1)S(1)} fusion(bf16[16,5,64,256]{3,2,1,0:T(8,128)(2,1)} %bitcast.79, s32[2]{0:T(128)S(1)} %fusion.20), kind=kCustom, calls=%fused_computation | custom fusion | bytes 131088 | tf_op jit(solution)/shard_map/gather | solution.py:49
  54.9 1.1 broadcast_in_dim.86
  56.0 7.0 %all-to-all-start = ((bf16[16,2,64,256]{3,2,1,0:T(8,128)(2,1)}), bf16[16,2,64,256]{3,2,1,0:T(8,128)(2,1)S(1)}, u32[]{:S(2)}, u32[]{:S(2)}) async-start(bf16[16,2,64,256]{3,2,1,0:T(8,128)(2,1)} %broadcast_in_dim.86), calls=%async_computation | async-start | bytes 2097152 | tf_op jit(solution)/shard_map/all_to_all | solution.py:21
  62.9 0.0 all-gather.7.cloned.1.call-start
  63.0 9.5 %convolution_convert_fusion = bf16[512,4,1024]{2,0,1:T(8,128)(2,1)} fusion(bf16[1024,512,1]{0,1,2:T(8,128)(2,1)S(1)} %bitcast.77, bf16[4,1024,1024]{2,1,0:T(8,128)(2,1)} %param.10), kind=kOutput, calls=%fused_computation.5 | convolution fusion | flops 4297064448 | bytes 13631488 | tf_op jit(solution)/shard_map/qst,tk->qsk/dot_general | solution.py:53
  72.4 8.7 %all-to-all-done = bf16[16,2,64,256]{3,2,1,0:T(8,128)(2,1)S(1)} async-done(((bf16[16,2,64,256]{3,2,1,0:T(8,128)(2,1)}), bf16[16,2,64,256]{3,2,1,0:T(8,128)(2,1)S(1)}, u32[]{:S(2)}, u32[]{:S(2)}) %all-to-all-start) | async-done | bytes 1048608 | tf_op jit(solution)/shard_map/all_to_all | solution.py:21
  81.1 0.1 copy.34
  81.2 0.5 fusion.23
  81.7 0.7 convolution_subtract_fusion.1
  82.4 0.7 fusion.9
  83.1 0.7 convolution_subtract_fusion
  83.8 0.7 fusion.24
  84.4 1.1 convolution_convert_fusion.2
  85.5 0.9 copy-done
  86.5 1.3 multiply_convert_fusion
  87.8 1.8 %fusion.5 = f32[2,1024,256,1]{2,1,0,3:T(8,128)S(1)} fusion(bf16[4,1024,2,256]{1,3,2,0:T(8,128)(2,1)S(1)} %bitcast.82, bf16[2,4,256,256]{3,2,1,0:T(8,128)(2,1)S(1)} %multiply_convert_fusion), kind=kOutput, calls=%fused_computation.14 | convolution fusion | flops 1073741824 | bytes 7340032 | tf_op jit(solution)/shard_map/qsbc,bqcd->bsd/dot_general | solution.py:70
  89.6 0.2 copy.65
  89.7 30.6 %all_to_all.20 = f32[16,2,64,256]{3,2,1,0:T(8,128)S(1)} all-to-all(f32[16,2,64,256]{3,2,1,0:T(8,128)S(1)} %bitcast.70), channel_id=1, replica_groups=mesh['det'=16,'orb'=16] {'orb'}, dimensions={0} | all-to-all | bytes 4194304 | tf_op jit(solution)/shard_map/all_to_all | solution.py:29
  120.4 0.1 reduce_sum.38
  120.5 1.3 fusion.25
  121.8 8.3 %convolution_convert_fusion.1 = bf16[512,4,1024]{2,0,1:T(8,128)(2,1)S(1)} fusion(bf16[1024,512,1]{0,1,2:T(8,128)(2,1)} %bitcast.76, bf16[4,1024,1024]{2,1,0:T(8,128)(2,1)} %param.10), kind=kOutput, calls=%fused_computation.6 | convolution fusion | flops 4297064448 | bytes 13631488 | tf_op jit(solution)/shard_map/qst,tk->qsk/dot_general | solution.py:63
  130.1 1.8 %fusion.7 = f32[2,1024,256,1]{2,1,0,3:T(8,128)S(1)} fusion(bf16[4,1024,2,256]{1,3,2,0:T(8,128)(2,1)S(1)} %bitcast.83, bf16[2,4,256,256]{3,2,1,0:T(8,128)(2,1)S(1)} %copy-done.6), kind=kOutput, calls=%fused_computation.16 | convolution fusion | flops 1073741824 | bytes 7340032 | tf_op jit(solution)/shard_map/qsbc,bqdc->bsd/dot_general | solution.py:76
  131.9 1.4 copy.66
  133.4 3.7 %all-to-all-start.2 = ((f32[16,2,64,256]{3,2,1,0:T(8,128)}), f32[16,2,64,256]{3,2,1,0:T(8,128)S(1)}, u32[]{:S(2)}, u32[]{:S(2)}) async-start(f32[16,2,64,256]{3,2,1,0:T(8,128)} %bitcast.69), calls=%async_computation.2 | async-start | bytes 4194304 | tf_op jit(solution)/shard_map/all_to_all | solution.py:29
  137.1 0.1 iota_compare_fusion.1
  137.2 1.1 slice.28
  138.3 0.3 copy.54
  138.6 0.1 broadcast_compare_fusion
  138.7 26.2 %all-to-all-done.2 = f32[16,2,64,256]{3,2,1,0:T(8,128)S(1)} async-done(((f32[16,2,64,256]{3,2,1,0:T(8,128)}), f32[16,2,64,256]{3,2,1,0:T(8,128)S(1)}, u32[]{:S(2)}, u32[]{:S(2)}) %all-to-all-start.2) | async-done | bytes 2097184 | tf_op jit(solution)/shard_map/all_to_all | solution.py:29
  164.9 0.1 reduce_sum.36
  165.0 0.1 select_reduce_fusion.1
  165.1 0.0 all-gather.7.cloned.1.call-done
  165.2 2.2 %select_reduce_fusion = f32[4,64,256]{2,1,0:T(8,128)S(1)} fusion(f32[16,2,64,256]{3,2,1,0:T(8,128)} %bitcast.72, pred[16,2,4]{2,1,0:T(4,128)(4,1)S(1)} %broadcast_compare_fusion), kind=kLoop, calls=%fused_computation.2 | loop fusion | flops 4128768 | bytes 2359424 | tf_op jit(solution)/shard_map/reduce_sum | solution.py:83
  167.4 0.7 add.45
  (24 shorter events, 0.1 us)
Async XLA Ops:
  6.5 14.7 %copy-start.2 = (s32[2]{0:T(128)S(1)}, s32[2]{0:T(128)}, u32[]{:S(2)}) copy-start(s32[2]{0:T(128)} %param.12) | copy-start | bytes 28
  6.5 14.7 %copy-start.3 = (f32[2]{0:T(128)S(1)}, f32[2]{0:T(128)}, u32[]{:S(2)}) copy-start(f32[2]{0:T(128)} %param.14) | copy-start | bytes 28
  6.5 14.8 %copy-start.1 = (s32[2,4]{1,0:T(2,128)S(1)}, s32[2,4]{1,0:T(2,128)}, u32[]{:S(2)}) copy-start(s32[2,4]{1,0:T(2,128)} %param.15) | copy-start | bytes 100
  6.5 46.0 %all-gather.5.cloned.1.call-start = ((), (), s32[]{:S(2)}) async-start(), calls=%async_computation.4 | async-start | bytes 2785280 | tf_op jit(solution)/shard_map/all_gather | solution.py:46
  13.5 24.8 %all-to-all-start.1 = ((bf16[16,2,64,256]{3,2,1,0:T(8,128)(2,1)}), bf16[16,2,64,256]{3,2,1,0:T(8,128)(2,1)S(1)}, u32[]{:S(2)}, u32[]{:S(2)}) async-start(bf16[16,2,64,256]{3,2,1,0:T(8,128)(2,1)} %broadcast_in_dim.90), calls=%async_computation.1 | async-start | bytes 2097152 | tf_op jit(solution)/shard_map/all_to_all | solution.py:21
  56.0 25.2 %all-to-all-start = ((bf16[16,2,64,256]{3,2,1,0:T(8,128)(2,1)}), bf16[16,2,64,256]{3,2,1,0:T(8,128)(2,1)S(1)}, u32[]{:S(2)}, u32[]{:S(2)}) async-start(bf16[16,2,64,256]{3,2,1,0:T(8,128)(2,1)} %broadcast_in_dim.86), calls=%async_computation | async-start | bytes 2097152 | tf_op jit(solution)/shard_map/all_to_all | solution.py:21
  62.9 102.2 %all-gather.7.cloned.1.call-start = ((), (), s32[]{:S(2)}) async-start(), calls=%async_computation.5 | async-start | bytes 2228224 | tf_op jit(solution)/shard_map/all_gather | solution.py:74
  82.4 4.1 %copy-start.4 = (bf16[512,4,1024]{2,0,1:T(8,128)(2,1)S(1)}, bf16[512,4,1024]{2,0,1:T(8,128)(2,1)}, u32[]{:S(2)}) copy-start(bf16[512,4,1024]{2,0,1:T(8,128)(2,1)} %convolution_convert_fusion) | copy-start | bytes 12582916
  85.5 1.0 copy-start
  87.7 2.0 %copy-start.5 = (bf16[2,4,256,256]{3,2,1,0:T(8,128)(2,1)}, bf16[2,4,256,256]{3,2,1,0:T(8,128)(2,1)S(1)}, u32[]{:S(2)}) copy-start(bf16[2,4,256,256]{3,2,1,0:T(8,128)(2,1)S(1)} %multiply_convert_fusion) | copy-start | bytes 3145732
  121.8 8.3 %copy-start.6 = (bf16[2,4,256,256]{3,2,1,0:T(8,128)(2,1)S(1)}, bf16[2,4,256,256]{3,2,1,0:T(8,128)(2,1)}, u32[]{:S(2)}) copy-start(bf16[2,4,256,256]{3,2,1,0:T(8,128)(2,1)} %copy-done.5) | copy-start | bytes 3145732
  133.4 31.5 %all-to-all-start.2 = ((f32[16,2,64,256]{3,2,1,0:T(8,128)}), f32[16,2,64,256]{3,2,1,0:T(8,128)S(1)}, u32[]{:S(2)}, u32[]{:S(2)}) async-start(f32[16,2,64,256]{3,2,1,0:T(8,128)} %bitcast.69), calls=%async_computation.2 | async-start | bytes 4194304 | tf_op jit(solution)/shard_map/all_to_all | solution.py:29
Sparse Core Ops, SparseCore 0:
  10.3 42.2 all-gather.4
  121.9 34.3 all-gather.6

commit v4 on v3

--- a/solution.py
+++ b/solution.py
@@ -41,12 +41,14 @@
     left_local = pair_left % det_local
     left_rows = jnp.take(orbitals, left_local, axis=0)
 
-    marks = jnp.zeros((1, rows * nocc), jnp.bfloat16).at[0, :capacity].set(pair_right.astype(jnp.bfloat16))
-    carried = jnp.concatenate([orbitals, marks.reshape(1, rows, nocc)], axis=0)
+    pad = 16
+    marks = jnp.zeros((pad, nocc), jnp.bfloat16).at[0, :capacity].set(pair_right.astype(jnp.bfloat16))
+    carried = jnp.concatenate([orbitals.reshape(det_local * rows, nocc), marks], axis=0)
     everyone = lax.all_gather(carried, "det", axis=0, tiled=False)
-    right_all = everyone[:, det_local].reshape(n_det, rows * nocc)[:, :capacity].astype(jnp.int32).reshape(-1)
+    right_all = everyone[:, det_local * rows, :capacity].astype(jnp.int32).reshape(-1)
+    fetched = everyone[:, : det_local * rows].reshape(n_det * det_local, rows, nocc)
     left_full = gather_rows(left_rows, n_orb)
-    right_rows = everyone[pair_right // det_local, pair_right % det_local]
+    right_rows = fetched[pair_right]
     right_full = gather_rows(right_rows, n_orb)
 
     left_stack = jnp.transpose(left_full, (1, 0, 2)).reshape(n_orb * rows, capacity * nocc)

time: 176 us -> 174 us (0.989)
  waiting for transfers between devices: 65.5 us -> 62.7 us
    all_to_all x2, waiting for transfers between devices: 25.6 us -> 23.6 us  [gather_rows(): got = lax.all_to_all(spread, 'orb', 0, 0, tiled=True)]
    another operation x2 -> x0, other arithmetic: 1.94 us -> none
  transfers between devices with their start and end apart: 5 -> 5, of which waited for: 4 -> 4; matrix products, arithmetic and copies ran while one was open for 15% -> 17% of each run, Pallas kernels for 0% -> 0%
where the time goes in v4:
time: 174 us; the launch traced here: 173 us
  waiting for transfers between devices  62.7 us (36%)
  blocking collectives  30.6 us (18%)
  matrix products  28.9 us (17%)
  starting transfers between devices  17.6 us (10%)
  between operations  14.3 us (8%)
  local copies, waits for them, and re-layouts  11.1 us (6%)
  other arithmetic  8.01 us (5%)
    all_to_all x1, blocking collectives, scatter_rows(): got = lax.all_to_all(parts, 'orb', 0, 0, tiled=True)  30.6 us
    all_to_all x1, waiting for transfers between devices, scatter_rows(): got = lax.all_to_all(parts, 'orb', 0, 0, tiled=True)  26.6 us
    all_to_all x2, waiting for transfers between devices, gather_rows(): got = lax.all_to_all(spread, 'orb', 0, 0, tiled=True)  23.6 us
    all_to_all x2, starting transfers between devices, gather_rows(): got = lax.all_to_all(spread, 'orb', 0, 0, tiled=True)  13.8 us
    all_gather x1, waiting for transfers between devices, local(): everyone = lax.all_gather(carried, 'det', axis=0, tiled=False)  12.4 us
    dot_general x1, matrix products, local(): jnp.einsum('qst,tk->qsk', dfit, left_stack, preferred_element_type=jnp.fl...  10.2 us
    dot_general x1, matrix products, local(): jnp.einsum('qst,tk->qsk', dfit, moved_stack, preferred_element_type=jnp.f...  8.32 us
    all_to_all x1, starting transfers between devices, scatter_rows(): got = lax.all_to_all(parts, 'orb', 0, 0, tiled=True)  3.72 us
  transfers between devices with their start and end apart: 5, of which 4 were waited for; matrix products, arithmetic and copies ran while one was open for 17% of the time, Pallas kernels for 0%

profile of v4, /device:TPU:32, one launch (start us, length us, event | category | flops | bytes accessed | tf_op | source)
XLA Modules:
  0.0 173.2 jit_solution(12613403297874627149)
XLA Ops:
  6.5 0.7 compare_select_fusion.1
  7.3 1.6 fusion.16
  8.9 0.7 compare_and_fusion
  9.6 1.5 gather_fusion.1
  11.0 0.1 broadcast_select_fusion
  11.1 1.1 broadcast_in_dim.86
  12.2 7.0 %all-to-all-start.1 = ((bf16[16,2,64,256]{3,2,1,0:T(8,128)(2,1)}), bf16[16,2,64,256]{3,2,1,0:T(8,128)(2,1)S(1)}, u32[]{:S(2)}, u32[]{:S(2)}) async-start(bf16[16,2,64,256]{3,2,1,0:T(8,128)(2,1)} %broadcast_in_dim.86), calls=%async_computation.1 | async-start | bytes 2097152 | tf_op jit(solution)/shard_map/all_to_all | solution.py:21
  19.9 0.7 fusion.17
  20.6 0.7 convert_multiply_fusion
  21.3 15.7 %all-to-all-done.1 = bf16[16,2,64,256]{3,2,1,0:T(8,128)(2,1)S(1)} async-done(((bf16[16,2,64,256]{3,2,1,0:T(8,128)(2,1)}), bf16[16,2,64,256]{3,2,1,0:T(8,128)(2,1)S(1)}, u32[]{:S(2)}, u32[]{:S(2)}) %all-to-all-start.1) | async-done | bytes 1048608 | tf_op jit(solution)/shard_map/all_to_all | solution.py:21
  37.0 0.1 copy.55
  37.1 1.3 copy.58
  38.4 12.4 %all-gather.5.cloned.1.call-done = bf16[4352,256]{1,0:T(8,128)(2,1)} async-done(((bf16[272,256]{1,0:T(8,128)(2,1)}), bf16[4352,256]{1,0:T(8,128)(2,1)}) %all-gather.5.cloned.1.call-update) | async-done | bytes 2228240 | tf_op jit(solution)/shard_map/all_gather | solution.py:47
  50.8 1.7 slice.28
  52.6 0.6 gather_fusion
  53.1 1.1 broadcast_in_dim.82
  54.3 6.8 %all-to-all-start = ((bf16[16,2,64,256]{3,2,1,0:T(8,128)(2,1)}), bf16[16,2,64,256]{3,2,1,0:T(8,128)(2,1)S(1)}, u32[]{:S(2)}, u32[]{:S(2)}) async-start(bf16[16,2,64,256]{3,2,1,0:T(8,128)(2,1)} %broadcast_in_dim.82), calls=%async_computation | async-start | bytes 2097152 | tf_op jit(solution)/shard_map/all_to_all | solution.py:21
  61.1 0.0 all-gather.7.cloned.1.call-start
  61.1 10.2 %convolution_convert_fusion = bf16[512,4,1024]{2,0,1:T(8,128)(2,1)} fusion(bf16[1024,512,1]{0,1,2:T(8,128)(2,1)} %bitcast.81, bf16[4,1024,1024]{2,1,0:T(8,128)(2,1)} %param.10), kind=kOutput, calls=%fused_computation.5 | convolution fusion | flops 4297064448 | bytes 13631488 | tf_op jit(solution)/shard_map/qst,tk->qsk/dot_general | solution.py:55
  71.3 7.9 %all-to-all-done = bf16[16,2,64,256]{3,2,1,0:T(8,128)(2,1)S(1)} async-done(((bf16[16,2,64,256]{3,2,1,0:T(8,128)(2,1)}), bf16[16,2,64,256]{3,2,1,0:T(8,128)(2,1)S(1)}, u32[]{:S(2)}, u32[]{:S(2)}) %all-to-all-start) | async-done | bytes 1048608 | tf_op jit(solution)/shard_map/all_to_all | solution.py:21
  79.3 0.1 copy.54
  79.4 0.5 fusion.19
  79.9 0.7 convolution_subtract_fusion.1
  80.6 0.7 fusion.9
  81.3 0.7 convolution_subtract_fusion
  81.9 0.7 fusion.20
  82.6 1.0 convolution_convert_fusion.2
  83.7 1.0 copy-done
  84.7 1.3 multiply_convert_fusion
  86.0 1.8 %fusion.5 = f32[2,1024,256,1]{2,1,0,3:T(8,128)S(1)} fusion(bf16[4,1024,2,256]{1,3,2,0:T(8,128)(2,1)S(1)} %bitcast.84, bf16[2,4,256,256]{3,2,1,0:T(8,128)(2,1)S(1)} %multiply_convert_fusion), kind=kOutput, calls=%fused_computation.14 | convolution fusion | flops 1073741824 | bytes 7340032 | tf_op jit(solution)/shard_map/qsbc,bqcd->bsd/dot_general | solution.py:72
  87.8 0.2 copy.87
  87.9 30.6 %all_to_all.20 = f32[16,2,64,256]{3,2,1,0:T(8,128)S(1)} all-to-all(f32[16,2,64,256]{3,2,1,0:T(8,128)S(1)} %bitcast.72), channel_id=1, replica_groups=mesh['det'=16,'orb'=16] {'orb'}, dimensions={0} | all-to-all | bytes 4194304 | tf_op jit(solution)/shard_map/all_to_all | solution.py:29
  118.6 0.1 reduce_sum.38
  118.7 1.3 fusion.21
  120.0 8.3 %convolution_convert_fusion.1 = bf16[512,4,1024]{2,0,1:T(8,128)(2,1)S(1)} fusion(bf16[1024,512,1]{0,1,2:T(8,128)(2,1)} %bitcast.80, bf16[4,1024,1024]{2,1,0:T(8,128)(2,1)} %param.10), kind=kOutput, calls=%fused_computation.6 | convolution fusion | flops 4297064448 | bytes 13631488 | tf_op jit(solution)/shard_map/qst,tk->qsk/dot_general | solution.py:65
  128.3 1.8 %fusion.7 = f32[2,1024,256,1]{2,1,0,3:T(8,128)S(1)} fusion(bf16[4,1024,2,256]{1,3,2,0:T(8,128)(2,1)S(1)} %bitcast.85, bf16[2,4,256,256]{3,2,1,0:T(8,128)(2,1)S(1)} %copy-done.3), kind=kOutput, calls=%fused_computation.16 | convolution fusion | flops 1073741824 | bytes 7340032 | tf_op jit(solution)/shard_map/qsbc,bqdc->bsd/dot_general | solution.py:78
  130.1 1.5 copy.88
  131.6 3.7 %all-to-all-start.2 = ((f32[16,2,64,256]{3,2,1,0:T(8,128)}), f32[16,2,64,256]{3,2,1,0:T(8,128)S(1)}, u32[]{:S(2)}, u32[]{:S(2)}) async-start(f32[16,2,64,256]{3,2,1,0:T(8,128)} %bitcast.71), calls=%async_computation.2 | async-start | bytes 4194304 | tf_op jit(solution)/shard_map/all_to_all | solution.py:29
  135.3 0.1 iota_compare_fusion.2
  135.4 0.8 slice.29
  136.2 0.1 copy.76
  136.3 0.1 copy.65
  136.4 0.1 broadcast_compare_fusion
  136.5 26.6 %all-to-all-done.2 = f32[16,2,64,256]{3,2,1,0:T(8,128)S(1)} async-done(((f32[16,2,64,256]{3,2,1,0:T(8,128)}), f32[16,2,64,256]{3,2,1,0:T(8,128)S(1)}, u32[]{:S(2)}, u32[]{:S(2)}) %all-to-all-start.2) | async-done | bytes 2097184 | tf_op jit(solution)/shard_map/all_to_all | solution.py:29
  163.1 0.1 reduce_sum.36
  163.2 0.1 select_reduce_fusion.1
  163.4 2.2 %select_reduce_fusion = f32[4,64,256]{2,1,0:T(8,128)S(1)} fusion(f32[16,2,64,256]{3,2,1,0:T(8,128)} %bitcast.75, pred[16,2,4]{2,1,0:T(4,128)(4,1)S(1)} %broadcast_compare_fusion), kind=kLoop, calls=%fused_computation.2 | loop fusion | flops 4128768 | bytes 2359424 | tf_op jit(solution)/shard_map/reduce_sum | solution.py:85
  165.6 0.7 add.35
  (17 shorter events, 0.1 us)
Async XLA Ops:
  6.5 44.3 %all-gather.5.cloned.1.call-start = ((), (), s32[]{:S(2)}) async-start(), calls=%async_computation.4 | async-start | bytes 2367488 | tf_op jit(solution)/shard_map/all_gather | solution.py:47
  12.2 24.8 %all-to-all-start.1 = ((bf16[16,2,64,256]{3,2,1,0:T(8,128)(2,1)}), bf16[16,2,64,256]{3,2,1,0:T(8,128)(2,1)S(1)}, u32[]{:S(2)}, u32[]{:S(2)}) async-start(bf16[16,2,64,256]{3,2,1,0:T(8,128)(2,1)} %broadcast_in_dim.86), calls=%async_computation.1 | async-start | bytes 2097152 | tf_op jit(solution)/shard_map/all_to_all | solution.py:21
  54.3 25.0 %all-to-all-start = ((bf16[16,2,64,256]{3,2,1,0:T(8,128)(2,1)}), bf16[16,2,64,256]{3,2,1,0:T(8,128)(2,1)S(1)}, u32[]{:S(2)}, u32[]{:S(2)}) async-start(bf16[16,2,64,256]{3,2,1,0:T(8,128)(2,1)} %broadcast_in_dim.82), calls=%async_computation | async-start | bytes 2097152 | tf_op jit(solution)/shard_map/all_to_all | solution.py:21
  61.1 102.3 %all-gather.7.cloned.1.call-start = ((), (), s32[]{:S(2)}) async-start(), calls=%async_computation.5 | async-start | bytes 2228224 | tf_op jit(solution)/shard_map/all_gather | solution.py:76
  80.6 4.1 %copy-start.1 = (bf16[512,4,1024]{2,0,1:T(8,128)(2,1)S(1)}, bf16[512,4,1024]{2,0,1:T(8,128)(2,1)}, u32[]{:S(2)}) copy-start(bf16[512,4,1024]{2,0,1:T(8,128)(2,1)} %convolution_convert_fusion) | copy-start | bytes 12582916
  83.7 1.0 copy-start
  86.0 2.0 %copy-start.2 = (bf16[2,4,256,256]{3,2,1,0:T(8,128)(2,1)}, bf16[2,4,256,256]{3,2,1,0:T(8,128)(2,1)S(1)}, u32[]{:S(2)}) copy-start(bf16[2,4,256,256]{3,2,1,0:T(8,128)(2,1)S(1)} %multiply_convert_fusion) | copy-start | bytes 3145732
  120.0 8.3 %copy-start.3 = (bf16[2,4,256,256]{3,2,1,0:T(8,128)(2,1)S(1)}, bf16[2,4,256,256]{3,2,1,0:T(8,128)(2,1)}, u32[]{:S(2)}) copy-start(bf16[2,4,256,256]{3,2,1,0:T(8,128)(2,1)} %copy-done.2) | copy-start | bytes 3145732
  131.6 31.5 %all-to-all-start.2 = ((f32[16,2,64,256]{3,2,1,0:T(8,128)}), f32[16,2,64,256]{3,2,1,0:T(8,128)S(1)}, u32[]{:S(2)}, u32[]{:S(2)}) async-start(f32[16,2,64,256]{3,2,1,0:T(8,128)} %bitcast.71), calls=%async_computation.2 | async-start | bytes 4194304 | tf_op jit(solution)/shard_map/all_to_all | solution.py:29
Sparse Core Ops, SparseCore 0:
  9.2 41.6 all-gather.4
  120.1 34.4 all-gather.6

commit v5 on v4

--- a/solution.py
+++ b/solution.py
@@ -71,12 +71,13 @@
     scaled = (factor * exchange).astype(jnp.bfloat16)
     moved_term = jnp.einsum("qsbc,bqcd->bsd", projected_t, scaled, preferred_element_type=jnp.float32)
     moved_grad = scatter_rows(moved_term, n_orb)
-    right_grad = jnp.einsum("brc,bdc->brd", moved_grad, inverse, precision=HI)
+    live = (weights != 0.0)[:, None, None]
+    right_grad = jnp.where(live, jnp.einsum("brc,bdc->brd", moved_grad, inverse, precision=HI), 0.0)
 
     came = lax.all_gather(right_grad, "det", axis=0, tiled=False)
 
     left_term = jnp.einsum("qsbc,bqdc->bsd", applied, scaled, preferred_element_type=jnp.float32)
-    left_grad = scatter_rows(left_term, n_orb)
+    left_grad = jnp.where(live, scatter_rows(left_term, n_orb), 0.0)
     own = left_local[:, None] == jnp.arange(det_local, dtype=jnp.int32)[None, :]
     own_sum = jnp.sum(jnp.where(own[:, :, None, None], left_grad[:, None], 0.0), axis=0)
 

time: 174 us -> 177 us (1.017)
  blocking collectives: 30.6 us -> 0 us
  waiting for transfers between devices: 62.7 us -> 90.9 us
  starting transfers between devices: 17.6 us -> 21.5 us
    all_to_all x1 -> x0, blocking collectives: 30.6 us -> none  [scatter_rows(): got = lax.all_to_all(parts, 'orb', 0, 0, tiled=True)]
    all_to_all x1 -> x2, waiting for transfers between devices: 26.6 us -> 54.8 us  [scatter_rows(): got = lax.all_to_all(parts, 'orb', 0, 0, tiled=True)]
    all_to_all x1 -> x2, starting transfers between devices: 3.72 us -> 7.45 us  [scatter_rows(): got = lax.all_to_all(parts, 'orb', 0, 0, tiled=True)]
  transfers between devices with their start and end apart: 5 -> 6, of which waited for: 4 -> 5; matrix products, arithmetic and copies ran while one was open for 17% -> 17% of each run, Pallas kernels for 0% -> 0%
where the time goes in v5:
time: 177 us; the launch traced here: 176 us
  waiting for transfers between devices  90.9 us (51%)
  matrix products  28.9 us (16%)
  starting transfers between devices  21.5 us (12%)
  between operations  14.3 us (8%)
  local copies, waits for them, and re-layouts  12.4 us (7%)
  other arithmetic  8.1 us (5%)
    all_to_all x2, waiting for transfers between devices, scatter_rows(): got = lax.all_to_all(parts, 'orb', 0, 0, tiled=True)  54.8 us
    all_to_all x2, waiting for transfers between devices, gather_rows(): got = lax.all_to_all(spread, 'orb', 0, 0, tiled=True)  23.6 us
    all_to_all x2, starting transfers between devices, gather_rows(): got = lax.all_to_all(spread, 'orb', 0, 0, tiled=True)  13.8 us
    all_gather x1, waiting for transfers between devices, local(): everyone = lax.all_gather(carried, 'det', axis=0, tiled=False)  12.4 us
    dot_general x1, matrix products, local(): jnp.einsum('qst,tk->qsk', dfit, left_stack, preferred_element_type=jnp.fl...  10.2 us
    dot_general x1, matrix products, local(): jnp.einsum('qst,tk->qsk', dfit, moved_stack, preferred_element_type=jnp.f...  8.32 us
    all_to_all x2, starting transfers between devices, scatter_rows(): got = lax.all_to_all(parts, 'orb', 0, 0, tiled=True)  7.45 us
  transfers between devices with their start and end apart: 6, of which 5 were waited for; matrix products, arithmetic and copies ran while one was open for 17% of the time, Pallas kernels for 0%

profile of v5, /device:TPU:32, one launch (start us, length us, event | category | flops | bytes accessed | tf_op | source)
XLA Modules:
  0.0 176.1 jit_solution(9813548415853753420)
XLA Ops:
  6.5 0.7 compare_select_fusion.1
  7.3 1.6 fusion.16
  8.9 0.7 compare_and_fusion
  9.6 1.5 gather_fusion.1
  11.1 1.1 broadcast_in_dim.104
  12.2 7.0 %all-to-all-start.1 = ((bf16[16,2,64,256]{3,2,1,0:T(8,128)(2,1)}), bf16[16,2,64,256]{3,2,1,0:T(8,128)(2,1)S(1)}, u32[]{:S(2)}, u32[]{:S(2)}) async-start(bf16[16,2,64,256]{3,2,1,0:T(8,128)(2,1)} %broadcast_in_dim.104), calls=%async_computation.1 | async-start | bytes 2097152 | tf_op jit(solution)/shard_map/all_to_all | solution.py:21
  19.9 0.7 broadcast_multiply_fusion
  20.6 0.7 convert_multiply_fusion
  21.3 15.7 %all-to-all-done.1 = bf16[16,2,64,256]{3,2,1,0:T(8,128)(2,1)S(1)} async-done(((bf16[16,2,64,256]{3,2,1,0:T(8,128)(2,1)}), bf16[16,2,64,256]{3,2,1,0:T(8,128)(2,1)S(1)}, u32[]{:S(2)}, u32[]{:S(2)}) %all-to-all-start.1) | async-done | bytes 1048608 | tf_op jit(solution)/shard_map/all_to_all | solution.py:21
  37.0 0.1 copy.55
  37.1 1.4 copy.58
  38.5 12.4 %all-gather.5.cloned.1.call-done = bf16[4352,256]{1,0:T(8,128)(2,1)} async-done(((bf16[272,256]{1,0:T(8,128)(2,1)}), bf16[4352,256]{1,0:T(8,128)(2,1)}) %all-gather.5.cloned.1.call-update) | async-done | bytes 2228240 | tf_op jit(solution)/shard_map/all_gather | solution.py:47
  50.8 1.7 slice.28
  52.6 0.6 gather_fusion
  53.1 1.1 broadcast_in_dim.100
  54.2 6.8 %all-to-all-start = ((bf16[16,2,64,256]{3,2,1,0:T(8,128)(2,1)}), bf16[16,2,64,256]{3,2,1,0:T(8,128)(2,1)S(1)}, u32[]{:S(2)}, u32[]{:S(2)}) async-start(bf16[16,2,64,256]{3,2,1,0:T(8,128)(2,1)} %broadcast_in_dim.100), calls=%async_computation | async-start | bytes 2097152 | tf_op jit(solution)/shard_map/all_to_all | solution.py:21
  61.1 10.2 %convolution_convert_fusion = bf16[512,4,1024]{2,0,1:T(8,128)(2,1)} fusion(bf16[1024,512,1]{0,1,2:T(8,128)(2,1)} %bitcast.82, bf16[4,1024,1024]{2,1,0:T(8,128)(2,1)} %param.10), kind=kOutput, calls=%fused_computation.5 | convolution fusion | flops 4297064448 | bytes 13631488 | tf_op jit(solution)/shard_map/qst,tk->qsk/dot_general | solution.py:55
  71.3 8.0 %all-to-all-done = bf16[16,2,64,256]{3,2,1,0:T(8,128)(2,1)S(1)} async-done(((bf16[16,2,64,256]{3,2,1,0:T(8,128)(2,1)}), bf16[16,2,64,256]{3,2,1,0:T(8,128)(2,1)S(1)}, u32[]{:S(2)}, u32[]{:S(2)}) %all-to-all-start) | async-done | bytes 1048608 | tf_op jit(solution)/shard_map/all_to_all | solution.py:21
  79.3 0.1 copy.54
  79.4 0.5 fusion.18
  79.9 0.7 convolution_subtract_fusion.1
  80.6 0.7 fusion.9
  81.3 0.7 convolution_subtract_fusion
  81.9 0.7 fusion.19
  82.6 1.0 convolution_convert_fusion.2
  83.7 1.0 copy-done
  84.6 1.3 multiply_convert_fusion
  85.9 1.8 %fusion.5 = f32[2,1024,256,1]{2,1,0,3:T(8,128)S(1)} fusion(bf16[4,1024,2,256]{1,3,2,0:T(8,128)(2,1)S(1)} %bitcast.85, bf16[2,4,256,256]{3,2,1,0:T(8,128)(2,1)S(1)} %multiply_convert_fusion), kind=kOutput, calls=%fused_computation.15 | convolution fusion | flops 1073741824 | bytes 7340032 | tf_op jit(solution)/shard_map/qsbc,bqcd->bsd/dot_general | solution.py:72
  87.7 1.5 copy.87
  89.2 3.7 %all-to-all-start.3 = ((f32[16,2,64,256]{3,2,1,0:T(8,128)}), f32[16,2,64,256]{3,2,1,0:T(8,128)S(1)}, u32[]{:S(2)}, u32[]{:S(2)}) async-start(f32[16,2,64,256]{3,2,1,0:T(8,128)} %bitcast.73), calls=%async_computation.3 | async-start | bytes 4194304 | tf_op jit(solution)/shard_map/all_to_all | solution.py:29
  93.0 0.2 all-gather.7.cloned.1.call-start
  93.2 28.3 %all-to-all-done.3 = f32[16,2,64,256]{3,2,1,0:T(8,128)S(1)} async-done(((f32[16,2,64,256]{3,2,1,0:T(8,128)}), f32[16,2,64,256]{3,2,1,0:T(8,128)S(1)}, u32[]{:S(2)}, u32[]{:S(2)}) %all-to-all-start.3) | async-done | bytes 2097184 | tf_op jit(solution)/shard_map/all_to_all | solution.py:29
  121.5 0.1 reduce_sum.38
  121.6 1.3 convolution_select_fusion
  122.9 8.3 %convolution_convert_fusion.1 = bf16[512,4,1024]{2,0,1:T(8,128)(2,1)S(1)} fusion(bf16[1024,512,1]{0,1,2:T(8,128)(2,1)} %bitcast.81, bf16[4,1024,1024]{2,1,0:T(8,128)(2,1)} %param.10), kind=kOutput, calls=%fused_computation.6 | convolution fusion | flops 4297064448 | bytes 13631488 | tf_op jit(solution)/shard_map/qst,tk->qsk/dot_general | solution.py:65
  131.2 1.8 %fusion.7 = f32[2,1024,256,1]{2,1,0,3:T(8,128)S(1)} fusion(bf16[4,1024,2,256]{1,3,2,0:T(8,128)(2,1)S(1)} %bitcast.86, bf16[2,4,256,256]{3,2,1,0:T(8,128)(2,1)S(1)} %copy-done.4), kind=kOutput, calls=%fused_computation.17 | convolution fusion | flops 1073741824 | bytes 7340032 | tf_op jit(solution)/shard_map/qsbc,bqdc->bsd/dot_general | solution.py:79
  133.0 1.5 copy.88
  134.5 3.7 %all-to-all-start.2 = ((f32[16,2,64,256]{3,2,1,0:T(8,128)}), f32[16,2,64,256]{3,2,1,0:T(8,128)S(1)}, u32[]{:S(2)}, u32[]{:S(2)}) async-start(f32[16,2,64,256]{3,2,1,0:T(8,128)} %bitcast.72), calls=%async_computation.2 | async-start | bytes 4194304 | tf_op jit(solution)/shard_map/all_to_all | solution.py:29
  138.3 0.8 slice.29
  139.1 0.1 copy.76
  139.2 0.1 copy.65
  139.3 0.1 broadcast_compare_fusion
  139.4 26.6 %all-to-all-done.2 = f32[16,2,64,256]{3,2,1,0:T(8,128)S(1)} async-done(((f32[16,2,64,256]{3,2,1,0:T(8,128)}), f32[16,2,64,256]{3,2,1,0:T(8,128)S(1)}, u32[]{:S(2)}, u32[]{:S(2)}) %all-to-all-start.2) | async-done | bytes 2097184 | tf_op jit(solution)/shard_map/all_to_all | solution.py:29
  165.9 0.1 reduce_sum.36
  166.1 0.1 broadcast_select_fusion
  166.2 0.1 select_reduce_fusion.1
  166.3 2.2 %select_reduce_fusion = f32[4,64,256]{2,1,0:T(8,128)S(1)} fusion(f32[16,2,64,256]{3,2,1,0:T(8,128)} %bitcast.76, pred[16,2,4]{2,1,0:T(4,128)(4,1)S(1)} %broadcast_compare_fusion), kind=kLoop, calls=%fused_computation.2 | loop fusion | flops 4128768 | bytes 2359424 | tf_op jit(solution)/shard_map/reduce_sum | solution.py:86
  168.5 0.7 add.35
  (22 shorter events, 0.3 us)
Async XLA Ops:
  6.5 44.3 %all-gather.5.cloned.1.call-start = ((), (), s32[]{:S(2)}) async-start(), calls=%async_computation.4 | async-start | bytes 2367488 | tf_op jit(solution)/shard_map/all_gather | solution.py:47
  12.2 24.8 %all-to-all-start.1 = ((bf16[16,2,64,256]{3,2,1,0:T(8,128)(2,1)}), bf16[16,2,64,256]{3,2,1,0:T(8,128)(2,1)S(1)}, u32[]{:S(2)}, u32[]{:S(2)}) async-start(bf16[16,2,64,256]{3,2,1,0:T(8,128)(2,1)} %broadcast_in_dim.104), calls=%async_computation.1 | async-start | bytes 2097152 | tf_op jit(solution)/shard_map/all_to_all | solution.py:21
  54.2 25.0 %all-to-all-start = ((bf16[16,2,64,256]{3,2,1,0:T(8,128)(2,1)}), bf16[16,2,64,256]{3,2,1,0:T(8,128)(2,1)S(1)}, u32[]{:S(2)}, u32[]{:S(2)}) async-start(bf16[16,2,64,256]{3,2,1,0:T(8,128)(2,1)} %broadcast_in_dim.100), calls=%async_computation | async-start | bytes 2097152 | tf_op jit(solution)/shard_map/all_to_all | solution.py:21
  80.6 4.1 %copy-start.2 = (bf16[512,4,1024]{2,0,1:T(8,128)(2,1)S(1)}, bf16[512,4,1024]{2,0,1:T(8,128)(2,1)}, u32[]{:S(2)}) copy-start(bf16[512,4,1024]{2,0,1:T(8,128)(2,1)} %convolution_convert_fusion) | copy-start | bytes 12582916
  83.6 1.0 copy-start
  85.9 3.3 %copy-start.3 = (bf16[2,4,256,256]{3,2,1,0:T(8,128)(2,1)}, bf16[2,4,256,256]{3,2,1,0:T(8,128)(2,1)S(1)}, u32[]{:S(2)}) copy-start(bf16[2,4,256,256]{3,2,1,0:T(8,128)(2,1)S(1)} %multiply_convert_fusion) | copy-start | bytes 3145732
  87.7 5.5 %copy-start.1 = (f32[2]{0:T(128)S(1)}, f32[2]{0:T(128)}, u32[]{:S(2)}) copy-start(f32[2]{0:T(128)} %param.14) | copy-start | bytes 28
  89.2 32.2 %all-to-all-start.3 = ((f32[16,2,64,256]{3,2,1,0:T(8,128)}), f32[16,2,64,256]{3,2,1,0:T(8,128)S(1)}, u32[]{:S(2)}, u32[]{:S(2)}) async-start(f32[16,2,64,256]{3,2,1,0:T(8,128)} %bitcast.73), calls=%async_computation.3 | async-start | bytes 4194304 | tf_op jit(solution)/shard_map/all_to_all | solution.py:29
  93.0 73.3 %all-gather.7.cloned.1.call-start = ((), (), s32[]{:S(2)}) async-start(), calls=%async_computation.5 | async-start | bytes 2228224 | tf_op jit(solution)/shard_map/all_gather | solution.py:77
  122.9 8.3 %copy-start.4 = (bf16[2,4,256,256]{3,2,1,0:T(8,128)(2,1)S(1)}, bf16[2,4,256,256]{3,2,1,0:T(8,128)(2,1)}, u32[]{:S(2)}) copy-start(bf16[2,4,256,256]{3,2,1,0:T(8,128)(2,1)} %copy-done.3) | copy-start | bytes 3145732
  134.5 31.4 %all-to-all-start.2 = ((f32[16,2,64,256]{3,2,1,0:T(8,128)}), f32[16,2,64,256]{3,2,1,0:T(8,128)S(1)}, u32[]{:S(2)}, u32[]{:S(2)}) async-start(f32[16,2,64,256]{3,2,1,0:T(8,128)} %bitcast.72), calls=%async_computation.2 | async-start | bytes 4194304 | tf_op jit(solution)/shard_map/all_to_all | solution.py:29
Sparse Core Ops, SparseCore 0:
  9.2 41.6 all-gather.4
  123.0 34.7 all-gather.6

commit v6 on v5

--- a/solution.py
+++ b/solution.py
@@ -10,7 +10,7 @@
 def newton(correlation):
     eye = jnp.eye(correlation.shape[-1], dtype=jnp.float32)
     inverse = 2.0 * eye - correlation
-    for sweep in range(NS - 1):
+    for _ in range(NS - 1):
         product = jnp.einsum("bij,bjk->bik", correlation, inverse, precision=HI)
         inverse = jnp.einsum("bij,bjk->bik", inverse, 2.0 * eye - product, precision=HI)
     return inverse
@@ -30,7 +30,7 @@
     return jnp.sum(got, axis=0)
 
 
-def local(orbitals, dfit, pair_left, pair_right, pair_count, pair_weight, aux_screen):
+def local_body(orbitals, dfit, pair_left, pair_right, pair_count, pair_weight, aux_screen):
     det_local, rows, nocc = orbitals.shape
     capacity = pair_left.shape[0]
     n_det = lax.axis_size("det")
@@ -98,4 +98,4 @@
         P("det", "orb"),
     )
     out_specs = P("det", "orb", None)
-    return jax.shard_map(local, mesh=mesh, in_specs=in_specs, out_specs=out_specs, check_vma=False)
+    return jax.shard_map(local_body, mesh=mesh, in_specs=in_specs, out_specs=out_specs, check_vma=False)

time: 177 us -> 177 us (level)
  no operation moved by 1% of the time
where the time goes in v6:
time: 177 us; the launch traced here: 176 us
  waiting for transfers between devices  90.9 us (51%)
  matrix products  28.9 us (16%)
  starting transfers between devices  21.5 us (12%)
  between operations  14.3 us (8%)
  local copies, waits for them, and re-layouts  12.4 us (7%)
  other arithmetic  8.1 us (5%)
    all_to_all x2, waiting for transfers between devices, scatter_rows(): got = lax.all_to_all(parts, 'orb', 0, 0, tiled=True)  54.8 us
    all_to_all x2, waiting for transfers between devices, gather_rows(): got = lax.all_to_all(spread, 'orb', 0, 0, tiled=True)  23.6 us
    all_to_all x2, starting transfers between devices, gather_rows(): got = lax.all_to_all(spread, 'orb', 0, 0, tiled=True)  13.8 us
    all_gather x1, waiting for transfers between devices, local_body(): everyone = lax.all_gather(carried, 'det', axis=0, tiled=False)  12.4 us
    dot_general x1, matrix products, local_body(): jnp.einsum('qst,tk->qsk', dfit, left_stack, preferred_element_type=jnp.fl...  10.2 us
    dot_general x1, matrix products, local_body(): jnp.einsum('qst,tk->qsk', dfit, moved_stack, preferred_element_type=jnp.f...  8.32 us
    all_to_all x2, starting transfers between devices, scatter_rows(): got = lax.all_to_all(parts, 'orb', 0, 0, tiled=True)  7.45 us
  transfers between devices with their start and end apart: 6, of which 5 were waited for; matrix products, arithmetic and copies ran while one was open for 17% of the time, Pallas kernels for 0%

profile of v6, /device:TPU:32, one launch (start us, length us, event | category | flops | bytes accessed | tf_op | source)
XLA Modules:
  0.0 176.1 jit_solution(9813548415853753420)
XLA Ops:
  6.5 0.7 compare_select_fusion.1
  7.3 1.6 fusion.16
  8.9 0.7 compare_and_fusion
  9.6 1.5 gather_fusion.1
  11.1 1.1 broadcast_in_dim.104
  12.2 7.0 %all-to-all-start.1 = ((bf16[16,2,64,256]{3,2,1,0:T(8,128)(2,1)}), bf16[16,2,64,256]{3,2,1,0:T(8,128)(2,1)S(1)}, u32[]{:S(2)}, u32[]{:S(2)}) async-start(bf16[16,2,64,256]{3,2,1,0:T(8,128)(2,1)} %broadcast_in_dim.104), calls=%async_computation.1 | async-start | bytes 2097152 | tf_op jit(solution)/shard_map/all_to_all | solution.py:21
  19.9 0.7 broadcast_multiply_fusion
  20.6 0.7 convert_multiply_fusion
  21.3 15.7 %all-to-all-done.1 = bf16[16,2,64,256]{3,2,1,0:T(8,128)(2,1)S(1)} async-done(((bf16[16,2,64,256]{3,2,1,0:T(8,128)(2,1)}), bf16[16,2,64,256]{3,2,1,0:T(8,128)(2,1)S(1)}, u32[]{:S(2)}, u32[]{:S(2)}) %all-to-all-start.1) | async-done | bytes 1048608 | tf_op jit(solution)/shard_map/all_to_all | solution.py:21
  37.0 0.1 copy.55
  37.1 1.4 copy.58
  38.5 12.4 %all-gather.5.cloned.1.call-done = bf16[4352,256]{1,0:T(8,128)(2,1)} async-done(((bf16[272,256]{1,0:T(8,128)(2,1)}), bf16[4352,256]{1,0:T(8,128)(2,1)}) %all-gather.5.cloned.1.call-update) | async-done | bytes 2228240 | tf_op jit(solution)/shard_map/all_gather | solution.py:47
  50.8 1.7 slice.28
  52.6 0.6 gather_fusion
  53.1 1.1 broadcast_in_dim.100
  54.2 6.8 %all-to-all-start = ((bf16[16,2,64,256]{3,2,1,0:T(8,128)(2,1)}), bf16[16,2,64,256]{3,2,1,0:T(8,128)(2,1)S(1)}, u32[]{:S(2)}, u32[]{:S(2)}) async-start(bf16[16,2,64,256]{3,2,1,0:T(8,128)(2,1)} %broadcast_in_dim.100), calls=%async_computation | async-start | bytes 2097152 | tf_op jit(solution)/shard_map/all_to_all | solution.py:21
  61.1 10.2 %convolution_convert_fusion = bf16[512,4,1024]{2,0,1:T(8,128)(2,1)} fusion(bf16[1024,512,1]{0,1,2:T(8,128)(2,1)} %bitcast.82, bf16[4,1024,1024]{2,1,0:T(8,128)(2,1)} %param.10), kind=kOutput, calls=%fused_computation.5 | convolution fusion | flops 4297064448 | bytes 13631488 | tf_op jit(solution)/shard_map/qst,tk->qsk/dot_general | solution.py:55
  71.3 8.0 %all-to-all-done = bf16[16,2,64,256]{3,2,1,0:T(8,128)(2,1)S(1)} async-done(((bf16[16,2,64,256]{3,2,1,0:T(8,128)(2,1)}), bf16[16,2,64,256]{3,2,1,0:T(8,128)(2,1)S(1)}, u32[]{:S(2)}, u32[]{:S(2)}) %all-to-all-start) | async-done | bytes 1048608 | tf_op jit(solution)/shard_map/all_to_all | solution.py:21
  79.3 0.1 copy.54
  79.4 0.5 fusion.18
  79.9 0.7 convolution_subtract_fusion.1
  80.6 0.7 fusion.9
  81.3 0.7 convolution_subtract_fusion
  81.9 0.7 fusion.19
  82.6 1.0 convolution_convert_fusion.2
  83.7 1.0 copy-done
  84.6 1.3 multiply_convert_fusion
  85.9 1.8 %fusion.5 = f32[2,1024,256,1]{2,1,0,3:T(8,128)S(1)} fusion(bf16[4,1024,2,256]{1,3,2,0:T(8,128)(2,1)S(1)} %bitcast.85, bf16[2,4,256,256]{3,2,1,0:T(8,128)(2,1)S(1)} %multiply_convert_fusion), kind=kOutput, calls=%fused_computation.15 | convolution fusion | flops 1073741824 | bytes 7340032 | tf_op jit(solution)/shard_map/qsbc,bqcd->bsd/dot_general | solution.py:72
  87.7 1.5 copy.87
  89.2 3.7 %all-to-all-start.3 = ((f32[16,2,64,256]{3,2,1,0:T(8,128)}), f32[16,2,64,256]{3,2,1,0:T(8,128)S(1)}, u32[]{:S(2)}, u32[]{:S(2)}) async-start(f32[16,2,64,256]{3,2,1,0:T(8,128)} %bitcast.73), calls=%async_computation.3 | async-start | bytes 4194304 | tf_op jit(solution)/shard_map/all_to_all | solution.py:29
  93.0 0.2 all-gather.7.cloned.1.call-start
  93.2 28.3 %all-to-all-done.3 = f32[16,2,64,256]{3,2,1,0:T(8,128)S(1)} async-done(((f32[16,2,64,256]{3,2,1,0:T(8,128)}), f32[16,2,64,256]{3,2,1,0:T(8,128)S(1)}, u32[]{:S(2)}, u32[]{:S(2)}) %all-to-all-start.3) | async-done | bytes 2097184 | tf_op jit(solution)/shard_map/all_to_all | solution.py:29
  121.5 0.1 reduce_sum.38
  121.6 1.3 convolution_select_fusion
  122.9 8.3 %convolution_convert_fusion.1 = bf16[512,4,1024]{2,0,1:T(8,128)(2,1)S(1)} fusion(bf16[1024,512,1]{0,1,2:T(8,128)(2,1)} %bitcast.81, bf16[4,1024,1024]{2,1,0:T(8,128)(2,1)} %param.10), kind=kOutput, calls=%fused_computation.6 | convolution fusion | flops 4297064448 | bytes 13631488 | tf_op jit(solution)/shard_map/qst,tk->qsk/dot_general | solution.py:65
  131.2 1.8 %fusion.7 = f32[2,1024,256,1]{2,1,0,3:T(8,128)S(1)} fusion(bf16[4,1024,2,256]{1,3,2,0:T(8,128)(2,1)S(1)} %bitcast.86, bf16[2,4,256,256]{3,2,1,0:T(8,128)(2,1)S(1)} %copy-done.4), kind=kOutput, calls=%fused_computation.17 | convolution fusion | flops 1073741824 | bytes 7340032 | tf_op jit(solution)/shard_map/qsbc,bqdc->bsd/dot_general | solution.py:79
  133.0 1.5 copy.88
  134.5 3.7 %all-to-all-start.2 = ((f32[16,2,64,256]{3,2,1,0:T(8,128)}), f32[16,2,64,256]{3,2,1,0:T(8,128)S(1)}, u32[]{:S(2)}, u32[]{:S(2)}) async-start(f32[16,2,64,256]{3,2,1,0:T(8,128)} %bitcast.72), calls=%async_computation.2 | async-start | bytes 4194304 | tf_op jit(solution)/shard_map/all_to_all | solution.py:29
  138.3 0.8 slice.29
  139.1 0.1 copy.76
  139.2 0.1 copy.65
  139.3 0.1 broadcast_compare_fusion
  139.4 26.6 %all-to-all-done.2 = f32[16,2,64,256]{3,2,1,0:T(8,128)S(1)} async-done(((f32[16,2,64,256]{3,2,1,0:T(8,128)}), f32[16,2,64,256]{3,2,1,0:T(8,128)S(1)}, u32[]{:S(2)}, u32[]{:S(2)}) %all-to-all-start.2) | async-done | bytes 2097184 | tf_op jit(solution)/shard_map/all_to_all | solution.py:29
  165.9 0.1 reduce_sum.36
  166.1 0.1 broadcast_select_fusion
  166.2 0.1 select_reduce_fusion.1
  166.3 2.2 %select_reduce_fusion = f32[4,64,256]{2,1,0:T(8,128)S(1)} fusion(f32[16,2,64,256]{3,2,1,0:T(8,128)} %bitcast.76, pred[16,2,4]{2,1,0:T(4,128)(4,1)S(1)} %broadcast_compare_fusion), kind=kLoop, calls=%fused_computation.2 | loop fusion | flops 4128768 | bytes 2359424 | tf_op jit(solution)/shard_map/reduce_sum | solution.py:86
  168.5 0.7 add.35
  (22 shorter events, 0.3 us)
Async XLA Ops:
  6.5 44.3 %all-gather.5.cloned.1.call-start = ((), (), s32[]{:S(2)}) async-start(), calls=%async_computation.4 | async-start | bytes 2367488 | tf_op jit(solution)/shard_map/all_gather | solution.py:47
  12.2 24.8 %all-to-all-start.1 = ((bf16[16,2,64,256]{3,2,1,0:T(8,128)(2,1)}), bf16[16,2,64,256]{3,2,1,0:T(8,128)(2,1)S(1)}, u32[]{:S(2)}, u32[]{:S(2)}) async-start(bf16[16,2,64,256]{3,2,1,0:T(8,128)(2,1)} %broadcast_in_dim.104), calls=%async_computation.1 | async-start | bytes 2097152 | tf_op jit(solution)/shard_map/all_to_all | solution.py:21
  54.2 25.0 %all-to-all-start = ((bf16[16,2,64,256]{3,2,1,0:T(8,128)(2,1)}), bf16[16,2,64,256]{3,2,1,0:T(8,128)(2,1)S(1)}, u32[]{:S(2)}, u32[]{:S(2)}) async-start(bf16[16,2,64,256]{3,2,1,0:T(8,128)(2,1)} %broadcast_in_dim.100), calls=%async_computation | async-start | bytes 2097152 | tf_op jit(solution)/shard_map/all_to_all | solution.py:21
  80.6 4.1 %copy-start.2 = (bf16[512,4,1024]{2,0,1:T(8,128)(2,1)S(1)}, bf16[512,4,1024]{2,0,1:T(8,128)(2,1)}, u32[]{:S(2)}) copy-start(bf16[512,4,1024]{2,0,1:T(8,128)(2,1)} %convolution_convert_fusion) | copy-start | bytes 12582916
  83.6 1.0 copy-start
  85.9 3.3 %copy-start.3 = (bf16[2,4,256,256]{3,2,1,0:T(8,128)(2,1)}, bf16[2,4,256,256]{3,2,1,0:T(8,128)(2,1)S(1)}, u32[]{:S(2)}) copy-start(bf16[2,4,256,256]{3,2,1,0:T(8,128)(2,1)S(1)} %multiply_convert_fusion) | copy-start | bytes 3145732
  87.7 5.5 %copy-start.1 = (f32[2]{0:T(128)S(1)}, f32[2]{0:T(128)}, u32[]{:S(2)}) copy-start(f32[2]{0:T(128)} %param.14) | copy-start | bytes 28
  89.2 32.2 %all-to-all-start.3 = ((f32[16,2,64,256]{3,2,1,0:T(8,128)}), f32[16,2,64,256]{3,2,1,0:T(8,128)S(1)}, u32[]{:S(2)}, u32[]{:S(2)}) async-start(f32[16,2,64,256]{3,2,1,0:T(8,128)} %bitcast.73), calls=%async_computation.3 | async-start | bytes 4194304 | tf_op jit(solution)/shard_map/all_to_all | solution.py:29
  93.0 73.3 %all-gather.7.cloned.1.call-start = ((), (), s32[]{:S(2)}) async-start(), calls=%async_computation.5 | async-start | bytes 2228224 | tf_op jit(solution)/shard_map/all_gather | solution.py:77
  122.9 8.3 %copy-start.4 = (bf16[2,4,256,256]{3,2,1,0:T(8,128)(2,1)S(1)}, bf16[2,4,256,256]{3,2,1,0:T(8,128)(2,1)}, u32[]{:S(2)}) copy-start(bf16[2,4,256,256]{3,2,1,0:T(8,128)(2,1)} %copy-done.3) | copy-start | bytes 3145732
  134.5 31.4 %all-to-all-start.2 = ((f32[16,2,64,256]{3,2,1,0:T(8,128)}), f32[16,2,64,256]{3,2,1,0:T(8,128)S(1)}, u32[]{:S(2)}, u32[]{:S(2)}) async-start(f32[16,2,64,256]{3,2,1,0:T(8,128)} %bitcast.72), calls=%async_computation.2 | async-start | bytes 4194304 | tf_op jit(solution)/shard_map/all_to_all | solution.py:29
Sparse Core Ops, SparseCore 0:
  9.2 41.6 all-gather.4
  123.0 34.7 all-gather.6

commit v7 on v6

--- a/solution.py
+++ b/solution.py
@@ -23,9 +23,7 @@
     return jnp.transpose(got, (1, 0, 2, 3)).reshape(count, n_orb * rows, nocc)
 
 
-def scatter_rows(full, n_orb):
-    count, total, nocc = full.shape
-    parts = jnp.transpose(full.reshape(count, n_orb, total // n_orb, nocc), (1, 0, 2, 3))
+def scatter_rows(parts):
     got = lax.all_to_all(parts, "orb", 0, 0, tiled=True)
     return jnp.sum(got, axis=0)
 
@@ -69,15 +67,20 @@
     exchange = jnp.einsum("qtbc,btd->bqcd", projected_t, moved_full, preferred_element_type=jnp.float32)
     factor = 2.0 * weights[:, None, None, None] * aux_screen.astype(jnp.float32)[:, :, None, None]
     scaled = (factor * exchange).astype(jnp.bfloat16)
-    moved_term = jnp.einsum("qsbc,bqcd->bsd", projected_t, scaled, preferred_element_type=jnp.float32)
-    moved_grad = scatter_rows(moved_term, n_orb)
+    blocks = (dfit.shape[0], n_orb, rows, capacity, nocc)
+    moved_term = jnp.einsum(
+        "qorbc,bqcd->obrd", projected_t.reshape(blocks), scaled, preferred_element_type=jnp.float32
+    )
+    moved_grad = scatter_rows(moved_term)
     live = (weights != 0.0)[:, None, None]
     right_grad = jnp.where(live, jnp.einsum("brc,bdc->brd", moved_grad, inverse, precision=HI), 0.0)
 
     came = lax.all_gather(right_grad, "det", axis=0, tiled=False)
 
-    left_term = jnp.einsum("qsbc,bqdc->bsd", applied, scaled, preferred_element_type=jnp.float32)
-    left_grad = jnp.where(live, scatter_rows(left_term, n_orb), 0.0)
+    left_term = jnp.einsum(
+        "qorbc,bqdc->obrd", applied.reshape(blocks), scaled, preferred_element_type=jnp.float32
+    )
+    left_grad = jnp.where(live, scatter_rows(left_term), 0.0)
     own = left_local[:, None] == jnp.arange(det_local, dtype=jnp.int32)[None, :]
     own_sum = jnp.sum(jnp.where(own[:, :, None, None], left_grad[:, None], 0.0), axis=0)
 

time: 177 us -> 205 us (1.16)
  local copies, waits for them, and re-layouts: 12.4 us -> 36.6 us
  matrix products: 28.9 us -> 35.6 us
  waiting for transfers between devices: 90.9 us -> 84.6 us
  starting transfers between devices: 21.5 us -> 25.1 us
    another operation x0 -> x2, local copies, waits for them, and re-layouts: none -> 23.3 us  [the longest x1 11.7 us: local_body(): applied.reshape(blocks)]
    all_to_all x2, waiting for transfers between devices: 23.6 us -> 15.7 us  [gather_rows(): got = lax.all_to_all(spread, 'orb', 0, 0, tiled=True)]
    dot_general x2, matrix products: 3.57 us -> 8.4 us  [the longest x1 5.92 us: local_body(): jnp.einsum('qorbc,bqdc->obrd', applied.reshape(blocks), scaled, preferred...]
    all_to_all x2, starting transfers between devices: 7.45 us -> 10.9 us  [scatter_rows(): got = lax.all_to_all(parts, 'orb', 0, 0, tiled=True)]
    transpose x0 -> x2, local copies, waits for them, and re-layouts: none -> 3 us  [the longest x1 1.5 us: local_body(): jnp.einsum('qorbc,bqcd->obrd', projected_t.reshape(blocks), scaled, prefe...]
    reshape x2 -> x0, local copies, waits for them, and re-layouts: 2.94 us -> none  [scatter_rows(): full.reshape(count, n_orb, total // n_orb, nocc)]
  transfers between devices with their start and end apart: 6 -> 6, of which waited for: 5 -> 4; matrix products, arithmetic and copies ran while one was open for 17% -> 29% of each run, Pallas kernels for 0% -> 0%
where the time goes in v7:
time: 205 us; the launch traced here: 204 us
  waiting for transfers between devices  84.6 us (41%)
  local copies, waits for them, and re-layouts  36.6 us (18%)
  matrix products  35.6 us (17%)
  starting transfers between devices  25.1 us (12%)
  between operations  14.3 us (7%)
  other arithmetic  8.1 us (4%)
    all_to_all x2, waiting for transfers between devices, scatter_rows(): got = lax.all_to_all(parts, 'orb', 0, 0, tiled=True)  56.4 us
    all_to_all x2, waiting for transfers between devices, gather_rows(): got = lax.all_to_all(spread, 'orb', 0, 0, tiled=True)  15.7 us
    all_to_all x2, starting transfers between devices, gather_rows(): got = lax.all_to_all(spread, 'orb', 0, 0, tiled=True)  13.8 us
    all_gather x1, waiting for transfers between devices, local_body(): everyone = lax.all_gather(carried, 'det', axis=0, tiled=False)  12.4 us
    another operation x1, local copies, waits for them, and re-layouts, local_body(): applied.reshape(blocks)  11.7 us
    another operation x1, local copies, waits for them, and re-layouts, local_body(): projected_t.reshape(blocks)  11.6 us
    all_to_all x2, starting transfers between devices, scatter_rows(): got = lax.all_to_all(parts, 'orb', 0, 0, tiled=True)  10.9 us
    dot_general x1, matrix products, local_body(): jnp.einsum('qst,tk->qsk', dfit, left_stack, preferred_element_type=jnp.fl...  10.2 us
  transfers between devices with their start and end apart: 6, of which 4 were waited for; matrix products, arithmetic and copies ran while one was open for 29% of the time, Pallas kernels for 0%

profile of v7, /device:TPU:32, one launch (start us, length us, event | category | flops | bytes accessed | tf_op | source)
XLA Modules:
  0.0 204.2 jit_solution(7273915789652941432)
XLA Ops:
  6.5 0.7 compare_select_fusion
  7.3 1.6 fusion.25
  8.9 0.7 compare_and_fusion
  9.6 1.5 gather_fusion
  11.1 1.1 broadcast_in_dim.102
  12.2 7.0 %all-to-all-start = ((bf16[16,2,64,256]{3,2,1,0:T(8,128)(2,1)}), bf16[16,2,64,256]{3,2,1,0:T(8,128)(2,1)S(1)}, u32[]{:S(2)}, u32[]{:S(2)}) async-start(bf16[16,2,64,256]{3,2,1,0:T(8,128)(2,1)} %broadcast_in_dim.102), calls=%async_computation | async-start | bytes 2097152 | tf_op jit(solution)/shard_map/all_to_all | solution.py:21
  19.9 0.7 broadcast_multiply_fusion
  20.6 0.7 convert_multiply_fusion
  21.3 15.7 %all-to-all-done = bf16[16,2,64,256]{3,2,1,0:T(8,128)(2,1)S(1)} async-done(((bf16[16,2,64,256]{3,2,1,0:T(8,128)(2,1)}), bf16[16,2,64,256]{3,2,1,0:T(8,128)(2,1)S(1)}, u32[]{:S(2)}, u32[]{:S(2)}) %all-to-all-start) | async-done | bytes 1048608 | tf_op jit(solution)/shard_map/all_to_all | solution.py:21
  37.0 0.1 copy.54
  37.1 1.3 copy.55
  38.4 12.4 %all-gather.5.cloned.1.call-done = bf16[4352,256]{1,0:T(8,128)(2,1)} async-done(((bf16[272,256]{1,0:T(8,128)(2,1)}), bf16[4352,256]{1,0:T(8,128)(2,1)}) %all-gather.5.cloned.1.call-update) | async-done | bytes 2228240 | tf_op jit(solution)/shard_map/all_gather | solution.py:45
  50.8 1.7 slice.28
  52.6 0.6 gather_fusion.1
  53.1 1.1 broadcast_in_dim.104
  54.2 6.8 %all-to-all-start.1 = ((bf16[16,2,64,256]{3,2,1,0:T(8,128)(2,1)}), bf16[16,2,64,256]{3,2,1,0:T(8,128)(2,1)S(1)}, u32[]{:S(2)}, u32[]{:S(2)}) async-start(bf16[16,2,64,256]{3,2,1,0:T(8,128)(2,1)} %broadcast_in_dim.104), calls=%async_computation.1 | async-start | bytes 2097152 | tf_op jit(solution)/shard_map/all_to_all | solution.py:21
  61.1 10.2 %convolution_convert_fusion = bf16[512,4,1024]{2,0,1:T(8,128)(2,1)} fusion(bf16[1024,512,1]{0,1,2:T(8,128)(2,1)} %bitcast.87, bf16[4,1024,1024]{2,1,0:T(8,128)(2,1)} %param.10), kind=kOutput, calls=%fused_computation.10 | convolution fusion | flops 4297064448 | bytes 13631488 | tf_op jit(solution)/shard_map/qst,tk->qsk/dot_general | solution.py:53
  71.3 11.6 %reshape.148 = bf16[4,16,64,2,256]{2,1,4,3,0:T(8,128)(2,1)} reshape(bf16[4,1024,512]{1,2,0:T(8,128)(2,1)} %bitcast.79) | data formatting | bytes 8388608 | tf_op jit(solution)/shard_map/reshape;reshape | solution.py:72
  82.9 0.1 copy.56
  83.0 0.5 fusion.27
  83.5 0.7 convolution_subtract_fusion.1
  84.2 0.7 fusion.18
  84.9 0.7 convolution_subtract_fusion
  85.6 0.7 fusion.28
  86.2 1.0 convolution_convert_fusion.1
  87.3 1.0 copy-done.1
  88.3 1.3 fusion.14
  89.6 0.9 slice-done.1
  90.4 2.5 %fusion.9 = f32[16,2,64,256]{3,2,0,1:T(8,128)S(1)} fusion(bf16[2,4,256,256,1]{3,2,1,4,0:T(8,128)(2,1)S(1)} %fusion.14, bf16[4,16,64,2,256]{2,1,4,3,0:T(8,128)(2,1)S(1)} %bitcast.78), kind=kOutput, calls=%fused_computation.13 | convolution fusion | flops 1073741824 | bytes 7340032 | tf_op jit(solution)/shard_map/qorbc,bqcd->obrd/dot_general | solution.py:71
  92.9 1.5 copy.68
  94.4 7.2 %all-to-all-start.3 = ((f32[16,2,64,256]{3,2,1,0:T(8,128)}), f32[16,2,64,256]{3,2,1,0:T(8,128)S(1)}, u32[]{:S(2)}, u32[]{:S(2)}) async-start(f32[16,2,64,256]{3,2,1,0:T(8,128)} %copy.68), calls=%async_computation.3 | async-start | bytes 4194304 | tf_op jit(solution)/shard_map/all_to_all | solution.py:27
  101.7 0.3 all-gather.7.cloned.1.call-start
  102.0 29.8 %all-to-all-done.3 = f32[16,2,64,256]{3,2,1,0:T(8,128)S(1)} async-done(((f32[16,2,64,256]{3,2,1,0:T(8,128)}), f32[16,2,64,256]{3,2,1,0:T(8,128)S(1)}, u32[]{:S(2)}, u32[]{:S(2)}) %all-to-all-start.3) | async-done | bytes 2097184 | tf_op jit(solution)/shard_map/all_to_all | solution.py:27
  131.8 0.1 reduce_sum.38
  131.9 1.3 convolution_select_fusion
  133.2 10.2 %convert_bitcast_fusion = bf16[4,1024,512]{1,2,0:T(8,128)(2,1)} fusion(bf16[1024,512,1]{0,1,2:T(8,128)(2,1)} %bitcast.86, bf16[4,1024,1024]{2,1,0:T(8,128)(2,1)} %param.10), kind=kOutput, calls=%fused_computation.9 | convolution fusion | flops 4297064448 | bytes 13631488 | tf_op jit(solution)/shard_map/qst,tk->qsk/dot_general | solution.py:63
  143.4 11.7 %reshape.147 = bf16[4,16,64,2,256]{2,1,4,3,0:T(8,128)(2,1)} reshape(bf16[4,1024,512]{1,2,0:T(8,128)(2,1)} %convert_bitcast_fusion) | data formatting | bytes 8388608 | tf_op jit(solution)/shard_map/reshape;reshape | solution.py:81
  155.1 5.9 %fusion.6 = f32[16,2,64,256]{3,2,0,1:T(8,128)S(1)} fusion(bf16[2,4,256,256,1]{3,2,1,4,0:T(8,128)(2,1)S(1)} %copy-done.4, bf16[4,16,64,2,256]{2,1,4,3,0:T(8,128)(2,1)} %reshape.147), kind=kOutput, calls=%fused_computation.12 | convolution fusion | flops 1073741824 | bytes 7340032 | tf_op jit(solution)/shard_map/qorbc,bqdc->obrd/dot_general | solution.py:80
  161.0 1.5 copy.63
  162.5 3.7 %all-to-all-start.2 = ((f32[16,2,64,256]{3,2,1,0:T(8,128)}), f32[16,2,64,256]{3,2,1,0:T(8,128)S(1)}, u32[]{:S(2)}, u32[]{:S(2)}) async-start(f32[16,2,64,256]{3,2,1,0:T(8,128)} %copy.63), calls=%async_computation.2 | async-start | bytes 4194304 | tf_op jit(solution)/shard_map/all_to_all | solution.py:27
  166.4 0.8 slice.29
  167.1 0.1 copy.81
  167.2 0.1 copy.65
  167.4 26.6 %all-to-all-done.2 = f32[16,2,64,256]{3,2,1,0:T(8,128)S(1)} async-done(((f32[16,2,64,256]{3,2,1,0:T(8,128)}), f32[16,2,64,256]{3,2,1,0:T(8,128)S(1)}, u32[]{:S(2)}, u32[]{:S(2)}) %all-to-all-start.2) | async-done | bytes 2097184 | tf_op jit(solution)/shard_map/all_to_all | solution.py:27
  194.1 0.1 reduce_sum.36
  194.3 0.1 select_reduce_fusion.1
  194.4 2.2 %select_reduce_fusion = f32[4,64,256]{2,1,0:T(8,128)S(1)} fusion(f32[16,2,64,256]{3,2,1,0:T(8,128)} %bitcast.83, pred[16,2,4]{2,1,0:T(4,128)(4,1)S(1)} %broadcast_compare_fusion), kind=kLoop, calls=%fused_computation.6 | loop fusion | flops 4128768 | bytes 2359424 | tf_op jit(solution)/shard_map/reduce_sum | solution.py:89
  196.7 0.7 add.35
  (29 shorter events, 0.5 us)
Async XLA Ops:
  6.5 44.3 %all-gather.5.cloned.1.call-start = ((), (), s32[]{:S(2)}) async-start(), calls=%async_computation.4 | async-start | bytes 2367488 | tf_op jit(solution)/shard_map/all_gather | solution.py:45
  12.2 24.8 %all-to-all-start = ((bf16[16,2,64,256]{3,2,1,0:T(8,128)(2,1)}), bf16[16,2,64,256]{3,2,1,0:T(8,128)(2,1)S(1)}, u32[]{:S(2)}, u32[]{:S(2)}) async-start(bf16[16,2,64,256]{3,2,1,0:T(8,128)(2,1)} %broadcast_in_dim.102), calls=%async_computation | async-start | bytes 2097152 | tf_op jit(solution)/shard_map/all_to_all | solution.py:21
  54.2 28.6 %all-to-all-start.1 = ((bf16[16,2,64,256]{3,2,1,0:T(8,128)(2,1)}), bf16[16,2,64,256]{3,2,1,0:T(8,128)(2,1)S(1)}, u32[]{:S(2)}, u32[]{:S(2)}) async-start(bf16[16,2,64,256]{3,2,1,0:T(8,128)(2,1)} %broadcast_in_dim.104), calls=%async_computation.1 | async-start | bytes 2097152 | tf_op jit(solution)/shard_map/all_to_all | solution.py:21
  84.2 4.0 %copy-start = (bf16[512,4,1024]{2,0,1:T(8,128)(2,1)S(1)}, bf16[512,4,1024]{2,0,1:T(8,128)(2,1)}, u32[]{:S(2)}) copy-start(bf16[512,4,1024]{2,0,1:T(8,128)(2,1)} %convolution_convert_fusion) | copy-start | bytes 12582916
  84.9 4.6 %slice-start = ((s8[8388608]{0:T(1024)(128)(4,1)}), s8[4194304]{0:T(1024)(128)(4,1)S(1)}, s32[]{:S(2)}) async-start(s8[8388608]{0:T(1024)(128)(4,1)} %bitcast.77), calls=%async_computation.6 | async-start | bytes 8388608
  87.3 1.0 copy-start.1
  88.2 2.2 %slice-start.1 = ((s8[8388608]{0:T(1024)(128)(4,1)}), s8[4194304]{0:T(1024)(128)(4,1)S(1)}, s32[]{:S(2)}) async-start(s8[8388608]{0:T(1024)(128)(4,1)} %bitcast.77), calls=%async_computation.7 | async-start | bytes 8388608
  90.4 2.5 %copy-start.3 = (bf16[2,4,256,256,1]{3,2,1,4,0:T(8,128)(2,1)}, bf16[2,4,256,256,1]{3,2,1,4,0:T(8,128)(2,1)S(1)}, u32[]{:S(2)}) copy-start(bf16[2,4,256,256,1]{3,2,1,4,0:T(8,128)(2,1)S(1)} %fusion.14) | copy-start | bytes 3145732
  92.9 9.0 %copy-start.2 = (f32[2]{0:T(128)S(1)}, f32[2]{0:T(128)}, u32[]{:S(2)}) copy-start(f32[2]{0:T(128)} %param.14) | copy-start | bytes 28
  94.4 37.3 %all-to-all-start.3 = ((f32[16,2,64,256]{3,2,1,0:T(8,128)}), f32[16,2,64,256]{3,2,1,0:T(8,128)S(1)}, u32[]{:S(2)}, u32[]{:S(2)}) async-start(f32[16,2,64,256]{3,2,1,0:T(8,128)} %copy.68), calls=%async_computation.3 | async-start | bytes 4194304 | tf_op jit(solution)/shard_map/all_to_all | solution.py:27
  101.7 92.7 %all-gather.7.cloned.1.call-start = ((), (), s32[]{:S(2)}) async-start(), calls=%async_computation.5 | async-start | bytes 2228224 | tf_op jit(solution)/shard_map/all_gather | solution.py:78
  143.4 11.7 %copy-start.4 = (bf16[2,4,256,256,1]{3,2,1,4,0:T(8,128)(2,1)S(1)}, bf16[2,4,256,256,1]{3,2,1,4,0:T(8,128)(2,1)}, u32[]{:S(2)}) copy-start(bf16[2,4,256,256,1]{3,2,1,4,0:T(8,128)(2,1)} %copy-done.3) | copy-start | bytes 3145732
  162.5 31.5 %all-to-all-start.2 = ((f32[16,2,64,256]{3,2,1,0:T(8,128)}), f32[16,2,64,256]{3,2,1,0:T(8,128)S(1)}, u32[]{:S(2)}, u32[]{:S(2)}) async-start(f32[16,2,64,256]{3,2,1,0:T(8,128)} %copy.63), calls=%async_computation.2 | async-start | bytes 4194304 | tf_op jit(solution)/shard_map/all_to_all | solution.py:27
Sparse Core Ops, SparseCore 0:
  9.2 41.6 all-gather.4
  133.3 34.7 all-gather.6

commit v8 on v6

--- a/solution.py
+++ b/solution.py
@@ -23,9 +23,13 @@
     return jnp.transpose(got, (1, 0, 2, 3)).reshape(count, n_orb * rows, nocc)
 
 
-def scatter_rows(full, n_orb):
+def row_blocks(full, n_orb):
     count, total, nocc = full.shape
-    parts = jnp.transpose(full.reshape(count, n_orb, total // n_orb, nocc), (1, 0, 2, 3))
+    return jnp.transpose(full.reshape(count, n_orb, total // n_orb, nocc), (1, 0, 2, 3))
+
+
+def scatter_rows(full, n_orb, parts=None):
+    parts = row_blocks(full, n_orb) if parts is None else parts
     got = lax.all_to_all(parts, "orb", 0, 0, tiled=True)
     return jnp.sum(got, axis=0)
 
@@ -77,7 +81,8 @@
     came = lax.all_gather(right_grad, "det", axis=0, tiled=False)
 
     left_term = jnp.einsum("qsbc,bqdc->bsd", applied, scaled, preferred_element_type=jnp.float32)
-    left_grad = jnp.where(live, scatter_rows(left_term, n_orb), 0.0)
+    left_parts = row_blocks(left_term, n_orb)
+    left_grad = jnp.where(live, scatter_rows(None, n_orb, left_parts), 0.0)
     own = left_local[:, None] == jnp.arange(det_local, dtype=jnp.int32)[None, :]
     own_sum = jnp.sum(jnp.where(own[:, :, None, None], left_grad[:, None], 0.0), axis=0)
 

time: 177 us -> 177 us (level)
  no operation moved by 1% of the time
where the time goes in v8:
time: 177 us; the launch traced here: 176 us
  waiting for transfers between devices  90.9 us (51%)
  matrix products  28.9 us (16%)
  starting transfers between devices  21.5 us (12%)
  between operations  14.3 us (8%)
  local copies, waits for them, and re-layouts  12.4 us (7%)
  other arithmetic  8.1 us (5%)
    all_to_all x2, waiting for transfers between devices, scatter_rows(): got = lax.all_to_all(parts, 'orb', 0, 0, tiled=True)  54.8 us
    all_to_all x2, waiting for transfers between devices, gather_rows(): got = lax.all_to_all(spread, 'orb', 0, 0, tiled=True)  23.6 us
    all_to_all x2, starting transfers between devices, gather_rows(): got = lax.all_to_all(spread, 'orb', 0, 0, tiled=True)  13.8 us
    all_gather x1, waiting for transfers between devices, local_body(): everyone = lax.all_gather(carried, 'det', axis=0, tiled=False)  12.4 us
    dot_general x1, matrix products, local_body(): jnp.einsum('qst,tk->qsk', dfit, left_stack, preferred_element_type=jnp.fl...  10.2 us
    dot_general x1, matrix products, local_body(): jnp.einsum('qst,tk->qsk', dfit, moved_stack, preferred_element_type=jnp.f...  8.32 us
    all_to_all x2, starting transfers between devices, scatter_rows(): got = lax.all_to_all(parts, 'orb', 0, 0, tiled=True)  7.45 us
  transfers between devices with their start and end apart: 6, of which 5 were waited for; matrix products, arithmetic and copies ran while one was open for 17% of the time, Pallas kernels for 0%

profile of v8, /device:TPU:32, one launch (start us, length us, event | category | flops | bytes accessed | tf_op | source)
XLA Modules:
  0.0 176.1 jit_solution(9813548415853753420)
XLA Ops:
  6.5 0.7 compare_select_fusion.1
  7.3 1.6 fusion.16
  8.9 0.7 compare_and_fusion
  9.6 1.5 gather_fusion.1
  11.1 1.1 broadcast_in_dim.104
  12.2 7.0 %all-to-all-start.1 = ((bf16[16,2,64,256]{3,2,1,0:T(8,128)(2,1)}), bf16[16,2,64,256]{3,2,1,0:T(8,128)(2,1)S(1)}, u32[]{:S(2)}, u32[]{:S(2)}) async-start(bf16[16,2,64,256]{3,2,1,0:T(8,128)(2,1)} %broadcast_in_dim.104), calls=%async_computation.1 | async-start | bytes 2097152 | tf_op jit(solution)/shard_map/all_to_all | solution.py:21
  19.9 0.7 broadcast_multiply_fusion
  20.6 0.7 convert_multiply_fusion
  21.3 15.7 %all-to-all-done.1 = bf16[16,2,64,256]{3,2,1,0:T(8,128)(2,1)S(1)} async-done(((bf16[16,2,64,256]{3,2,1,0:T(8,128)(2,1)}), bf16[16,2,64,256]{3,2,1,0:T(8,128)(2,1)S(1)}, u32[]{:S(2)}, u32[]{:S(2)}) %all-to-all-start.1) | async-done | bytes 1048608 | tf_op jit(solution)/shard_map/all_to_all | solution.py:21
  37.0 0.1 copy.55
  37.1 1.4 copy.58
  38.5 12.4 %all-gather.5.cloned.1.call-done = bf16[4352,256]{1,0:T(8,128)(2,1)} async-done(((bf16[272,256]{1,0:T(8,128)(2,1)}), bf16[4352,256]{1,0:T(8,128)(2,1)}) %all-gather.5.cloned.1.call-update) | async-done | bytes 2228240 | tf_op jit(solution)/shard_map/all_gather | solution.py:51
  50.8 1.7 slice.28
  52.6 0.6 gather_fusion
  53.1 1.1 broadcast_in_dim.100
  54.2 6.8 %all-to-all-start = ((bf16[16,2,64,256]{3,2,1,0:T(8,128)(2,1)}), bf16[16,2,64,256]{3,2,1,0:T(8,128)(2,1)S(1)}, u32[]{:S(2)}, u32[]{:S(2)}) async-start(bf16[16,2,64,256]{3,2,1,0:T(8,128)(2,1)} %broadcast_in_dim.100), calls=%async_computation | async-start | bytes 2097152 | tf_op jit(solution)/shard_map/all_to_all | solution.py:21
  61.1 10.2 %convolution_convert_fusion = bf16[512,4,1024]{2,0,1:T(8,128)(2,1)} fusion(bf16[1024,512,1]{0,1,2:T(8,128)(2,1)} %bitcast.82, bf16[4,1024,1024]{2,1,0:T(8,128)(2,1)} %param.10), kind=kOutput, calls=%fused_computation.5 | convolution fusion | flops 4297064448 | bytes 13631488 | tf_op jit(solution)/shard_map/qst,tk->qsk/dot_general | solution.py:59
  71.3 8.0 %all-to-all-done = bf16[16,2,64,256]{3,2,1,0:T(8,128)(2,1)S(1)} async-done(((bf16[16,2,64,256]{3,2,1,0:T(8,128)(2,1)}), bf16[16,2,64,256]{3,2,1,0:T(8,128)(2,1)S(1)}, u32[]{:S(2)}, u32[]{:S(2)}) %all-to-all-start) | async-done | bytes 1048608 | tf_op jit(solution)/shard_map/all_to_all | solution.py:21
  79.3 0.1 copy.54
  79.4 0.5 fusion.18
  79.9 0.7 convolution_subtract_fusion.1
  80.6 0.7 fusion.9
  81.3 0.7 convolution_subtract_fusion
  81.9 0.7 fusion.19
  82.6 1.0 convolution_convert_fusion.2
  83.7 1.0 copy-done
  84.6 1.3 multiply_convert_fusion
  85.9 1.8 %fusion.5 = f32[2,1024,256,1]{2,1,0,3:T(8,128)S(1)} fusion(bf16[4,1024,2,256]{1,3,2,0:T(8,128)(2,1)S(1)} %bitcast.85, bf16[2,4,256,256]{3,2,1,0:T(8,128)(2,1)S(1)} %multiply_convert_fusion), kind=kOutput, calls=%fused_computation.15 | convolution fusion | flops 1073741824 | bytes 7340032 | tf_op jit(solution)/shard_map/qsbc,bqcd->bsd/dot_general | solution.py:76
  87.7 1.5 copy.87
  89.2 3.7 %all-to-all-start.3 = ((f32[16,2,64,256]{3,2,1,0:T(8,128)}), f32[16,2,64,256]{3,2,1,0:T(8,128)S(1)}, u32[]{:S(2)}, u32[]{:S(2)}) async-start(f32[16,2,64,256]{3,2,1,0:T(8,128)} %bitcast.73), calls=%async_computation.3 | async-start | bytes 4194304 | tf_op jit(solution)/shard_map/all_to_all | solution.py:33
  93.0 0.2 all-gather.7.cloned.1.call-start
  93.2 28.3 %all-to-all-done.3 = f32[16,2,64,256]{3,2,1,0:T(8,128)S(1)} async-done(((f32[16,2,64,256]{3,2,1,0:T(8,128)}), f32[16,2,64,256]{3,2,1,0:T(8,128)S(1)}, u32[]{:S(2)}, u32[]{:S(2)}) %all-to-all-start.3) | async-done | bytes 2097184 | tf_op jit(solution)/shard_map/all_to_all | solution.py:33
  121.5 0.1 reduce_sum.38
  121.6 1.3 convolution_select_fusion
  122.9 8.3 %convolution_convert_fusion.1 = bf16[512,4,1024]{2,0,1:T(8,128)(2,1)S(1)} fusion(bf16[1024,512,1]{0,1,2:T(8,128)(2,1)} %bitcast.81, bf16[4,1024,1024]{2,1,0:T(8,128)(2,1)} %param.10), kind=kOutput, calls=%fused_computation.6 | convolution fusion | flops 4297064448 | bytes 13631488 | tf_op jit(solution)/shard_map/qst,tk->qsk/dot_general | solution.py:69
  131.2 1.8 %fusion.7 = f32[2,1024,256,1]{2,1,0,3:T(8,128)S(1)} fusion(bf16[4,1024,2,256]{1,3,2,0:T(8,128)(2,1)S(1)} %bitcast.86, bf16[2,4,256,256]{3,2,1,0:T(8,128)(2,1)S(1)} %copy-done.4), kind=kOutput, calls=%fused_computation.17 | convolution fusion | flops 1073741824 | bytes 7340032 | tf_op jit(solution)/shard_map/qsbc,bqdc->bsd/dot_general | solution.py:83
  133.0 1.5 copy.88
  134.5 3.7 %all-to-all-start.2 = ((f32[16,2,64,256]{3,2,1,0:T(8,128)}), f32[16,2,64,256]{3,2,1,0:T(8,128)S(1)}, u32[]{:S(2)}, u32[]{:S(2)}) async-start(f32[16,2,64,256]{3,2,1,0:T(8,128)} %bitcast.72), calls=%async_computation.2 | async-start | bytes 4194304 | tf_op jit(solution)/shard_map/all_to_all | solution.py:33
  138.3 0.8 slice.29
  139.1 0.1 copy.76
  139.2 0.1 copy.65
  139.3 0.1 broadcast_compare_fusion
  139.4 26.6 %all-to-all-done.2 = f32[16,2,64,256]{3,2,1,0:T(8,128)S(1)} async-done(((f32[16,2,64,256]{3,2,1,0:T(8,128)}), f32[16,2,64,256]{3,2,1,0:T(8,128)S(1)}, u32[]{:S(2)}, u32[]{:S(2)}) %all-to-all-start.2) | async-done | bytes 2097184 | tf_op jit(solution)/shard_map/all_to_all | solution.py:33
  165.9 0.1 reduce_sum.36
  166.1 0.1 broadcast_select_fusion
  166.2 0.1 select_reduce_fusion.1
  166.3 2.2 %select_reduce_fusion = f32[4,64,256]{2,1,0:T(8,128)S(1)} fusion(f32[16,2,64,256]{3,2,1,0:T(8,128)} %bitcast.76, pred[16,2,4]{2,1,0:T(4,128)(4,1)S(1)} %broadcast_compare_fusion), kind=kLoop, calls=%fused_computation.2 | loop fusion | flops 4128768 | bytes 2359424 | tf_op jit(solution)/shard_map/reduce_sum | solution.py:91
  168.5 0.7 add.35
  (22 shorter events, 0.3 us)
Async XLA Ops:
  6.5 44.3 %all-gather.5.cloned.1.call-start = ((), (), s32[]{:S(2)}) async-start(), calls=%async_computation.4 | async-start | bytes 2367488 | tf_op jit(solution)/shard_map/all_gather | solution.py:51
  12.2 24.8 %all-to-all-start.1 = ((bf16[16,2,64,256]{3,2,1,0:T(8,128)(2,1)}), bf16[16,2,64,256]{3,2,1,0:T(8,128)(2,1)S(1)}, u32[]{:S(2)}, u32[]{:S(2)}) async-start(bf16[16,2,64,256]{3,2,1,0:T(8,128)(2,1)} %broadcast_in_dim.104), calls=%async_computation.1 | async-start | bytes 2097152 | tf_op jit(solution)/shard_map/all_to_all | solution.py:21
  54.2 25.0 %all-to-all-start = ((bf16[16,2,64,256]{3,2,1,0:T(8,128)(2,1)}), bf16[16,2,64,256]{3,2,1,0:T(8,128)(2,1)S(1)}, u32[]{:S(2)}, u32[]{:S(2)}) async-start(bf16[16,2,64,256]{3,2,1,0:T(8,128)(2,1)} %broadcast_in_dim.100), calls=%async_computation | async-start | bytes 2097152 | tf_op jit(solution)/shard_map/all_to_all | solution.py:21
  80.6 4.1 %copy-start.2 = (bf16[512,4,1024]{2,0,1:T(8,128)(2,1)S(1)}, bf16[512,4,1024]{2,0,1:T(8,128)(2,1)}, u32[]{:S(2)}) copy-start(bf16[512,4,1024]{2,0,1:T(8,128)(2,1)} %convolution_convert_fusion) | copy-start | bytes 12582916
  83.6 1.0 copy-start
  85.9 3.3 %copy-start.3 = (bf16[2,4,256,256]{3,2,1,0:T(8,128)(2,1)}, bf16[2,4,256,256]{3,2,1,0:T(8,128)(2,1)S(1)}, u32[]{:S(2)}) copy-start(bf16[2,4,256,256]{3,2,1,0:T(8,128)(2,1)S(1)} %multiply_convert_fusion) | copy-start | bytes 3145732
  87.7 5.5 %copy-start.1 = (f32[2]{0:T(128)S(1)}, f32[2]{0:T(128)}, u32[]{:S(2)}) copy-start(f32[2]{0:T(128)} %param.14) | copy-start | bytes 28
  89.2 32.2 %all-to-all-start.3 = ((f32[16,2,64,256]{3,2,1,0:T(8,128)}), f32[16,2,64,256]{3,2,1,0:T(8,128)S(1)}, u32[]{:S(2)}, u32[]{:S(2)}) async-start(f32[16,2,64,256]{3,2,1,0:T(8,128)} %bitcast.73), calls=%async_computation.3 | async-start | bytes 4194304 | tf_op jit(solution)/shard_map/all_to_all | solution.py:33
  93.0 73.3 %all-gather.7.cloned.1.call-start = ((), (), s32[]{:S(2)}) async-start(), calls=%async_computation.5 | async-start | bytes 2228224 | tf_op jit(solution)/shard_map/all_gather | solution.py:81
  122.9 8.3 %copy-start.4 = (bf16[2,4,256,256]{3,2,1,0:T(8,128)(2,1)S(1)}, bf16[2,4,256,256]{3,2,1,0:T(8,128)(2,1)}, u32[]{:S(2)}) copy-start(bf16[2,4,256,256]{3,2,1,0:T(8,128)(2,1)} %copy-done.3) | copy-start | bytes 3145732
  134.5 31.4 %all-to-all-start.2 = ((f32[16,2,64,256]{3,2,1,0:T(8,128)}), f32[16,2,64,256]{3,2,1,0:T(8,128)S(1)}, u32[]{:S(2)}, u32[]{:S(2)}) async-start(f32[16,2,64,256]{3,2,1,0:T(8,128)} %bitcast.72), calls=%async_computation.2 | async-start | bytes 4194304 | tf_op jit(solution)/shard_map/all_to_all | solution.py:33
Sparse Core Ops, SparseCore 0:
  9.2 41.6 all-gather.4
  123.0 34.7 all-gather.6

commit v9 on v8

--- a/solution.py
+++ b/solution.py
@@ -50,9 +50,11 @@
     carried = jnp.concatenate([orbitals.reshape(det_local * rows, nocc), marks], axis=0)
     everyone = lax.all_gather(carried, "det", axis=0, tiled=False)
     right_all = everyone[:, det_local * rows, :capacity].astype(jnp.int32).reshape(-1)
-    fetched = everyone[:, : det_local * rows].reshape(n_det * det_local, rows, nocc)
     left_full = gather_rows(left_rows, n_orb)
-    right_rows = fetched[pair_right]
+    right_rows = jnp.stack([
+        lax.dynamic_slice(everyone, (pair_right[k] // det_local, (pair_right[k] % det_local) * rows, 0), (1, rows, nocc))[0]
+        for k in range(capacity)
+    ])
     right_full = gather_rows(right_rows, n_orb)
 
     left_stack = jnp.transpose(left_full, (1, 0, 2)).reshape(n_orb * rows, capacity * nocc)

time: 177 us -> 175 us (0.989)
  between operations: 14.3 us -> 19.4 us
  waiting for transfers between devices: 90.9 us -> 87.4 us
    all_to_all x2, waiting for transfers between devices: 23.6 us -> 19.2 us  [gather_rows(): got = lax.all_to_all(spread, 'orb', 0, 0, tiled=True)]
  transfers between devices with their start and end apart: 6 -> 6, of which waited for: 5 -> 5; matrix products, arithmetic and copies ran while one was open for 17% -> 16% of each run, Pallas kernels for 0% -> 0%
where the time goes in v9:
time: 175 us
  waiting for transfers between devices  87.4 us (50%)
  matrix products  28.1 us (16%)
  starting transfers between devices  21.5 us (12%)
  between operations  19.4 us (11%)
  local copies, waits for them, and re-layouts  11.4 us (7%)
  other arithmetic  6.72 us (4%)
    all_to_all x2, waiting for transfers between devices, scatter_rows(): got = lax.all_to_all(parts, 'orb', 0, 0, tiled=True)  54.9 us
    all_to_all x2, waiting for transfers between devices, gather_rows(): got = lax.all_to_all(spread, 'orb', 0, 0, tiled=True)  19.2 us
    all_to_all x2, starting transfers between devices, gather_rows(): got = lax.all_to_all(spread, 'orb', 0, 0, tiled=True)  13.8 us
    all_gather x1, waiting for transfers between devices, local_body(): everyone = lax.all_gather(carried, 'det', axis=0, tiled=False)  13.3 us
    dot_general x1, matrix products, local_body(): jnp.einsum('qst,tk->qsk', dfit, left_stack, preferred_element_type=jnp.fl...  9.45 us
    dot_general x1, matrix products, local_body(): jnp.einsum('qst,tk->qsk', dfit, moved_stack, preferred_element_type=jnp.f...  8.32 us
    all_to_all x2, starting transfers between devices, scatter_rows(): got = lax.all_to_all(parts, 'orb', 0, 0, tiled=True)  7.45 us
  transfers between devices with their start and end apart: 6, of which 5 were waited for; matrix products, arithmetic and copies ran while one was open for 16% of the time, Pallas kernels for 0%

profile of v9, /device:TPU:32, one launch (start us, length us, event | category | flops | bytes accessed | tf_op | source)
XLA Modules:
  0.0 174.6 jit_solution(7217668087286738744)
XLA Ops:
  6.5 0.7 convert_bitcast_fusion
  7.2 1.6 fusion.16
  8.8 0.7 compare_and_fusion
  9.5 1.5 gather_fusion
  11.0 0.1 broadcast_select_fusion.1
  11.1 1.1 broadcast_in_dim.100
  12.2 7.0 %all-to-all-start.1 = ((bf16[16,2,64,256]{3,2,1,0:T(8,128)(2,1)}), bf16[16,2,64,256]{3,2,1,0:T(8,128)(2,1)S(1)}, u32[]{:S(2)}, u32[]{:S(2)}) async-start(bf16[16,2,64,256]{3,2,1,0:T(8,128)(2,1)} %broadcast_in_dim.100), calls=%async_computation.1 | async-start | bytes 2097152 | tf_op jit(solution)/shard_map/all_to_all | solution.py:21
  19.2 1.4 fusion.18
  26.4 10.5 %all-to-all-done.1 = bf16[16,2,64,256]{3,2,1,0:T(8,128)(2,1)S(1)} async-done(((bf16[16,2,64,256]{3,2,1,0:T(8,128)(2,1)}), bf16[16,2,64,256]{3,2,1,0:T(8,128)(2,1)S(1)}, u32[]{:S(2)}, u32[]{:S(2)}) %all-to-all-start.1) | async-done | bytes 1048608 | tf_op jit(solution)/shard_map/all_to_all | solution.py:21
  36.9 0.1 copy.56
  37.1 0.5 copy.59
  37.6 13.3 %all-gather.5.cloned.1.call-done = bf16[4352,256]{1,0:T(8,128)(2,1)} async-done(((bf16[272,256]{1,0:T(8,128)(2,1)}), bf16[4352,256]{1,0:T(8,128)(2,1)}) %all-gather.5.cloned.1.call-update) | async-done | bytes 2228240 | tf_op jit(solution)/shard_map/all_gather | solution.py:51
  50.9 0.8 constant_dynamic-slice_fusion.1
  51.7 1.1 broadcast_in_dim.96
  52.8 6.8 %all-to-all-start = ((bf16[16,2,64,256]{3,2,1,0:T(8,128)(2,1)}), bf16[16,2,64,256]{3,2,1,0:T(8,128)(2,1)S(1)}, u32[]{:S(2)}, u32[]{:S(2)}) async-start(bf16[16,2,64,256]{3,2,1,0:T(8,128)(2,1)} %broadcast_in_dim.96), calls=%async_computation | async-start | bytes 2097152 | tf_op jit(solution)/shard_map/all_to_all | solution.py:21
  59.6 9.4 %convolution_convert_fusion = bf16[512,4,1024]{2,0,1:T(8,128)(2,1)} fusion(bf16[1024,512,1]{0,1,2:T(8,128)(2,1)S(1)} %bitcast.80, bf16[4,1024,1024]{2,1,0:T(8,128)(2,1)} %param.10), kind=kOutput, calls=%fused_computation.4 | convolution fusion | flops 4297064448 | bytes 13631488 | tf_op jit(solution)/shard_map/qst,tk->qsk/dot_general | solution.py:61
  69.0 8.7 %all-to-all-done = bf16[16,2,64,256]{3,2,1,0:T(8,128)(2,1)S(1)} async-done(((bf16[16,2,64,256]{3,2,1,0:T(8,128)(2,1)}), bf16[16,2,64,256]{3,2,1,0:T(8,128)(2,1)S(1)}, u32[]{:S(2)}, u32[]{:S(2)}) %all-to-all-start) | async-done | bytes 1048608 | tf_op jit(solution)/shard_map/all_to_all | solution.py:21
  77.8 0.1 copy.55
  77.9 0.5 fusion.19
  78.4 0.7 convolution_subtract_fusion.1
  79.1 0.7 fusion.9
  79.8 0.7 convolution_subtract_fusion
  80.4 0.7 fusion.20
  81.1 1.0 convolution_convert_fusion.2
  82.2 1.0 copy-done
  83.1 1.3 multiply_convert_fusion
  84.4 1.8 %fusion.5 = f32[2,1024,256,1]{2,1,0,3:T(8,128)S(1)} fusion(bf16[4,1024,2,256]{1,3,2,0:T(8,128)(2,1)S(1)} %bitcast.85, bf16[2,4,256,256]{3,2,1,0:T(8,128)(2,1)S(1)} %multiply_convert_fusion), kind=kOutput, calls=%fused_computation.14 | convolution fusion | flops 1073741824 | bytes 7340032 | tf_op jit(solution)/shard_map/qsbc,bqcd->bsd/dot_general | solution.py:78
  86.2 1.5 copy.88
  87.7 3.7 %all-to-all-start.3 = ((f32[16,2,64,256]{3,2,1,0:T(8,128)}), f32[16,2,64,256]{3,2,1,0:T(8,128)S(1)}, u32[]{:S(2)}, u32[]{:S(2)}) async-start(f32[16,2,64,256]{3,2,1,0:T(8,128)} %bitcast.74), calls=%async_computation.3 | async-start | bytes 4194304 | tf_op jit(solution)/shard_map/all_to_all | solution.py:33
  91.4 0.2 all-gather.7.cloned.1.call-start
  91.7 28.3 %all-to-all-done.3 = f32[16,2,64,256]{3,2,1,0:T(8,128)S(1)} async-done(((f32[16,2,64,256]{3,2,1,0:T(8,128)}), f32[16,2,64,256]{3,2,1,0:T(8,128)S(1)}, u32[]{:S(2)}, u32[]{:S(2)}) %all-to-all-start.3) | async-done | bytes 2097184 | tf_op jit(solution)/shard_map/all_to_all | solution.py:33
  120.0 0.1 reduce_sum.38
  120.1 1.3 convolution_select_fusion
  121.4 8.3 %convolution_convert_fusion.1 = bf16[512,4,1024]{2,0,1:T(8,128)(2,1)S(1)} fusion(bf16[1024,512,1]{0,1,2:T(8,128)(2,1)} %bitcast.79, bf16[4,1024,1024]{2,1,0:T(8,128)(2,1)} %param.10), kind=kOutput, calls=%fused_computation.5 | convolution fusion | flops 4297064448 | bytes 13631488 | tf_op jit(solution)/shard_map/qst,tk->qsk/dot_general | solution.py:71
  129.7 1.8 %fusion.7 = f32[2,1024,256,1]{2,1,0,3:T(8,128)S(1)} fusion(bf16[4,1024,2,256]{1,3,2,0:T(8,128)(2,1)S(1)} %bitcast.86, bf16[2,4,256,256]{3,2,1,0:T(8,128)(2,1)S(1)} %copy-done.5), kind=kOutput, calls=%fused_computation.16 | convolution fusion | flops 1073741824 | bytes 7340032 | tf_op jit(solution)/shard_map/qsbc,bqdc->bsd/dot_general | solution.py:85
  131.5 1.5 copy.89
  133.0 3.7 %all-to-all-start.2 = ((f32[16,2,64,256]{3,2,1,0:T(8,128)}), f32[16,2,64,256]{3,2,1,0:T(8,128)S(1)}, u32[]{:S(2)}, u32[]{:S(2)}) async-start(f32[16,2,64,256]{3,2,1,0:T(8,128)} %bitcast.73), calls=%async_computation.2 | async-start | bytes 4194304 | tf_op jit(solution)/shard_map/all_to_all | solution.py:33
  136.7 0.1 iota_compare_fusion.2
  136.8 0.8 slice.32
  137.6 0.1 copy.77
  137.7 0.1 copy.66
  137.8 0.1 broadcast_compare_fusion
  137.8 26.6 %all-to-all-done.2 = f32[16,2,64,256]{3,2,1,0:T(8,128)S(1)} async-done(((f32[16,2,64,256]{3,2,1,0:T(8,128)}), f32[16,2,64,256]{3,2,1,0:T(8,128)S(1)}, u32[]{:S(2)}, u32[]{:S(2)}) %all-to-all-start.2) | async-done | bytes 2097184 | tf_op jit(solution)/shard_map/all_to_all | solution.py:33
  164.4 0.1 reduce_sum.36
  164.5 0.1 broadcast_select_fusion
  164.6 0.1 select_reduce_fusion.1
  164.8 2.2 %select_reduce_fusion = f32[4,64,256]{2,1,0:T(8,128)S(1)} fusion(f32[16,2,64,256]{3,2,1,0:T(8,128)} %bitcast.76, pred[16,2,4]{2,1,0:T(4,128)(4,1)S(1)} %broadcast_compare_fusion), kind=kLoop, calls=%fused_computation.1 | loop fusion | flops 4128768 | bytes 2359424 | tf_op jit(solution)/shard_map/reduce_sum | solution.py:93
  167.0 0.7 add.58
  (24 shorter events, 0.2 us)
Async XLA Ops:
  6.5 19.8 %copy-start.2 = (f32[2]{0:T(128)S(1)}, f32[2]{0:T(128)}, u32[]{:S(2)}) copy-start(f32[2]{0:T(128)} %param.14) | copy-start | bytes 28
  6.5 19.8 %copy-start.1 = (s32[2,4]{1,0:T(2,128)S(1)}, s32[2,4]{1,0:T(2,128)}, u32[]{:S(2)}) copy-start(s32[2,4]{1,0:T(2,128)} %param.15) | copy-start | bytes 100
  6.5 44.3 %all-gather.5.cloned.1.call-start = ((), (), s32[]{:S(2)}) async-start(), calls=%async_computation.4 | async-start | bytes 2367488 | tf_op jit(solution)/shard_map/all_gather | solution.py:51
  12.2 24.8 %all-to-all-start.1 = ((bf16[16,2,64,256]{3,2,1,0:T(8,128)(2,1)}), bf16[16,2,64,256]{3,2,1,0:T(8,128)(2,1)S(1)}, u32[]{:S(2)}, u32[]{:S(2)}) async-start(bf16[16,2,64,256]{3,2,1,0:T(8,128)(2,1)} %broadcast_in_dim.100), calls=%async_computation.1 | async-start | bytes 2097152 | tf_op jit(solution)/shard_map/all_to_all | solution.py:21
  52.8 25.0 %all-to-all-start = ((bf16[16,2,64,256]{3,2,1,0:T(8,128)(2,1)}), bf16[16,2,64,256]{3,2,1,0:T(8,128)(2,1)S(1)}, u32[]{:S(2)}, u32[]{:S(2)}) async-start(bf16[16,2,64,256]{3,2,1,0:T(8,128)(2,1)} %broadcast_in_dim.96), calls=%async_computation | async-start | bytes 2097152 | tf_op jit(solution)/shard_map/all_to_all | solution.py:21
  79.1 4.0 %copy-start.3 = (bf16[512,4,1024]{2,0,1:T(8,128)(2,1)S(1)}, bf16[512,4,1024]{2,0,1:T(8,128)(2,1)}, u32[]{:S(2)}) copy-start(bf16[512,4,1024]{2,0,1:T(8,128)(2,1)} %convolution_convert_fusion) | copy-start | bytes 12582916
  82.2 1.0 copy-start
  84.4 3.3 %copy-start.4 = (bf16[2,4,256,256]{3,2,1,0:T(8,128)(2,1)}, bf16[2,4,256,256]{3,2,1,0:T(8,128)(2,1)S(1)}, u32[]{:S(2)}) copy-start(bf16[2,4,256,256]{3,2,1,0:T(8,128)(2,1)S(1)} %multiply_convert_fusion) | copy-start | bytes 3145732
  87.7 32.3 %all-to-all-start.3 = ((f32[16,2,64,256]{3,2,1,0:T(8,128)}), f32[16,2,64,256]{3,2,1,0:T(8,128)S(1)}, u32[]{:S(2)}, u32[]{:S(2)}) async-start(f32[16,2,64,256]{3,2,1,0:T(8,128)} %bitcast.74), calls=%async_computation.3 | async-start | bytes 4194304 | tf_op jit(solution)/shard_map/all_to_all | solution.py:33
  91.4 73.3 %all-gather.7.cloned.1.call-start = ((), (), s32[]{:S(2)}) async-start(), calls=%async_computation.5 | async-start | bytes 2228224 | tf_op jit(solution)/shard_map/all_gather | solution.py:83
  121.4 8.3 %copy-start.5 = (bf16[2,4,256,256]{3,2,1,0:T(8,128)(2,1)S(1)}, bf16[2,4,256,256]{3,2,1,0:T(8,128)(2,1)}, u32[]{:S(2)}) copy-start(bf16[2,4,256,256]{3,2,1,0:T(8,128)(2,1)} %copy-done.4) | copy-start | bytes 3145732
  133.0 31.4 %all-to-all-start.2 = ((f32[16,2,64,256]{3,2,1,0:T(8,128)}), f32[16,2,64,256]{3,2,1,0:T(8,128)S(1)}, u32[]{:S(2)}, u32[]{:S(2)}) async-start(f32[16,2,64,256]{3,2,1,0:T(8,128)} %bitcast.73), calls=%async_computation.2 | async-start | bytes 4194304 | tf_op jit(solution)/shard_map/all_to_all | solution.py:33
Sparse Core Ops, SparseCore 0:
  9.2 41.6 all-gather.4
  121.5 34.9 all-gather.6

commit v10 on v9

--- a/solution.py
+++ b/solution.py
@@ -45,14 +45,16 @@
     left_local = pair_left % det_local
     left_rows = jnp.take(orbitals, left_local, axis=0)
 
-    pad = 16
-    marks = jnp.zeros((pad, nocc), jnp.bfloat16).at[0, :capacity].set(pair_right.astype(jnp.bfloat16))
-    carried = jnp.concatenate([orbitals.reshape(det_local * rows, nocc), marks], axis=0)
-    everyone = lax.all_gather(carried, "det", axis=0, tiled=False)
-    right_all = everyone[:, det_local * rows, :capacity].astype(jnp.int32).reshape(-1)
+    everyone = lax.all_gather(orbitals.reshape(det_local * rows, nocc), "det", axis=0, tiled=False)
+    right_all = lax.all_to_all(
+        jnp.broadcast_to(pair_right[None], (n_det, capacity)), "det", 0, 0, tiled=True
+    ).reshape(n_det * capacity)
     left_full = gather_rows(left_rows, n_orb)
+    early = jnp.minimum(jnp.min(right_all), 0)
     right_rows = jnp.stack([
-        lax.dynamic_slice(everyone, (pair_right[k] // det_local, (pair_right[k] % det_local) * rows, 0), (1, rows, nocc))[0]
+        lax.dynamic_slice(
+            everyone, (pair_right[k] // det_local + early, (pair_right[k] % det_local) * rows, 0), (1, rows, nocc)
+        )[0]
         for k in range(capacity)
     ])
     right_full = gather_rows(right_rows, n_orb)

time: 175 us -> 175 us (level)
  waiting for transfers between devices: 87.4 us -> 77.9 us
  starting transfers between devices: 21.5 us -> 30.1 us
    all_gather x1, waiting for transfers between devices: 13.3 us -> 0.75 us  [local_body(): lax.all_gather(orbitals.reshape(det_local * rows, nocc), 'det', axis=0, t...]
    all_to_all x0 -> x1, starting transfers between devices: none -> 8.59 us  [local_body(): lax.all_to_all(jnp.broadcast_to(pair_right[None], (n_det, capacity)), 'de...]
    all_to_all x0 -> x1, waiting for transfers between devices: none -> 3.92 us  [local_body(): lax.all_to_all(jnp.broadcast_to(pair_right[None], (n_det, capacity)), 'de...]
    all_to_all x2, waiting for transfers between devices: 19.2 us -> 16.6 us  [gather_rows(): got = lax.all_to_all(spread, 'orb', 0, 0, tiled=True)]
  transfers between devices with their start and end apart: 6 -> 7, of which waited for: 5 -> 6; matrix products, arithmetic and copies ran while one was open for 16% -> 17% of each run, Pallas kernels for 0% -> 0%
where the time goes in v10:
time: 175 us; the launch traced here: 174 us
  waiting for transfers between devices  77.9 us (45%)
  starting transfers between devices  30.1 us (17%)
  matrix products  28.1 us (16%)
  between operations  20.2 us (12%)
  local copies, waits for them, and re-layouts  11.7 us (7%)
  other arithmetic  6.44 us (4%)
    all_to_all x2, waiting for transfers between devices, scatter_rows(): got = lax.all_to_all(parts, 'orb', 0, 0, tiled=True)  55.8 us
    all_to_all x2, waiting for transfers between devices, gather_rows(): got = lax.all_to_all(spread, 'orb', 0, 0, tiled=True)  16.6 us
    all_to_all x2, starting transfers between devices, gather_rows(): got = lax.all_to_all(spread, 'orb', 0, 0, tiled=True)  13.9 us
    dot_general x1, matrix products, local_body(): jnp.einsum('qst,tk->qsk', dfit, left_stack, preferred_element_type=jnp.fl...  9.45 us
    all_to_all x1, starting transfers between devices, local_body(): lax.all_to_all(jnp.broadcast_to(pair_right[None], (n_det, capacity)), 'de...  8.59 us
    dot_general x1, matrix products, local_body(): jnp.einsum('qst,tk->qsk', dfit, moved_stack, preferred_element_type=jnp.f...  8.32 us
    all_to_all x2, starting transfers between devices, scatter_rows(): got = lax.all_to_all(parts, 'orb', 0, 0, tiled=True)  7.45 us
    all_to_all x1, waiting for transfers between devices, local_body(): lax.all_to_all(jnp.broadcast_to(pair_right[None], (n_det, capacity)), 'de...  3.92 us
  transfers between devices with their start and end apart: 7, of which 6 were waited for; matrix products, arithmetic and copies ran while one was open for 17% of the time, Pallas kernels for 0%

profile of v10, /device:TPU:32, one launch (start us, length us, event | category | flops | bytes accessed | tf_op | source)
XLA Modules:
  0.0 174.4 jit_solution(18126875556419099134)
XLA Ops:
  6.5 0.7 all-gather.4.cloned.1.call-update
  7.3 1.3 broadcast_in_dim.101
  8.5 8.6 %all-to-all-start = ((s32[16,1,2]{2,1,0:T(1,128)}), s32[16,1,2]{2,1,0:T(1,128)S(1)}, u32[]{:S(2)}, u32[]{:S(2)}) async-start(s32[16,1,2]{2,1,0:T(1,128)} %broadcast_in_dim.101), calls=%async_computation | async-start | bytes 16384 | tf_op jit(solution)/shard_map/all_to_all | solution.py:49
  17.1 0.7 compare_and_fusion
  17.8 1.5 gather_fusion
  19.3 3.9 %all-to-all-done = s32[16,1,2]{2,1,0:T(1,128)S(1)} async-done(((s32[16,1,2]{2,1,0:T(1,128)}), s32[16,1,2]{2,1,0:T(1,128)S(1)}, u32[]{:S(2)}, u32[]{:S(2)}) %all-to-all-start) | async-done | bytes 160 | tf_op jit(solution)/shard_map/all_to_all | solution.py:49
  23.3 1.1 broadcast_in_dim.106
  24.4 7.0 %all-to-all-start.2 = ((bf16[16,2,64,256]{3,2,1,0:T(8,128)(2,1)}), bf16[16,2,64,256]{3,2,1,0:T(8,128)(2,1)S(1)}, u32[]{:S(2)}, u32[]{:S(2)}) async-start(bf16[16,2,64,256]{3,2,1,0:T(8,128)(2,1)} %broadcast_in_dim.106), calls=%async_computation.2 | async-start | bytes 2097152 | tf_op jit(solution)/shard_map/all_to_all | solution.py:21
  31.4 1.4 fusion.16
  38.6 0.7 broadcast_multiply_fusion
  39.3 0.7 convert_multiply_fusion
  40.0 0.6 reduce_min.9
  41.3 7.9 %all-to-all-done.2 = bf16[16,2,64,256]{3,2,1,0:T(8,128)(2,1)S(1)} async-done(((bf16[16,2,64,256]{3,2,1,0:T(8,128)(2,1)}), bf16[16,2,64,256]{3,2,1,0:T(8,128)(2,1)S(1)}, u32[]{:S(2)}, u32[]{:S(2)}) %all-to-all-start.2) | async-done | bytes 1048608 | tf_op jit(solution)/shard_map/all_to_all | solution.py:21
  49.2 0.1 copy.39
  49.3 0.5 copy.42
  49.9 0.8 all-gather.4.cloned.1.call-done
  50.6 0.8 constant_dynamic-slice_fusion.1
  51.4 1.1 broadcast_in_dim.102
  52.5 6.8 %all-to-all-start.1 = ((bf16[16,2,64,256]{3,2,1,0:T(8,128)(2,1)}), bf16[16,2,64,256]{3,2,1,0:T(8,128)(2,1)S(1)}, u32[]{:S(2)}, u32[]{:S(2)}) async-start(bf16[16,2,64,256]{3,2,1,0:T(8,128)(2,1)} %broadcast_in_dim.102), calls=%async_computation.1 | async-start | bytes 2097152 | tf_op jit(solution)/shard_map/all_to_all | solution.py:21
  59.3 9.4 %convolution_convert_fusion = bf16[512,4,1024]{2,0,1:T(8,128)(2,1)} fusion(bf16[1024,512,1]{0,1,2:T(8,128)(2,1)S(1)} %bitcast.75, bf16[4,1024,1024]{2,1,0:T(8,128)(2,1)} %param.8), kind=kOutput, calls=%fused_computation.4 | convolution fusion | flops 4297064448 | bytes 13631488 | tf_op jit(solution)/shard_map/qst,tk->qsk/dot_general | solution.py:63
  68.8 8.7 %all-to-all-done.1 = bf16[16,2,64,256]{3,2,1,0:T(8,128)(2,1)S(1)} async-done(((bf16[16,2,64,256]{3,2,1,0:T(8,128)(2,1)}), bf16[16,2,64,256]{3,2,1,0:T(8,128)(2,1)S(1)}, u32[]{:S(2)}, u32[]{:S(2)}) %all-to-all-start.1) | async-done | bytes 1048608 | tf_op jit(solution)/shard_map/all_to_all | solution.py:21
  77.5 0.1 copy.38
  77.6 0.5 fusion.17
  78.2 0.7 convolution_subtract_fusion.1
  78.8 0.7 fusion.9
  79.5 0.7 convolution_subtract_fusion
  80.2 0.7 fusion.18
  80.9 1.0 convolution_convert_fusion.2
  81.9 1.0 copy-done
  82.9 1.3 multiply_convert_fusion
  84.2 1.8 %fusion.5 = f32[2,1024,256,1]{2,1,0,3:T(8,128)S(1)} fusion(bf16[4,1024,2,256]{1,3,2,0:T(8,128)(2,1)S(1)} %bitcast.79, bf16[2,4,256,256]{3,2,1,0:T(8,128)(2,1)S(1)} %multiply_convert_fusion), kind=kOutput, calls=%fused_computation.14 | convolution fusion | flops 1073741824 | bytes 7340032 | tf_op jit(solution)/shard_map/qsbc,bqcd->bsd/dot_general | solution.py:80
  86.0 1.5 copy.71
  87.5 3.7 %all-to-all-start.4 = ((f32[16,2,64,256]{3,2,1,0:T(8,128)}), f32[16,2,64,256]{3,2,1,0:T(8,128)S(1)}, u32[]{:S(2)}, u32[]{:S(2)}) async-start(f32[16,2,64,256]{3,2,1,0:T(8,128)} %bitcast.69), calls=%async_computation.4 | async-start | bytes 4194304 | tf_op jit(solution)/shard_map/all_to_all | solution.py:33
  91.2 0.2 all-gather.6.cloned.1.call-start
  91.5 28.3 %all-to-all-done.4 = f32[16,2,64,256]{3,2,1,0:T(8,128)S(1)} async-done(((f32[16,2,64,256]{3,2,1,0:T(8,128)}), f32[16,2,64,256]{3,2,1,0:T(8,128)S(1)}, u32[]{:S(2)}, u32[]{:S(2)}) %all-to-all-start.4) | async-done | bytes 2097184 | tf_op jit(solution)/shard_map/all_to_all | solution.py:33
  119.7 0.1 reduce_sum.38
  119.9 1.3 convolution_select_fusion
  121.2 8.3 %convolution_convert_fusion.1 = bf16[512,4,1024]{2,0,1:T(8,128)(2,1)S(1)} fusion(bf16[1024,512,1]{0,1,2:T(8,128)(2,1)} %bitcast.74, bf16[4,1024,1024]{2,1,0:T(8,128)(2,1)} %param.8), kind=kOutput, calls=%fused_computation.5 | convolution fusion | flops 4297064448 | bytes 13631488 | tf_op jit(solution)/shard_map/qst,tk->qsk/dot_general | solution.py:73
  129.5 1.8 %fusion.7 = f32[2,1024,256,1]{2,1,0,3:T(8,128)S(1)} fusion(bf16[4,1024,2,256]{1,3,2,0:T(8,128)(2,1)S(1)} %bitcast.80, bf16[2,4,256,256]{3,2,1,0:T(8,128)(2,1)S(1)} %copy-done.4), kind=kOutput, calls=%fused_computation.16 | convolution fusion | flops 1073741824 | bytes 7340032 | tf_op jit(solution)/shard_map/qsbc,bqdc->bsd/dot_general | solution.py:87
  131.3 1.5 copy.72
  132.7 3.7 %all-to-all-start.3 = ((f32[16,2,64,256]{3,2,1,0:T(8,128)}), f32[16,2,64,256]{3,2,1,0:T(8,128)S(1)}, u32[]{:S(2)}, u32[]{:S(2)}) async-start(f32[16,2,64,256]{3,2,1,0:T(8,128)} %bitcast.68), calls=%async_computation.3 | async-start | bytes 4194304 | tf_op jit(solution)/shard_map/all_to_all | solution.py:33
  136.6 0.1 broadcast_compare_fusion
  136.7 27.5 %all-to-all-done.3 = f32[16,2,64,256]{3,2,1,0:T(8,128)S(1)} async-done(((f32[16,2,64,256]{3,2,1,0:T(8,128)}), f32[16,2,64,256]{3,2,1,0:T(8,128)S(1)}, u32[]{:S(2)}, u32[]{:S(2)}) %all-to-all-start.3) | async-done | bytes 2097184 | tf_op jit(solution)/shard_map/all_to_all | solution.py:33
  164.2 0.1 reduce_sum.36
  164.3 0.1 broadcast_select_fusion
  164.4 0.1 select_reduce_fusion.1
  164.5 2.3 %select_reduce_fusion = f32[4,64,256]{2,1,0:T(8,128)S(1)} fusion(f32[16,2,64,256]{3,2,1,0:T(8,128)} %bitcast.71, pred[16,2,4]{2,1,0:T(4,128)(4,1)S(1)} %broadcast_compare_fusion), kind=kLoop, calls=%fused_computation.1 | loop fusion | flops 4128768 | bytes 2359424 | tf_op jit(solution)/shard_map/reduce_sum | solution.py:95
  166.8 0.7 add.62
  (20 shorter events, 0.3 us)
Async XLA Ops:
  6.5 44.1 %all-gather.4.cloned.1.call-start = ((), (), s32[]{:S(2)}) async-start(), calls=%async_computation.5 | async-start | bytes 2228224 | tf_op jit(solution)/shard_map/all_gather | solution.py:48
  8.5 14.7 %all-to-all-start = ((s32[16,1,2]{2,1,0:T(1,128)}), s32[16,1,2]{2,1,0:T(1,128)S(1)}, u32[]{:S(2)}, u32[]{:S(2)}) async-start(s32[16,1,2]{2,1,0:T(1,128)} %broadcast_in_dim.101), calls=%async_computation | async-start | bytes 16384 | tf_op jit(solution)/shard_map/all_to_all | solution.py:49
  24.4 24.9 %all-to-all-start.2 = ((bf16[16,2,64,256]{3,2,1,0:T(8,128)(2,1)}), bf16[16,2,64,256]{3,2,1,0:T(8,128)(2,1)S(1)}, u32[]{:S(2)}, u32[]{:S(2)}) async-start(bf16[16,2,64,256]{3,2,1,0:T(8,128)(2,1)} %broadcast_in_dim.106), calls=%async_computation.2 | async-start | bytes 2097152 | tf_op jit(solution)/shard_map/all_to_all | solution.py:21
  52.5 25.0 %all-to-all-start.1 = ((bf16[16,2,64,256]{3,2,1,0:T(8,128)(2,1)}), bf16[16,2,64,256]{3,2,1,0:T(8,128)(2,1)S(1)}, u32[]{:S(2)}, u32[]{:S(2)}) async-start(bf16[16,2,64,256]{3,2,1,0:T(8,128)(2,1)} %broadcast_in_dim.102), calls=%async_computation.1 | async-start | bytes 2097152 | tf_op jit(solution)/shard_map/all_to_all | solution.py:21
  78.8 4.0 %copy-start.2 = (bf16[512,4,1024]{2,0,1:T(8,128)(2,1)S(1)}, bf16[512,4,1024]{2,0,1:T(8,128)(2,1)}, u32[]{:S(2)}) copy-start(bf16[512,4,1024]{2,0,1:T(8,128)(2,1)} %convolution_convert_fusion) | copy-start | bytes 12582916
  81.9 1.0 copy-start
  84.2 3.3 %copy-start.3 = (bf16[2,4,256,256]{3,2,1,0:T(8,128)(2,1)}, bf16[2,4,256,256]{3,2,1,0:T(8,128)(2,1)S(1)}, u32[]{:S(2)}) copy-start(bf16[2,4,256,256]{3,2,1,0:T(8,128)(2,1)S(1)} %multiply_convert_fusion) | copy-start | bytes 3145732
  86.0 5.5 %copy-start.1 = (f32[2]{0:T(128)S(1)}, f32[2]{0:T(128)}, u32[]{:S(2)}) copy-start(f32[2]{0:T(128)} %param.12) | copy-start | bytes 28
  87.5 32.3 %all-to-all-start.4 = ((f32[16,2,64,256]{3,2,1,0:T(8,128)}), f32[16,2,64,256]{3,2,1,0:T(8,128)S(1)}, u32[]{:S(2)}, u32[]{:S(2)}) async-start(f32[16,2,64,256]{3,2,1,0:T(8,128)} %bitcast.69), calls=%async_computation.4 | async-start | bytes 4194304 | tf_op jit(solution)/shard_map/all_to_all | solution.py:33
  91.2 73.3 %all-gather.6.cloned.1.call-start = ((), (), s32[]{:S(2)}) async-start(), calls=%async_computation.6 | async-start | bytes 2228224 | tf_op jit(solution)/shard_map/all_gather | solution.py:85
  121.2 8.3 %copy-start.4 = (bf16[2,4,256,256]{3,2,1,0:T(8,128)(2,1)S(1)}, bf16[2,4,256,256]{3,2,1,0:T(8,128)(2,1)}, u32[]{:S(2)}) copy-start(bf16[2,4,256,256]{3,2,1,0:T(8,128)(2,1)} %copy-done.3) | copy-start | bytes 3145732
  132.7 31.4 %all-to-all-start.3 = ((f32[16,2,64,256]{3,2,1,0:T(8,128)}), f32[16,2,64,256]{3,2,1,0:T(8,128)S(1)}, u32[]{:S(2)}, u32[]{:S(2)}) async-start(f32[16,2,64,256]{3,2,1,0:T(8,128)} %bitcast.68), calls=%async_computation.3 | async-start | bytes 4194304 | tf_op jit(solution)/shard_map/all_to_all | solution.py:33
Sparse Core Ops, SparseCore 0:
  9.2 41.4 all-gather.3
  121.3 34.8 all-gather.5

commit v11 on v9

--- a/solution.py
+++ b/solution.py
@@ -88,9 +88,10 @@
     own = left_local[:, None] == jnp.arange(det_local, dtype=jnp.int32)[None, :]
     own_sum = jnp.sum(jnp.where(own[:, :, None, None], left_grad[:, None], 0.0), axis=0)
 
-    asked = right_all.reshape(n_det, capacity)
-    mine = asked[:, :, None] == (me * det_local + jnp.arange(det_local, dtype=jnp.int32))[None, None, :]
-    returned = jnp.sum(jnp.where(mine[:, :, :, None, None], came[:, :, None], 0.0), axis=(0, 1))
+    target = jnp.where(right_all // det_local == me, right_all % det_local, det_local)
+    returned = jnp.zeros((det_local, rows, nocc), jnp.float32).at[target].add(
+        came.reshape(n_det * capacity, rows, nocc), mode="drop"
+    )
     return own_sum + returned
 
 

time: 175 us -> 180 us (1.029)
  other arithmetic: 6.72 us -> 12 us
    scatter-add x0 -> x1, other arithmetic: none -> 6.88 us  [local_body(): jnp.zeros((det_local, rows, nocc), jnp.float32).at[target]]
    reduce_sum x1 -> x0, other arithmetic: 2.24 us -> none  [local_body(): jnp.sum(jnp.where(mine[:, :, :, None, None], came[:, :, None], 0.0), axis...]
where the time goes in v11:
time: 180 us; the launch traced here: 179 us
  waiting for transfers between devices  87.7 us (49%)
  matrix products  28.1 us (16%)
  starting transfers between devices  21.5 us (12%)
  between operations  19.3 us (11%)
  other arithmetic  12 us (7%)
  local copies, waits for them, and re-layouts  10.5 us (6%)
    all_to_all x2, waiting for transfers between devices, scatter_rows(): got = lax.all_to_all(parts, 'orb', 0, 0, tiled=True)  55 us
    all_to_all x2, waiting for transfers between devices, gather_rows(): got = lax.all_to_all(spread, 'orb', 0, 0, tiled=True)  19.4 us
    all_to_all x2, starting transfers between devices, gather_rows(): got = lax.all_to_all(spread, 'orb', 0, 0, tiled=True)  13.8 us
    all_gather x1, waiting for transfers between devices, local_body(): everyone = lax.all_gather(carried, 'det', axis=0, tiled=False)  13.3 us
    dot_general x1, matrix products, local_body(): jnp.einsum('qst,tk->qsk', dfit, left_stack, preferred_element_type=jnp.fl...  9.43 us
    dot_general x1, matrix products, local_body(): jnp.einsum('qst,tk->qsk', dfit, moved_stack, preferred_element_type=jnp.f...  8.32 us
    all_to_all x2, starting transfers between devices, scatter_rows(): got = lax.all_to_all(parts, 'orb', 0, 0, tiled=True)  7.45 us
    scatter-add x1, other arithmetic, local_body(): jnp.zeros((det_local, rows, nocc), jnp.float32).at[target]  6.88 us
  transfers between devices with their start and end apart: 6, of which 5 were waited for; matrix products, arithmetic and copies ran while one was open for 16% of the time, Pallas kernels for 0%

profile of v11, /device:TPU:32, one launch (start us, length us, event | category | flops | bytes accessed | tf_op | source)
XLA Modules:
  0.0 179.2 jit_solution(12564728368159187524)
XLA Ops:
  6.5 0.7 convert_bitcast_fusion
  7.2 1.6 fusion.16
  8.8 0.0 all-gather.5.cloned.1.call-update
  8.8 0.7 compare_and_fusion
  9.5 1.5 gather_fusion
  11.0 0.1 broadcast_select_fusion.1
  11.1 1.1 broadcast_in_dim.81
  12.1 7.0 %all-to-all-start.1 = ((bf16[16,2,64,256]{3,2,1,0:T(8,128)(2,1)}), bf16[16,2,64,256]{3,2,1,0:T(8,128)(2,1)S(1)}, u32[]{:S(2)}, u32[]{:S(2)}) async-start(bf16[16,2,64,256]{3,2,1,0:T(8,128)(2,1)} %broadcast_in_dim.81), calls=%async_computation.1 | async-start | bytes 2097152 | tf_op jit(solution)/shard_map/all_to_all | solution.py:21
  19.2 1.3 fusion.20
  26.2 0.1 convert_multiply_fusion
  26.3 10.7 %all-to-all-done.1 = bf16[16,2,64,256]{3,2,1,0:T(8,128)(2,1)S(1)} async-done(((bf16[16,2,64,256]{3,2,1,0:T(8,128)(2,1)}), bf16[16,2,64,256]{3,2,1,0:T(8,128)(2,1)S(1)}, u32[]{:S(2)}, u32[]{:S(2)}) %all-to-all-start.1) | async-done | bytes 1048608 | tf_op jit(solution)/shard_map/all_to_all | solution.py:21
  36.9 0.1 copy.36
  37.0 0.5 copy.39
  37.6 13.3 %all-gather.5.cloned.1.call-done = bf16[4352,256]{1,0:T(8,128)(2,1)} async-done(((bf16[272,256]{1,0:T(8,128)(2,1)}), bf16[4352,256]{1,0:T(8,128)(2,1)}) %all-gather.5.cloned.1.call-update) | async-done | bytes 2228240 | tf_op jit(solution)/shard_map/all_gather | solution.py:51
  50.8 0.8 constant_dynamic-slice_fusion.1
  51.6 1.1 broadcast_in_dim.77
  52.8 6.8 %all-to-all-start = ((bf16[16,2,64,256]{3,2,1,0:T(8,128)(2,1)}), bf16[16,2,64,256]{3,2,1,0:T(8,128)(2,1)S(1)}, u32[]{:S(2)}, u32[]{:S(2)}) async-start(bf16[16,2,64,256]{3,2,1,0:T(8,128)(2,1)} %broadcast_in_dim.77), calls=%async_computation | async-start | bytes 2097152 | tf_op jit(solution)/shard_map/all_to_all | solution.py:21
  59.6 9.4 %convolution_convert_fusion = bf16[512,4,1024]{2,0,1:T(8,128)(2,1)} fusion(bf16[1024,512,1]{0,1,2:T(8,128)(2,1)S(1)} %bitcast.77, bf16[4,1024,1024]{2,1,0:T(8,128)(2,1)} %param.10), kind=kOutput, calls=%fused_computation.4 | convolution fusion | flops 4297064448 | bytes 13631488 | tf_op jit(solution)/shard_map/qst,tk->qsk/dot_general | solution.py:61
  69.0 8.8 %all-to-all-done = bf16[16,2,64,256]{3,2,1,0:T(8,128)(2,1)S(1)} async-done(((bf16[16,2,64,256]{3,2,1,0:T(8,128)(2,1)}), bf16[16,2,64,256]{3,2,1,0:T(8,128)(2,1)S(1)}, u32[]{:S(2)}, u32[]{:S(2)}) %all-to-all-start) | async-done | bytes 1048608 | tf_op jit(solution)/shard_map/all_to_all | solution.py:21
  77.8 0.1 copy.35
  77.9 0.5 fusion.21
  78.4 0.7 convolution_subtract_fusion.1
  79.1 0.7 fusion.9
  79.8 0.7 convolution_subtract_fusion
  80.4 0.7 fusion.22
  81.1 1.0 convolution_convert_fusion.2
  82.2 1.0 copy-done
  83.1 1.3 multiply_convert_fusion
  84.4 1.8 fusion.5
  86.2 1.5 copy.65
  87.7 3.7 %all-to-all-start.3 = ((f32[16,2,64,256]{3,2,1,0:T(8,128)}), f32[16,2,64,256]{3,2,1,0:T(8,128)S(1)}, u32[]{:S(2)}, u32[]{:S(2)}) async-start(f32[16,2,64,256]{3,2,1,0:T(8,128)} %bitcast.72), calls=%async_computation.3 | async-start | bytes 4194304 | tf_op jit(solution)/shard_map/all_to_all | solution.py:33
  91.5 0.2 all-gather.7.cloned.1.call-start
  91.7 28.3 %all-to-all-done.3 = f32[16,2,64,256]{3,2,1,0:T(8,128)S(1)} async-done(((f32[16,2,64,256]{3,2,1,0:T(8,128)}), f32[16,2,64,256]{3,2,1,0:T(8,128)S(1)}, u32[]{:S(2)}, u32[]{:S(2)}) %all-to-all-start.3) | async-done | bytes 2097184 | tf_op jit(solution)/shard_map/all_to_all | solution.py:33
  120.0 0.1 reduce_sum.29
  120.1 1.3 convolution_select_fusion
  121.4 0.0 all-gather.7.cloned.1.call-update
  121.4 8.3 %convolution_convert_fusion.1 = bf16[512,4,1024]{2,0,1:T(8,128)(2,1)S(1)} fusion(bf16[1024,512,1]{0,1,2:T(8,128)(2,1)} %bitcast.76, bf16[4,1024,1024]{2,1,0:T(8,128)(2,1)} %param.10), kind=kOutput, calls=%fused_computation.5 | convolution fusion | flops 4297064448 | bytes 13631488 | tf_op jit(solution)/shard_map/qst,tk->qsk/dot_general | solution.py:71
  129.8 1.8 fusion.7
  131.5 1.4 copy.66
  133.0 3.7 %all-to-all-start.2 = ((f32[16,2,64,256]{3,2,1,0:T(8,128)}), f32[16,2,64,256]{3,2,1,0:T(8,128)S(1)}, u32[]{:S(2)}, u32[]{:S(2)}) async-start(f32[16,2,64,256]{3,2,1,0:T(8,128)} %bitcast.71), calls=%async_computation.2 | async-start | bytes 4194304 | tf_op jit(solution)/shard_map/all_to_all | solution.py:33
  136.7 0.1 iota_compare_fusion.2
  136.8 0.8 fusion.17
  137.6 0.1 reshape.212
  137.7 26.7 %all-to-all-done.2 = f32[16,2,64,256]{3,2,1,0:T(8,128)S(1)} async-done(((f32[16,2,64,256]{3,2,1,0:T(8,128)}), f32[16,2,64,256]{3,2,1,0:T(8,128)S(1)}, u32[]{:S(2)}, u32[]{:S(2)}) %all-to-all-start.2) | async-done | bytes 2097184 | tf_op jit(solution)/shard_map/all_to_all | solution.py:33
  164.4 0.1 reduce_sum.27
  164.6 0.1 broadcast_select_fusion
  164.6 0.8 select_reduce_fusion
  165.4 6.9 %scatter_fusion = f32[4,64,256]{2,1,0:T(8,128)} fusion(f32[4,64,256]{2,1,0:T(8,128)} %select_reduce_fusion, s32[32]{0:T(128)S(1)} %fusion.19, f32[32,64,256]{2,1,0:T(8,128)} %all-gather.7.cloned.1.call-done), kind=kCustom, calls=%fused_computation.1 | custom fusion | flops 524288 | bytes 6291584 | tf_op jit(solution)/shard_map/scatter-add | solution.py:92
  (20 shorter events, 0.1 us)
Async XLA Ops:
  6.5 19.6 %copy-start.2 = (f32[2]{0:T(128)S(1)}, f32[2]{0:T(128)}, u32[]{:S(2)}) copy-start(f32[2]{0:T(128)} %param.14) | copy-start | bytes 28
  6.5 19.7 %copy-start.1 = (s32[2,4]{1,0:T(2,128)S(1)}, s32[2,4]{1,0:T(2,128)}, u32[]{:S(2)}) copy-start(s32[2,4]{1,0:T(2,128)} %param.15) | copy-start | bytes 100
  6.5 44.3 %all-gather.5.cloned.1.call-start = ((), (), s32[]{:S(2)}) async-start(), calls=%async_computation.4 | async-start | bytes 2367488 | tf_op jit(solution)/shard_map/all_gather | solution.py:51
  12.1 24.8 %all-to-all-start.1 = ((bf16[16,2,64,256]{3,2,1,0:T(8,128)(2,1)}), bf16[16,2,64,256]{3,2,1,0:T(8,128)(2,1)S(1)}, u32[]{:S(2)}, u32[]{:S(2)}) async-start(bf16[16,2,64,256]{3,2,1,0:T(8,128)(2,1)} %broadcast_in_dim.81), calls=%async_computation.1 | async-start | bytes 2097152 | tf_op jit(solution)/shard_map/all_to_all | solution.py:21
  52.8 25.0 %all-to-all-start = ((bf16[16,2,64,256]{3,2,1,0:T(8,128)(2,1)}), bf16[16,2,64,256]{3,2,1,0:T(8,128)(2,1)S(1)}, u32[]{:S(2)}, u32[]{:S(2)}) async-start(bf16[16,2,64,256]{3,2,1,0:T(8,128)(2,1)} %broadcast_in_dim.77), calls=%async_computation | async-start | bytes 2097152 | tf_op jit(solution)/shard_map/all_to_all | solution.py:21
  79.1 4.1 %copy-start.3 = (bf16[512,4,1024]{2,0,1:T(8,128)(2,1)S(1)}, bf16[512,4,1024]{2,0,1:T(8,128)(2,1)}, u32[]{:S(2)}) copy-start(bf16[512,4,1024]{2,0,1:T(8,128)(2,1)} %convolution_convert_fusion) | copy-start | bytes 12582916
  82.1 1.0 copy-start
  84.4 3.3 %copy-start.4 = (bf16[2,4,256,256]{3,2,1,0:T(8,128)(2,1)}, bf16[2,4,256,256]{3,2,1,0:T(8,128)(2,1)S(1)}, u32[]{:S(2)}) copy-start(bf16[2,4,256,256]{3,2,1,0:T(8,128)(2,1)S(1)} %multiply_convert_fusion) | copy-start | bytes 3145732
  87.7 32.3 %all-to-all-start.3 = ((f32[16,2,64,256]{3,2,1,0:T(8,128)}), f32[16,2,64,256]{3,2,1,0:T(8,128)S(1)}, u32[]{:S(2)}, u32[]{:S(2)}) async-start(f32[16,2,64,256]{3,2,1,0:T(8,128)} %bitcast.72), calls=%async_computation.3 | async-start | bytes 4194304 | tf_op jit(solution)/shard_map/all_to_all | solution.py:33
  91.5 74.0 %all-gather.7.cloned.1.call-start = ((), (), s32[]{:S(2)}) async-start(), calls=%async_computation.5 | async-start | bytes 2228224 | tf_op jit(solution)/shard_map/all_gather | solution.py:83
  121.4 8.3 %copy-start.5 = (bf16[2,4,256,256]{3,2,1,0:T(8,128)(2,1)S(1)}, bf16[2,4,256,256]{3,2,1,0:T(8,128)(2,1)}, u32[]{:S(2)}) copy-start(bf16[2,4,256,256]{3,2,1,0:T(8,128)(2,1)} %copy-done.4) | copy-start | bytes 3145732
  133.0 31.4 %all-to-all-start.2 = ((f32[16,2,64,256]{3,2,1,0:T(8,128)}), f32[16,2,64,256]{3,2,1,0:T(8,128)S(1)}, u32[]{:S(2)}, u32[]{:S(2)}) async-start(f32[16,2,64,256]{3,2,1,0:T(8,128)} %bitcast.71), calls=%async_computation.2 | async-start | bytes 4194304 | tf_op jit(solution)/shard_map/all_to_all | solution.py:33
Sparse Core Ops, SparseCore 0:
  9.2 41.6 all-gather.4
  121.5 34.8 all-gather.6
